TPU v7x, 32 devices: a whole 2x2x4 slice. The times are simulated.
32 devices in a mesh: pipe: 8 (over z, y), tensor: 4 (over x, core).
Axes of the slice: x: 2, y: 2, z: 4, core: 2. Of those that a mesh axis runs over, the one named last changes fastest.
Arguments:
- arriving: float32 [8, 8192, 384], P('pipe', 'tensor'), may hold values from -6 to 6
- stash: bfloat16 [2, 8, 8192, 384], P(None, 'pipe', 'tensor'), may hold values from -6 to 6
- grad_in: float32 [8, 8192, 384], P('pipe', 'tensor'), may hold values from -6 to 6
- first_up: bfloat16 [8, 64, 128, 128], P('pipe', 'tensor'), may hold values from -0.5 to 0.5
- second_up: bfloat16 [8, 128, 64, 256], P('pipe', 'tensor'), may hold values from -0.75 to 0.75
- first_down: bfloat16 [8, 128, 64, 256], P('pipe', 'tensor'), may hold values from -0.375 to 0.375
- second_down: bfloat16 [8, 64, 128, 128], P('pipe', 'tensor'), may hold values from -0.5 to 0.5
Outputs:
- arriving_out: float32 [8, 8192, 384], P('pipe', 'tensor')
- grad_out: float32 [8, 8192, 384], P('pipe', 'tensor')
- first_up_grad: float32 [8, 64, 128, 128], P('pipe', 'tensor')
- second_up_grad: float32 [8, 128, 64, 256], P('pipe', 'tensor')
- first_down_grad: float32 [8, 128, 64, 256], P('pipe', 'tensor')
- second_down_grad: float32 [8, 64, 128, 128], P('pipe', 'tensor')
All inputs are finite; a program needn't handle non-finite values.
Results may differ from a plain program's by a relative error of at most 0.007.
Values may be sent and summed in bfloat16 or wider, within the bound.
No kernel may reach another device: no remote copies, remote signals or barrier semaphores. Data moves between devices by JAX's collectives and lax.ppermute only.
A program may use at most 192 MiB of HBM per device.

v0:
```python
import jax
import jax.numpy as jnp
from jax import lax
from jax.sharding import PartitionSpec as P


def shifted(value, axis, by):
    count = lax.axis_size(axis)
    return lax.ppermute(value, axis, [(i, (i + by) % count) for i in range(count)])


def smooth(values):
    return jax.nn.gelu(values, approximate=True)


def to_columns(value):
    return lax.all_to_all(value, "tensor", split_axis=1, concat_axis=0, tiled=True)


def to_rows(value):
    return lax.all_to_all(value, "tensor", split_axis=0, concat_axis=1, tiled=True)


def front(narrow_in, first_up, second_up, first_down):
    first_out = jnp.einsum(
        "njr,nji->nir", narrow_in, first_up, preferred_element_type=jnp.float32
    ).astype(jnp.bfloat16)
    spread = to_columns(first_out)
    hidden_pre = jnp.einsum("nir,inf->ifr", spread, second_up, preferred_element_type=jnp.float32)
    hidden = smooth(hidden_pre).astype(jnp.bfloat16)
    local_fold = jnp.einsum(
        "ifr,inf->nir", hidden, first_down, preferred_element_type=jnp.float32
    ).astype(jnp.bfloat16)
    folded = to_rows(local_fold)
    return (spread, hidden_pre, hidden, folded)


def backward(narrow_in, cotangent, first_up, second_up, first_down, second_down, parts, held=None):
    spread, hidden_pre, hidden, folded = parts
    narrow_grad = cotangent.astype(jnp.bfloat16).reshape(narrow_in.shape)
    grad_second_down = jnp.einsum(
        "nir,nkr->nik", folded, narrow_grad, preferred_element_type=jnp.float32
    )
    local_grad = jnp.einsum(
        "nkr,nik->nir", narrow_grad, second_down, preferred_element_type=jnp.float32
    ).astype(jnp.bfloat16)
    grad_folded = to_columns(local_grad)
    grad_first_down = jnp.einsum(
        "ifr,nir->inf", hidden, grad_folded, preferred_element_type=jnp.float32
    )
    grad_hidden = jnp.einsum(
        "nir,inf->ifr", grad_folded, first_down, preferred_element_type=jnp.float32
    )
    smooth_back = jax.vjp(smooth, hidden_pre)[1]
    grad_pre = smooth_back(grad_hidden)[0].astype(jnp.bfloat16)
    grad_second_up = jnp.einsum(
        "nir,ifr->inf", spread, grad_pre, preferred_element_type=jnp.float32
    )
    column_grad = jnp.einsum(
        "ifr,inf->nir", grad_pre, second_up, preferred_element_type=jnp.float32
    ).astype(jnp.bfloat16)
    if held is not None:
        column_grad, held = lax.optimization_barrier((column_grad, held))
    grad_first = to_rows(column_grad)
    grad_first_up = jnp.einsum(
        "njr,nir->nji", narrow_in, grad_first, preferred_element_type=jnp.float32
    )
    grad_input = jnp.einsum(
        "nir,nji->njr", grad_first, first_up, preferred_element_type=jnp.float32
    ).reshape(cotangent.shape)
    terms = (grad_first_up, grad_second_up, grad_first_down, grad_second_down)
    if held is not None:
        return (grad_input, terms, held)
    return (grad_input, terms)


def body(arriving, stash, grad_in, first_up, second_up, first_down, second_down):
    activation = arriving[0]
    cotangent = grad_in[0]
    up_first = first_up[0]
    up_second = second_up[0]
    down_first = first_down[0]
    down_second = second_down[0]
    blocks = up_first.shape[0]
    width = up_first.shape[1]
    rows = activation.shape[1]
    current = activation.astype(jnp.bfloat16)
    folded_ahead = front(current.reshape(blocks, width, rows), up_first, up_second, down_first)[3]
    output = activation + jnp.einsum(
        "nir,nik->nkr", folded_ahead, down_second, preferred_element_type=jnp.float32
    ).reshape(activation.shape)
    sent = output.astype(jnp.bfloat16)
    near_activation = shifted(sent, "pipe", 1)

    stored = stash[0, 0].reshape(blocks, width, rows)
    behind = front(stored, up_first, up_second, down_first)
    grad_step, totals = backward(
        stored, cotangent, up_first, up_second, down_first, down_second, behind
    )
    sent_back = (cotangent + grad_step).astype(jnp.bfloat16)
    near_cotangent = shifted(sent_back, "pipe", -1)
    near_activation, sent_back = lax.optimization_barrier((near_activation, sent_back))

    folded_ahead = front(near_activation.reshape(blocks, width, rows), up_first, up_second, down_first)[3]
    output = near_activation.astype(jnp.float32) + jnp.einsum(
        "nir,nik->nkr", folded_ahead, down_second, preferred_element_type=jnp.float32
    ).reshape(activation.shape)
    sent = output.astype(jnp.bfloat16)
    last_activation = shifted(sent, "pipe", 1)

    stored = stash[1, 0].reshape(blocks, width, rows)
    behind = front(stored, up_first, up_second, down_first)
    grad_step, terms, last_activation = backward(
        stored, near_cotangent, up_first, up_second, down_first, down_second, behind,
        last_activation,
    )
    sent_back = (near_cotangent.astype(jnp.float32) + grad_step).astype(jnp.bfloat16)
    last_cotangent = shifted(sent_back, "pipe", -1)
    activation = last_activation.astype(jnp.float32)
    cotangent = last_cotangent.astype(jnp.float32)
    totals = (
        totals[0] + terms[0],
        totals[1] + terms[1],
        totals[2] + terms[2],
        totals[3] + terms[3],
    )
    return (
        activation[None],
        cotangent[None],
        totals[0][None],
        totals[1][None],
        totals[2][None],
        totals[3][None],
    )


def solution(mesh):
    placed = (
        P("pipe", "tensor", None),
        P(None, "pipe", "tensor", None),
        P("pipe", "tensor", None),
        P("pipe", "tensor", None, None),
        P("pipe", "tensor", None, None),
        P("pipe", "tensor", None, None),
        P("pipe", "tensor", None, None),
    )
    return jax.shard_map(
        body,
        mesh=mesh,
        in_specs=placed,
        out_specs=(
            P("pipe", "tensor", None),
            P("pipe", "tensor", None),
            P("pipe", "tensor", None, None),
            P("pipe", "tensor", None, None),
            P("pipe", "tensor", None, None),
            P("pipe", "tensor", None, None),
        ),
        check_vma=False,
    )
```

profile of v0, /device:TPU:0, one launch (start us, length us, event | category | flops | bytes accessed | tf_op | source)
XLA Modules:
  0.0 402.1 jit_solution(12744179568943893838)
XLA Ops:
  0.7 2.2 convert_element_type.126
  3.5 2.1 copy.92
  5.5 4.2 %all-to-all-start.5 = ((bf16[16,128,384]{2,0,1:T(8,128)(2,1)}), bf16[16,128,384]{2,0,1:T(8,128)(2,1)S(1)}, u32[]{:S(2)}, u32[]{:S(2)}) async-start(bf16[16,128,384]{2,0,1:T(8,128)(2,1)} %copy.92), calls=%async_computation.5 | async-start | bytes 3145728 | tf_op jit(solution)/shard_map/all_to_all | solution.py:17
  9.8 2.1 convert_element_type.112
  13.6 2.1 copy.75
  15.7 14.1 %all-to-all-done.5 = bf16[16,128,384]{2,0,1:T(8,128)(2,1)S(1)} async-done(((bf16[16,128,384]{2,0,1:T(8,128)(2,1)}), bf16[16,128,384]{2,0,1:T(8,128)(2,1)S(1)}, u32[]{:S(2)}, u32[]{:S(2)}) %all-to-all-start.5) | async-done | bytes 1572896 | tf_op jit(solution)/shard_map/all_to_all | solution.py:17
  31.0 4.4 %all-to-all-start = ((bf16[16,128,384]{2,0,1:T(8,128)(2,1)}), bf16[16,128,384]{2,0,1:T(8,128)(2,1)}, u32[]{:S(2)}, u32[]{:S(2)}) async-start(bf16[16,128,384]{2,0,1:T(8,128)(2,1)} %copy.75), calls=%async_computation | async-start | bytes 3145728 | tf_op jit(solution)/shard_map/all_to_all | solution.py:17
  35.4 2.2 fusion.110
  39.4 2.1 copy.78
  41.4 14.1 %all-to-all-done = bf16[16,128,384]{2,0,1:T(8,128)(2,1)} async-done(((bf16[16,128,384]{2,0,1:T(8,128)(2,1)}), bf16[16,128,384]{2,0,1:T(8,128)(2,1)}, u32[]{:S(2)}, u32[]{:S(2)}) %all-to-all-start) | async-done | bytes 1572896 | tf_op jit(solution)/shard_map/all_to_all | solution.py:17
  55.5 4.5 %all-to-all-start.1 = ((bf16[16,128,384]{2,0,1:T(8,128)(2,1)}), bf16[16,128,384]{2,0,1:T(8,128)(2,1)}, u32[]{:S(2)}, u32[]{:S(2)}) async-start(bf16[16,128,384]{2,0,1:T(8,128)(2,1)} %copy.78), calls=%async_computation.1 | async-start | bytes 3145728 | tf_op jit(solution)/shard_map/all_to_all | solution.py:17
  60.0 2.8 copy.93
  62.9 7.6 %fusion.59 = bf16[64,32,384]{2,0,1:T(8,128)(2,1)} fusion(bf16[64,32,384]{2,0,1:T(8,128)(2,1)} %bitcast.299, bf16[1,32,64,256]{3,2,1,0:T(8,128)(2,1)S(1)} %copy-done, bf16[1,32,64,256]{3,2,1,0:T(8,128)(2,1)} %param.12), kind=kOutput, calls=%fused_computation.79 | convolution fusion | flops 834404352 | bytes 5242880 | tf_op jit(solution)/shard_map/ifr,inf->nir/dot_general | solution.py:31
  70.5 3.5 copy.95
  74.0 2.8 copy.76
  76.8 3.3 all-to-all-done.1
  80.2 4.6 %all-to-all-start.6 = ((bf16[64,32,384]{2,1,0:T(8,128)(2,1)}), bf16[64,32,384]{2,1,0:T(8,128)(2,1)}, u32[]{:S(2)}, u32[]{:S(2)}) async-start(bf16[64,32,384]{2,1,0:T(8,128)(2,1)} %copy.95), calls=%async_computation.6 | async-start | bytes 3145728 | tf_op jit(solution)/shard_map/all_to_all | solution.py:21
  86.4 8.7 %fusion.34 = (bf16[32,256,384]{1,2,0:T(8,128)(2,1)}, f32[32,384,256]{2,1,0:T(8,128)}) fusion(bf16[64,32,384]{2,0,1:T(8,128)(2,1)S(1)} %bitcast.286, bf16[1,32,64,256]{3,2,1,0:T(8,128)(2,1)S(1)} %copy-done), kind=kOutput, calls=%fused_computation.45 | convolution fusion | flops 430964736 | bytes 21495808 | tf_op jit(solution)/shard_map/nir,inf->ifr/dot_general | solution.py:29
  95.1 11.6 %fusion.6 = bf16[32,256,384]{1,2,0:T(8,128)(2,1)S(1)} fusion(f32[32,384,256]{2,1,0:T(8,128)} %get-tuple-element.33, bf16[64,32,384]{2,0,1:T(8,128)(2,1)S(1)} %bitcast.288, bf16[1,32,64,256]{3,2,1,0:T(8,128)(2,1)S(1)} %copy-done.34), kind=kOutput, calls=%fused_computation.12 | convolution fusion | flops 465567744 | bytes 21495808 | tf_op jit(solution)/shard_map/nir,inf->ifr/dot_general | solution.py:51
  106.8 2.1 fusion.62
  109.4 2.1 copy.81
  111.5 4.4 %all-to-all-start.2 = ((bf16[64,32,384]{2,1,0:T(8,128)(2,1)}), bf16[64,32,384]{2,1,0:T(8,128)(2,1)}, u32[]{:S(2)}, u32[]{:S(2)}) async-start(bf16[64,32,384]{2,1,0:T(8,128)(2,1)} %copy.81), calls=%async_computation.2 | async-start | bytes 3145728 | tf_op jit(solution)/shard_map/all_to_all | solution.py:21
  121.0 2.3 collective-permute-start.1
  123.9 2.1 copy.88
  126.0 10.1 %all-to-all-done.2 = bf16[64,32,384]{2,1,0:T(8,128)(2,1)} async-done(((bf16[64,32,384]{2,1,0:T(8,128)(2,1)}), bf16[64,32,384]{2,1,0:T(8,128)(2,1)}, u32[]{:S(2)}, u32[]{:S(2)}) %all-to-all-start.2) | async-done | bytes 1572896 | tf_op jit(solution)/shard_map/all_to_all | solution.py:21
  136.0 4.8 %all-to-all-start.4 = ((bf16[16,128,384]{2,0,1:T(8,128)(2,1)}), bf16[16,128,384]{2,0,1:T(8,128)(2,1)}, u32[]{:S(2)}, u32[]{:S(2)}) async-start(bf16[16,128,384]{2,0,1:T(8,128)(2,1)} %copy.88), calls=%async_computation.4 | async-start | bytes 3145728 | tf_op jit(solution)/shard_map/all_to_all | solution.py:17
  146.4 5.3 %collective-permute-start = (bf16[2048,384]{1,0:T(8,128)(2,1)}, bf16[2048,384]{1,0:T(8,128)(2,1)S(1)}, u32[]{:S(2)}, u32[]{:S(2)}) collective-permute-start(bf16[2048,384]{1,0:T(8,128)(2,1)} %fusion.49), channel_id=1, source_target_pairs={{0,28},{4,0},{8,4},{12,8},{16,12},{20,16},{24,20},{28,24},{1,29},{... | collective-permute-start | bytes 4718600 | tf_op jit(solution)/shard_map/ppermute | solution.py:9
  151.8 39.8 %collective-permute-done.1 = bf16[2048,384]{1,0:T(8,128)(2,1)} collective-permute-done((bf16[2048,384]{1,0:T(8,128)(2,1)}, bf16[2048,384]{1,0:T(8,128)(2,1)}, u32[]{:S(2)}, u32[]{:S(2)}) %collective-permute-start.1) | collective-permute-done | bytes 1572896 | tf_op jit(solution)/shard_map/ppermute | solution.py:9
  191.6 3.2 fusion.67
  194.7 2.9 copy.99
  197.6 4.5 %all-to-all-start.7 = ((bf16[16,128,384]{2,0,1:T(8,128)(2,1)}), bf16[16,128,384]{2,0,1:T(8,128)(2,1)}, u32[]{:S(2)}, u32[]{:S(2)}) async-start(bf16[16,128,384]{2,0,1:T(8,128)(2,1)} %copy.99), calls=%async_computation.7 | async-start | bytes 3145728 | tf_op jit(solution)/shard_map/all_to_all | solution.py:17
  202.1 2.8 copy.89
  206.7 2.9 copy.84
  209.7 12.6 %all-to-all-done.7 = bf16[16,128,384]{2,0,1:T(8,128)(2,1)} async-done(((bf16[16,128,384]{2,0,1:T(8,128)(2,1)}), bf16[16,128,384]{2,0,1:T(8,128)(2,1)}, u32[]{:S(2)}, u32[]{:S(2)}) %all-to-all-start.7) | async-done | bytes 1572896 | tf_op jit(solution)/shard_map/all_to_all | solution.py:17
  222.3 4.5 %all-to-all-start.3 = ((bf16[16,128,384]{2,0,1:T(8,128)(2,1)}), bf16[16,128,384]{2,0,1:T(8,128)(2,1)}, u32[]{:S(2)}, u32[]{:S(2)}) async-start(bf16[16,128,384]{2,0,1:T(8,128)(2,1)} %copy.84), calls=%async_computation.3 | async-start | bytes 3145728 | tf_op jit(solution)/shard_map/all_to_all | solution.py:17
  226.8 6.4 %fusion.75 = f32[32,384,256]{2,1,0:T(8,128)} fusion(bf16[64,32,384]{2,0,1:T(8,128)(2,1)S(1)} %bitcast.280, bf16[1,32,64,256]{3,2,1,0:T(8,128)(2,1)S(1)} %copy-done), kind=kOutput, calls=%fused_computation.93 | convolution fusion | flops 402653184 | bytes 15204352 | tf_op jit(solution)/shard_map/nir,inf->ifr/dot_general | solution.py:29
  234.9 7.1 %fusion.56 = bf16[64,32,384]{2,0,1:T(8,128)(2,1)} fusion(bf16[64,32,384]{2,0,1:T(8,128)(2,1)S(1)} %bitcast.300, bf16[1,32,64,256]{3,2,1,0:T(8,128)(2,1)S(1)} %copy-done, bf16[1,32,64,256]{3,2,1,0:T(8,128)(2,1)} %param.12), kind=kOutput, calls=%fused_computation.78 | convolution fusion | flops 834404352 | bytes 5242880 | tf_op jit(solution)/shard_map/ifr,inf->nir/dot_general | solution.py:31
  241.9 3.5 copy.103
  246.9 4.7 %all-to-all-start.8 = ((bf16[64,32,384]{2,1,0:T(8,128)(2,1)}), bf16[64,32,384]{2,1,0:T(8,128)(2,1)}, u32[]{:S(2)}, u32[]{:S(2)}) async-start(bf16[64,32,384]{2,1,0:T(8,128)(2,1)} %copy.103), calls=%async_computation.8 | async-start | bytes 3145728 | tf_op jit(solution)/shard_map/all_to_all | solution.py:21
  251.6 9.2 %fusion.65 = bf16[64,32,384]{2,0,1:T(8,128)(2,1)S(1)} fusion(bf16[1,32,64,256]{3,2,1,0:T(8,128)(2,1)} %param.12, f32[32,384,256]{2,1,0:T(8,128)} %fusion.75), kind=kOutput, calls=%fused_computation.83 | convolution fusion | flops 431751168 | bytes 15204352 | tf_op jit(solution)/shard_map/ifr,inf->nir/dot_general | solution.py:31
  260.8 2.1 copy.116
  262.9 2.6 fusion.113
  265.5 6.2 %all-to-all-done.8 = bf16[64,32,384]{2,1,0:T(8,128)(2,1)} async-done(((bf16[64,32,384]{2,1,0:T(8,128)(2,1)}), bf16[64,32,384]{2,1,0:T(8,128)(2,1)}, u32[]{:S(2)}, u32[]{:S(2)}) %all-to-all-start.8) | async-done | bytes 1572896 | tf_op jit(solution)/shard_map/all_to_all | solution.py:21
  271.7 3.6 all-to-all-start.11
  275.3 5.1 %fusion.64 = bf16[64,32,384]{2,0,1:T(8,128)(2,1)S(1)} fusion(bf16[32,256,384]{1,2,0:T(8,128)(2,1)} %get-tuple-element.32, bf16[1,32,64,256]{3,2,1,0:T(8,128)(2,1)} %param.12), kind=kOutput, calls=%fused_computation.82 | convolution fusion | flops 403439616 | bytes 8912896 | tf_op jit(solution)/shard_map/ifr,inf->nir/dot_general | solution.py:31
  280.4 2.1 copy.113
  282.4 2.9 copy.86
  287.6 3.3 fusion.47
  290.9 2.5 collective-permute-start.2
  293.4 1.9 all-to-all-done.11
  295.3 4.6 %all-to-all-start.10 = ((bf16[64,32,384]{2,1,0:T(8,128)(2,1)}), bf16[64,32,384]{2,1,0:T(8,128)(2,1)}, u32[]{:S(2)}, u32[]{:S(2)}) async-start(bf16[64,32,384]{2,1,0:T(8,128)(2,1)} %copy.113), calls=%async_computation.10 | async-start | bytes 3145728 | tf_op jit(solution)/shard_map/all_to_all | solution.py:21
  299.9 13.3 %fusion.13 = bf16[32,256,384]{1,2,0:T(8,128)(2,1)S(1)} fusion(f32[32,384,256]{2,1,0:T(8,128)} %fusion.75, bf16[64,32,384]{2,0,1:T(8,128)(2,1)} %bitcast.297, bf16[1,32,64,256]{3,2,1,0:T(8,128)(2,1)} %param.12), kind=kOutput, calls=%fused_computation.19 | convolution fusion | flops 465567744 | bytes 21495808 | tf_op jit(solution)/shard_map/nir,inf->ifr/dot_general | solution.py:51
  313.2 2.1 fusion.63
  315.9 15.9 %collective-permute-done.2 = bf16[2048,384]{1,0:T(8,128)(2,1)} collective-permute-done((bf16[2048,384]{1,0:T(8,128)(2,1)}, bf16[2048,384]{1,0:T(8,128)(2,1)}, u32[]{:S(2)}, u32[]{:S(2)}) %collective-permute-start.2) | collective-permute-done | bytes 1572896 | tf_op jit(solution)/shard_map/ppermute | solution.py:9
  331.8 2.1 copy.106
  333.8 4.3 %all-to-all-start.9 = ((bf16[64,32,384]{2,1,0:T(8,128)(2,1)}), bf16[64,32,384]{2,1,0:T(8,128)(2,1)}, u32[]{:S(2)}, u32[]{:S(2)}) async-start(bf16[64,32,384]{2,1,0:T(8,128)(2,1)} %copy.106), calls=%async_computation.9 | async-start | bytes 3145728 | tf_op jit(solution)/shard_map/all_to_all | solution.py:21
  338.2 5.5 %fusion.112 = f32[32,64,256]{2,1,0:T(8,128)} fusion(bf16[64,32,384]{2,0,1:T(8,128)(2,1)S(1)} %bitcast.287, bf16[32,256,384]{1,2,0:T(8,128)(2,1)} %copy-done.1), kind=kOutput, calls=%fused_computation.128 | convolution fusion | flops 402653184 | bytes 9961472 | tf_op jit(solution)/shard_map/nir,ifr->inf/dot_general | solution.py:56
  350.9 7.3 %all-to-all-done.9 = bf16[64,32,384]{2,1,0:T(8,128)(2,1)} async-done(((bf16[64,32,384]{2,1,0:T(8,128)(2,1)}), bf16[64,32,384]{2,1,0:T(8,128)(2,1)}, u32[]{:S(2)}, u32[]{:S(2)}) %all-to-all-start.9) | async-done | bytes 1572896 | tf_op jit(solution)/shard_map/all_to_all | solution.py:21
  362.1 2.0 collective-permute-start.3
  364.1 9.8 %add_bitcast_fusion = f32[1,32,64,256]{3,2,1,0:T(8,128)} fusion(f32[32,64,256]{2,1,0:T(8,128)S(1)} %copy-done.32, bf16[64,32,384]{2,0,1:T(8,128)(2,1)S(1)} %bitcast.298, f32[32,384,256]{2,1,0:T(8,128)} %fusion.75), kind=kOutput, calls=%fused_computation.62 | convolution fusion | flops 431489024 | bytes 18350080 | tf_op jit(solution)/shard_map/ifr,nir->inf/dot_general | solution.py:48
  373.9 2.6 add_bitcast_fusion.1
  376.5 3.4 bitcast_convert_fusion.1
  382.0 16.6 %collective-permute-done.3 = bf16[2048,384]{1,0:T(8,128)(2,1)} collective-permute-done((bf16[2048,384]{1,0:T(8,128)(2,1)}, bf16[2048,384]{1,0:T(8,128)(2,1)}, u32[]{:S(2)}, u32[]{:S(2)}) %collective-permute-start.3) | collective-permute-done | bytes 1572896 | tf_op jit(solution)/shard_map/ppermute | solution.py:9
  398.6 3.3 bitcast_convert_fusion
  (110 shorter events, 39.8 us)
Async XLA Ops:
  0.6 62.2 %copy-start = (bf16[1,32,64,256]{3,2,1,0:T(8,128)(2,1)S(1)}, bf16[1,32,64,256]{3,2,1,0:T(8,128)(2,1)}, u32[]{:S(2)}) copy-start(bf16[1,32,64,256]{3,2,1,0:T(8,128)(2,1)} %param.11) | copy-start | bytes 3145732
  0.6 2.2 copy-start.3
  5.5 24.3 %all-to-all-start.5 = ((bf16[16,128,384]{2,0,1:T(8,128)(2,1)}), bf16[16,128,384]{2,0,1:T(8,128)(2,1)S(1)}, u32[]{:S(2)}, u32[]{:S(2)}) async-start(bf16[16,128,384]{2,0,1:T(8,128)(2,1)} %copy.92), calls=%async_computation.5 | async-start | bytes 3145728 | tf_op jit(solution)/shard_map/all_to_all | solution.py:17
  9.7 3.3 copy-start.19
  11.9 1.2 copy-start.7
  29.8 1.1 copy-start.30
  31.0 24.5 %all-to-all-start = ((bf16[16,128,384]{2,0,1:T(8,128)(2,1)}), bf16[16,128,384]{2,0,1:T(8,128)(2,1)}, u32[]{:S(2)}, u32[]{:S(2)}) async-start(bf16[16,128,384]{2,0,1:T(8,128)(2,1)} %copy.75), calls=%async_computation | async-start | bytes 3145728 | tf_op jit(solution)/shard_map/all_to_all | solution.py:17
  37.6 1.2 copy-start.9
  37.6 85.7 %copy-start.5 = (bf16[1,1,2048,384]{3,2,1,0:T(8,128)(2,1)}, bf16[1,1,2048,384]{3,2,1,0:T(8,128)(2,1)S(1)}, u32[]{:S(2)}) copy-start(bf16[1,1,2048,384]{3,2,1,0:T(8,128)(2,1)S(1)} %get-tuple-element.31) | copy-start | bytes 4718596
  55.5 24.7 %all-to-all-start.1 = ((bf16[16,128,384]{2,0,1:T(8,128)(2,1)}), bf16[16,128,384]{2,0,1:T(8,128)(2,1)}, u32[]{:S(2)}, u32[]{:S(2)}) async-start(bf16[16,128,384]{2,0,1:T(8,128)(2,1)} %copy.78), calls=%async_computation.1 | async-start | bytes 3145728 | tf_op jit(solution)/shard_map/all_to_all | solution.py:17
  80.2 31.3 %all-to-all-start.6 = ((bf16[64,32,384]{2,1,0:T(8,128)(2,1)}), bf16[64,32,384]{2,1,0:T(8,128)(2,1)}, u32[]{:S(2)}, u32[]{:S(2)}) async-start(bf16[64,32,384]{2,1,0:T(8,128)(2,1)} %copy.95), calls=%async_computation.6 | async-start | bytes 3145728 | tf_op jit(solution)/shard_map/all_to_all | solution.py:21
  86.4 8.7 %copy-start.24 = (bf16[16,4,32,384]{3,0,1,2:T(8,128)(2,1)}, bf16[16,4,32,384]{3,0,1,2:T(8,128)(2,1)S(1)}, u32[]{:S(2)}) copy-start(bf16[16,4,32,384]{3,0,1,2:T(8,128)(2,1)S(1)} %copy.79) | copy-start | bytes 4718596
  86.4 8.7 %copy-start.26 = (bf16[16,4,32,384]{3,0,1,2:T(8,128)(2,1)S(1)}, bf16[16,4,32,384]{3,0,1,2:T(8,128)(2,1)}, u32[]{:S(2)}) copy-start(bf16[16,4,32,384]{3,0,1,2:T(8,128)(2,1)} %copy.76) | copy-start | bytes 4718596
  86.4 8.7 %copy-start.34 = (bf16[1,32,64,256]{3,2,1,0:T(8,128)(2,1)S(1)}, bf16[1,32,64,256]{3,2,1,0:T(8,128)(2,1)}, u32[]{:S(2)}) copy-start(bf16[1,32,64,256]{3,2,1,0:T(8,128)(2,1)} %param.12) | copy-start | bytes 3145732
  106.8 2.6 copy-start.1
  111.5 24.5 %all-to-all-start.2 = ((bf16[64,32,384]{2,1,0:T(8,128)(2,1)}), bf16[64,32,384]{2,1,0:T(8,128)(2,1)}, u32[]{:S(2)}, u32[]{:S(2)}) async-start(bf16[64,32,384]{2,1,0:T(8,128)(2,1)} %copy.81), calls=%async_computation.2 | async-start | bytes 3145728 | tf_op jit(solution)/shard_map/all_to_all | solution.py:21
  115.9 1.8 copy-start.20
  117.6 1.9 copy-start.17
  121.0 70.6 %collective-permute-start.1 = (bf16[2048,384]{1,0:T(8,128)(2,1)}, bf16[2048,384]{1,0:T(8,128)(2,1)}, u32[]{:S(2)}, u32[]{:S(2)}) collective-permute-start(bf16[2048,384]{1,0:T(8,128)(2,1)} %fusion.48), channel_id=1, source_target_pairs={{0,4},{4,8},{8,12},{12,16},{16,20},{20,24},{24,28},{28,0},{1,5},{5... | collective-permute-start | bytes 4718600 | tf_op jit(solution)/shard_map/ppermute | solution.py:9
  136.0 61.6 %all-to-all-start.4 = ((bf16[16,128,384]{2,0,1:T(8,128)(2,1)}), bf16[16,128,384]{2,0,1:T(8,128)(2,1)}, u32[]{:S(2)}, u32[]{:S(2)}) async-start(bf16[16,128,384]{2,0,1:T(8,128)(2,1)} %copy.88), calls=%async_computation.4 | async-start | bytes 3145728 | tf_op jit(solution)/shard_map/all_to_all | solution.py:17
  142.4 1.2 copy-start.15
  142.4 2.5 copy-start.18
  146.4 58.5 %collective-permute-start = (bf16[2048,384]{1,0:T(8,128)(2,1)}, bf16[2048,384]{1,0:T(8,128)(2,1)S(1)}, u32[]{:S(2)}, u32[]{:S(2)}) collective-permute-start(bf16[2048,384]{1,0:T(8,128)(2,1)} %fusion.49), channel_id=1, source_target_pairs={{0,28},{4,0},{8,4},{12,8},{16,12},{20,16},{24,20},{28,24},{1,29},{... | collective-permute-start | bytes 4718600 | tf_op jit(solution)/shard_map/ppermute | solution.py:9
  197.6 7.3 %copy-start.21 = (bf16[1,16,128,128]{3,2,1,0:T(8,128)(2,1)S(1)}, bf16[1,16,128,128]{3,2,1,0:T(8,128)(2,1)}, u32[]{:S(2)}) copy-start(bf16[1,16,128,128]{3,2,1,0:T(8,128)(2,1)} %param.13) | copy-start | bytes 1572868
  197.6 24.6 %all-to-all-start.7 = ((bf16[16,128,384]{2,0,1:T(8,128)(2,1)}), bf16[16,128,384]{2,0,1:T(8,128)(2,1)}, u32[]{:S(2)}, u32[]{:S(2)}) async-start(bf16[16,128,384]{2,0,1:T(8,128)(2,1)} %copy.99), calls=%async_computation.7 | async-start | bytes 3145728 | tf_op jit(solution)/shard_map/all_to_all | solution.py:17
  205.0 4.7 %copy-start.11 = (bf16[2048,384]{1,0:T(8,128)(2,1)}, bf16[2048,384]{1,0:T(8,128)(2,1)S(1)}, u32[]{:S(2)}) copy-start(bf16[2048,384]{1,0:T(8,128)(2,1)S(1)} %collective-permute-done) | copy-start | bytes 4718596
  222.3 4.5 %copy-start.13 = (bf16[16,4,32,384]{3,0,1,2:T(8,128)(2,1)S(1)}, bf16[16,4,32,384]{3,0,1,2:T(8,128)(2,1)}, u32[]{:S(2)}) copy-start(bf16[16,4,32,384]{3,0,1,2:T(8,128)(2,1)} %copy.89) | copy-start | bytes 4718596
  222.3 24.6 %all-to-all-start.3 = ((bf16[16,128,384]{2,0,1:T(8,128)(2,1)}), bf16[16,128,384]{2,0,1:T(8,128)(2,1)}, u32[]{:S(2)}, u32[]{:S(2)}) async-start(bf16[16,128,384]{2,0,1:T(8,128)(2,1)} %copy.84), calls=%async_computation.3 | async-start | bytes 3145728 | tf_op jit(solution)/shard_map/all_to_all | solution.py:17
  246.9 16.0 %slice-start = ((s8[6291456]{0:T(1024)(128)(4,1)}), s8[2097152]{0:T(1024)(128)(4,1)S(1)}, s32[]{:S(2)}) async-start(s8[6291456]{0:T(1024)(128)(4,1)} %bitcast.268), calls=%async_computation.12 | async-start | bytes 4194304
  246.9 24.8 %all-to-all-start.8 = ((bf16[64,32,384]{2,1,0:T(8,128)(2,1)}), bf16[64,32,384]{2,1,0:T(8,128)(2,1)}, u32[]{:S(2)}, u32[]{:S(2)}) async-start(bf16[64,32,384]{2,1,0:T(8,128)(2,1)} %copy.103), calls=%async_computation.8 | async-start | bytes 3145728 | tf_op jit(solution)/shard_map/all_to_all | solution.py:21
  251.6 11.3 %slice-start.1 = ((s8[6291456]{0:T(1024)(128)(4,1)}), s8[4194304]{0:T(1024)(128)(4,1)S(1)}, s32[]{:S(2)}) async-start(s8[6291456]{0:T(1024)(128)(4,1)} %bitcast.268), calls=%async_computation.13 | async-start | bytes 8388608
  260.8 2.1 copy-start.27
  271.7 23.6 %all-to-all-start.11 = ((bf16[64,32,384]{2,1,0:T(8,128)(2,1)}), bf16[64,32,384]{2,1,0:T(8,128)(2,1)S(1)}, u32[]{:S(2)}, u32[]{:S(2)}) async-start(bf16[64,32,384]{2,1,0:T(8,128)(2,1)} %copy.116), calls=%async_computation.11 | async-start | bytes 3145728 | tf_op jit(solution)/shard_map/all_to_all | solution.py:21
  282.4 4.6 %copy-start.22 = (bf16[1,16,128,128]{3,2,1,0:T(8,128)(2,1)S(1)}, bf16[1,16,128,128]{3,2,1,0:T(8,128)(2,1)}, u32[]{:S(2)}) copy-start(bf16[1,16,128,128]{3,2,1,0:T(8,128)(2,1)} %param.13) | copy-start | bytes 1572868
  290.9 40.9 %collective-permute-start.2 = (bf16[2048,384]{1,0:T(8,128)(2,1)}, bf16[2048,384]{1,0:T(8,128)(2,1)}, u32[]{:S(2)}, u32[]{:S(2)}) collective-permute-start(bf16[2048,384]{1,0:T(8,128)(2,1)} %fusion.47), channel_id=1, source_target_pairs={{0,4},{4,8},{8,12},{12,16},{16,20},{20,24},{24,28},{28,0},{1,5},{5... | collective-permute-start | bytes 4718600 | tf_op jit(solution)/shard_map/ppermute | solution.py:9
  295.3 17.9 %copy-start.28 = (bf16[64,32,384]{2,1,0:T(8,128)(2,1)}, bf16[64,32,384]{2,1,0:T(8,128)(2,1)S(1)}, u32[]{:S(2)}) copy-start(bf16[64,32,384]{2,1,0:T(8,128)(2,1)S(1)} %all-to-all-done.11) | copy-start | bytes 4718596
  295.3 38.5 %all-to-all-start.10 = ((bf16[64,32,384]{2,1,0:T(8,128)(2,1)}), bf16[64,32,384]{2,1,0:T(8,128)(2,1)}, u32[]{:S(2)}, u32[]{:S(2)}) async-start(bf16[64,32,384]{2,1,0:T(8,128)(2,1)} %copy.113), calls=%async_computation.10 | async-start | bytes 3145728 | tf_op jit(solution)/shard_map/all_to_all | solution.py:21
  313.2 2.7 copy-start.2
  315.9 22.3 %copy-start.25 = (bf16[16,4,32,384]{3,0,1,2:T(8,128)(2,1)S(1)}, bf16[16,4,32,384]{3,0,1,2:T(8,128)(2,1)}, u32[]{:S(2)}) copy-start(bf16[16,4,32,384]{3,0,1,2:T(8,128)(2,1)} %copy-done.24) | copy-start | bytes 4718596
  333.8 24.5 %all-to-all-start.9 = ((bf16[64,32,384]{2,1,0:T(8,128)(2,1)}), bf16[64,32,384]{2,1,0:T(8,128)(2,1)}, u32[]{:S(2)}, u32[]{:S(2)}) async-start(bf16[64,32,384]{2,1,0:T(8,128)(2,1)} %copy.106), calls=%async_computation.9 | async-start | bytes 3145728 | tf_op jit(solution)/shard_map/all_to_all | solution.py:21
  338.2 5.5 %copy-start.29 = (bf16[64,32,384]{2,1,0:T(8,128)(2,1)S(1)}, bf16[64,32,384]{2,1,0:T(8,128)(2,1)}, u32[]{:S(2)}) copy-start(bf16[64,32,384]{2,1,0:T(8,128)(2,1)} %copy-done.28) | copy-start | bytes 4718596
  343.6 2.1 copy-start.10
  343.6 2.4 copy-start.16
  343.9 3.8 copy-start.8
  347.7 1.4 copy-start.12
  349.2 10.8 %copy-start.4 = (bf16[1,16,128,128]{3,2,1,0:T(8,128)(2,1)S(1)}, bf16[1,16,128,128]{3,2,1,0:T(8,128)(2,1)}, u32[]{:S(2)}) copy-start(bf16[1,16,128,128]{3,2,1,0:T(8,128)(2,1)} %param.10) | copy-start | bytes 1572868
  360.0 4.1 %copy-start.33 = (bf16[4,16,32,384]{3,1,0,2:T(8,128)(2,1)S(1)}, bf16[4,16,32,384]{3,1,0,2:T(8,128)(2,1)}, u32[]{:S(2)}) copy-start(bf16[4,16,32,384]{3,1,0,2:T(8,128)(2,1)} %copy.86) | copy-start | bytes 4718596
  360.5 3.5 copy-start.32
  360.6 13.3 %slice-start.2 = ((s8[6291456]{0:T(1024)(128)(4,1)}), s8[4194304]{0:T(1024)(128)(4,1)S(1)}, s32[]{:S(2)}) async-start(s8[6291456]{0:T(1024)(128)(4,1)} %bitcast.270), calls=%async_computation.14 | async-start | bytes 8388608
  362.1 11.8 %slice-start.3 = ((s8[6291456]{0:T(1024)(128)(4,1)}), s8[2097152]{0:T(1024)(128)(4,1)S(1)}, s32[]{:S(2)}) async-start(s8[6291456]{0:T(1024)(128)(4,1)} %bitcast.270), calls=%async_computation.15 | async-start | bytes 4194304
  362.1 11.8 %copy-start.14 = (bf16[16,4,32,384]{3,0,1,2:T(8,128)(2,1)S(1)}, bf16[16,4,32,384]{3,0,1,2:T(8,128)(2,1)}, u32[]{:S(2)}) copy-start(bf16[16,4,32,384]{3,0,1,2:T(8,128)(2,1)} %copy.89) | copy-start | bytes 4718596
  362.1 11.8 %copy-start.23 = (f32[32,64,256]{2,1,0:T(8,128)S(1)}, f32[32,64,256]{2,1,0:T(8,128)}, u32[]{:S(2)}) copy-start(f32[32,64,256]{2,1,0:T(8,128)} %fusion.112) | copy-start | bytes 6291460
  362.1 36.5 %collective-permute-start.3 = (bf16[2048,384]{1,0:T(8,128)(2,1)}, bf16[2048,384]{1,0:T(8,128)(2,1)}, u32[]{:S(2)}, u32[]{:S(2)}) collective-permute-start(bf16[2048,384]{1,0:T(8,128)(2,1)} %fusion.46), channel_id=1, source_target_pairs={{0,28},{4,0},{8,4},{12,8},{16,12},{20,16},{24,20},{28,24},{1,29},{... | collective-permute-start | bytes 4718600 | tf_op jit(solution)/shard_map/ppermute | solution.py:9
  376.5 3.4 copy-start.6
  376.5 3.4 copy-start.31
where the time goes:
time: 408 us; the launch traced here: 402 us
  waiting for transfers between devices  143 us (35%)
  matrix products  108 us (26%)
  local copies, waits for them, and re-layouts  65.1 us (16%)
  starting transfers between devices  64.9 us (16%)
  other arithmetic  18.8 us (5%)
    ppermute x4, waiting for transfers between devices, shifted(): lax.ppermute(value, axis, [(i, (i + by) % count) for i in range(count)])  72.2 us
    all_to_all x6, waiting for transfers between devices, to_columns(): lax.all_to_all(value, 'tensor', split_axis=1, concat_axis=0, tiled=True)  45.6 us
    dot_general x4, matrix products, front(): jnp.einsum('ifr,inf->nir', hidden, first_down, preferred_element_type=jnp...  29 us
    all_to_all x6, starting transfers between devices, to_columns(): lax.all_to_all(value, 'tensor', split_axis=1, concat_axis=0, tiled=True)  26.8 us
    all_to_all x6, starting transfers between devices, to_rows(): lax.all_to_all(value, 'tensor', split_axis=0, concat_axis=1, tiled=True)  26 us
    all_to_all x6, waiting for transfers between devices, to_rows(): lax.all_to_all(value, 'tensor', split_axis=0, concat_axis=1, tiled=True)  25.5 us
    dot_general x2, matrix products, backward(): jnp.einsum('nir,inf->ifr', grad_folded, first_down, preferred_element_typ...  24.9 us
    dot_general x2, matrix products, front(): jnp.einsum('nir,inf->ifr', spread, second_up, preferred_element_type=jnp....  15.1 us
  transfers between devices with their start and end apart: 16, of which 12 were waited for; matrix products, arithmetic and copies ran while one was open for 43% of the time, Pallas kernels for 0%

commit v1 on v0

--- a/solution.py
+++ b/solution.py
@@ -98,6 +98,7 @@
         stored, cotangent, up_first, up_second, down_first, down_second, behind
     )
     sent_back = (cotangent + grad_step).astype(jnp.bfloat16)
+    later, sent_back = lax.optimization_barrier((stash[1, 0], sent_back))
     near_cotangent = shifted(sent_back, "pipe", -1)
     near_activation, sent_back = lax.optimization_barrier((near_activation, sent_back))
 
@@ -108,7 +109,7 @@
     sent = output.astype(jnp.bfloat16)
     last_activation = shifted(sent, "pipe", 1)
 
-    stored = stash[1, 0].reshape(blocks, width, rows)
+    stored = later.reshape(blocks, width, rows)
     behind = front(stored, up_first, up_second, down_first)
     grad_step, terms, last_activation = backward(
         stored, near_cotangent, up_first, up_second, down_first, down_second, behind,

time: 408 us -> 413 us (1.012)
    all_to_all x6, waiting for transfers between devices: 45.6 us -> 55 us  [to_columns(): lax.all_to_all(value, 'tensor', split_axis=1, concat_axis=0, tiled=True)]
    all_to_all x6, waiting for transfers between devices: 25.5 us -> 20.4 us  [to_rows(): lax.all_to_all(value, 'tensor', split_axis=0, concat_axis=1, tiled=True)]
  transfers between devices with their start and end apart: 16 -> 16, of which waited for: 12 -> 11; matrix products, arithmetic and copies ran while one was open for 43% -> 42% of each run, Pallas kernels for 0% -> 0%
where the time goes in v1:
time: 413 us; the launch traced here: 407 us
  waiting for transfers between devices  145 us (35%)
  matrix products  110 us (27%)
  local copies, waits for them, and re-layouts  66.6 us (16%)
  starting transfers between devices  65 us (16%)
  other arithmetic  18.8 us (5%)
    ppermute x4, waiting for transfers between devices, shifted(): lax.ppermute(value, axis, [(i, (i + by) % count) for i in range(count)])  69.7 us
    all_to_all x6, waiting for transfers between devices, to_columns(): lax.all_to_all(value, 'tensor', split_axis=1, concat_axis=0, tiled=True)  55 us
    dot_general x4, matrix products, front(): jnp.einsum('ifr,inf->nir', hidden, first_down, preferred_element_type=jnp...  29 us
    all_to_all x6, starting transfers between devices, to_columns(): lax.all_to_all(value, 'tensor', split_axis=1, concat_axis=0, tiled=True)  26.5 us
    all_to_all x6, starting transfers between devices, to_rows(): lax.all_to_all(value, 'tensor', split_axis=0, concat_axis=1, tiled=True)  26.2 us
    dot_general x2, matrix products, backward(): jnp.einsum('nir,inf->ifr', grad_folded, first_down, preferred_element_typ...  24.9 us
    all_to_all x6, waiting for transfers between devices, to_rows(): lax.all_to_all(value, 'tensor', split_axis=0, concat_axis=1, tiled=True)  20.4 us
    dot_general x2, matrix products, front(): jnp.einsum('nir,inf->ifr', spread, second_up, preferred_element_type=jnp....  15.1 us
  transfers between devices with their start and end apart: 16, of which 11 were waited for; matrix products, arithmetic and copies ran while one was open for 42% of the time, Pallas kernels for 0%

profile of v1, /device:TPU:0, one launch (start us, length us, event | category | flops | bytes accessed | tf_op | source)
XLA Modules:
  0.0 406.5 jit_solution(11089411180344069506)
XLA Ops:
  0.7 2.2 convert_element_type.130
  3.5 2.1 copy.96
  5.5 4.2 %all-to-all-start.5 = ((bf16[16,128,384]{2,0,1:T(8,128)(2,1)}), bf16[16,128,384]{2,0,1:T(8,128)(2,1)S(1)}, u32[]{:S(2)}, u32[]{:S(2)}) async-start(bf16[16,128,384]{2,0,1:T(8,128)(2,1)} %copy.96), calls=%async_computation.5 | async-start | bytes 3145728 | tf_op jit(solution)/shard_map/all_to_all | solution.py:17
  9.8 2.1 convert_element_type.115
  13.6 2.1 copy.78
  15.7 14.2 %all-to-all-done.5 = bf16[16,128,384]{2,0,1:T(8,128)(2,1)S(1)} async-done(((bf16[16,128,384]{2,0,1:T(8,128)(2,1)}), bf16[16,128,384]{2,0,1:T(8,128)(2,1)S(1)}, u32[]{:S(2)}, u32[]{:S(2)}) %all-to-all-start.5) | async-done | bytes 1572896 | tf_op jit(solution)/shard_map/all_to_all | solution.py:17
  31.0 4.4 %all-to-all-start = ((bf16[16,128,384]{2,0,1:T(8,128)(2,1)}), bf16[16,128,384]{2,0,1:T(8,128)(2,1)}, u32[]{:S(2)}, u32[]{:S(2)}) async-start(bf16[16,128,384]{2,0,1:T(8,128)(2,1)} %copy.78), calls=%async_computation | async-start | bytes 3145728 | tf_op jit(solution)/shard_map/all_to_all | solution.py:17
  35.3 2.2 fusion.111
  39.3 2.1 copy.81
  41.4 14.1 %all-to-all-done = bf16[16,128,384]{2,0,1:T(8,128)(2,1)} async-done(((bf16[16,128,384]{2,0,1:T(8,128)(2,1)}), bf16[16,128,384]{2,0,1:T(8,128)(2,1)}, u32[]{:S(2)}, u32[]{:S(2)}) %all-to-all-start) | async-done | bytes 1572896 | tf_op jit(solution)/shard_map/all_to_all | solution.py:17
  55.5 4.9 %all-to-all-start.1 = ((bf16[16,128,384]{2,0,1:T(8,128)(2,1)}), bf16[16,128,384]{2,0,1:T(8,128)(2,1)}, u32[]{:S(2)}, u32[]{:S(2)}) async-start(bf16[16,128,384]{2,0,1:T(8,128)(2,1)} %copy.81), calls=%async_computation.1 | async-start | bytes 3145728 | tf_op jit(solution)/shard_map/all_to_all | solution.py:17
  60.4 2.8 copy.97
  63.2 7.6 %fusion.59 = bf16[64,32,384]{2,0,1:T(8,128)(2,1)} fusion(bf16[64,32,384]{2,0,1:T(8,128)(2,1)} %bitcast.303, bf16[1,32,64,256]{3,2,1,0:T(8,128)(2,1)S(1)} %copy-done, bf16[1,32,64,256]{3,2,1,0:T(8,128)(2,1)} %param.12), kind=kOutput, calls=%fused_computation.80 | convolution fusion | flops 834404352 | bytes 5242880 | tf_op jit(solution)/shard_map/ifr,inf->nir/dot_general | solution.py:31
  70.8 3.5 copy.99
  74.3 2.8 copy.79
  77.1 3.3 all-to-all-done.1
  80.5 4.5 %all-to-all-start.6 = ((bf16[64,32,384]{2,1,0:T(8,128)(2,1)}), bf16[64,32,384]{2,1,0:T(8,128)(2,1)}, u32[]{:S(2)}, u32[]{:S(2)}) async-start(bf16[64,32,384]{2,1,0:T(8,128)(2,1)} %copy.99), calls=%async_computation.6 | async-start | bytes 3145728 | tf_op jit(solution)/shard_map/all_to_all | solution.py:21
  86.7 8.7 %fusion.34 = (bf16[32,256,384]{1,2,0:T(8,128)(2,1)}, f32[32,384,256]{2,1,0:T(8,128)}) fusion(bf16[64,32,384]{2,0,1:T(8,128)(2,1)S(1)} %bitcast.290, bf16[1,32,64,256]{3,2,1,0:T(8,128)(2,1)S(1)} %copy-done), kind=kOutput, calls=%fused_computation.45 | convolution fusion | flops 430964736 | bytes 21495808 | tf_op jit(solution)/shard_map/nir,inf->ifr/dot_general | solution.py:29
  95.5 11.6 %fusion.6 = bf16[32,256,384]{1,2,0:T(8,128)(2,1)S(1)} fusion(f32[32,384,256]{2,1,0:T(8,128)} %get-tuple-element.37, bf16[64,32,384]{2,0,1:T(8,128)(2,1)S(1)} %bitcast.292, bf16[1,32,64,256]{3,2,1,0:T(8,128)(2,1)S(1)} %copy-done.34), kind=kOutput, calls=%fused_computation.12 | convolution fusion | flops 465567744 | bytes 21495808 | tf_op jit(solution)/shard_map/nir,inf->ifr/dot_general | solution.py:51
  107.1 2.1 fusion.62
  109.8 2.1 copy.84
  111.9 4.4 %all-to-all-start.2 = ((bf16[64,32,384]{2,1,0:T(8,128)(2,1)}), bf16[64,32,384]{2,1,0:T(8,128)(2,1)}, u32[]{:S(2)}, u32[]{:S(2)}) async-start(bf16[64,32,384]{2,1,0:T(8,128)(2,1)} %copy.84), calls=%async_computation.2 | async-start | bytes 3145728 | tf_op jit(solution)/shard_map/all_to_all | solution.py:21
  121.3 2.3 collective-permute-start.1
  123.6 12.7 %all-to-all-done.2 = bf16[64,32,384]{2,1,0:T(8,128)(2,1)} async-done(((bf16[64,32,384]{2,1,0:T(8,128)(2,1)}), bf16[64,32,384]{2,1,0:T(8,128)(2,1)}, u32[]{:S(2)}, u32[]{:S(2)}) %all-to-all-start.2) | async-done | bytes 1572896 | tf_op jit(solution)/shard_map/all_to_all | solution.py:21
  143.7 2.9 copy.91
  146.6 4.3 %all-to-all-start.4 = ((bf16[16,128,384]{2,0,1:T(8,128)(2,1)}), bf16[16,128,384]{2,0,1:T(8,128)(2,1)}, u32[]{:S(2)}, u32[]{:S(2)}) async-start(bf16[16,128,384]{2,0,1:T(8,128)(2,1)} %copy.91), calls=%async_computation.4 | async-start | bytes 3145728 | tf_op jit(solution)/shard_map/all_to_all | solution.py:17
  151.0 5.6 %collective-permute-start = (bf16[2048,384]{1,0:T(8,128)(2,1)}, bf16[2048,384]{1,0:T(8,128)(2,1)S(1)}, u32[]{:S(2)}, u32[]{:S(2)}) collective-permute-start(bf16[2048,384]{1,0:T(8,128)(2,1)} %fusion.49), channel_id=1, source_target_pairs={{0,28},{4,0},{8,4},{12,8},{16,12},{20,16},{24,20},{28,24},{1,29},{... | collective-permute-start | bytes 4718600 | tf_op jit(solution)/shard_map/ppermute | solution.py:9
  156.6 35.3 %collective-permute-done.1 = bf16[2048,384]{1,0:T(8,128)(2,1)} collective-permute-done((bf16[2048,384]{1,0:T(8,128)(2,1)}, bf16[2048,384]{1,0:T(8,128)(2,1)}, u32[]{:S(2)}, u32[]{:S(2)}) %collective-permute-start.1) | collective-permute-done | bytes 1572896 | tf_op jit(solution)/shard_map/ppermute | solution.py:9
  191.9 3.2 fusion.68
  195.1 3.0 copy.103
  198.1 4.3 %all-to-all-start.7 = ((bf16[16,128,384]{2,0,1:T(8,128)(2,1)}), bf16[16,128,384]{2,0,1:T(8,128)(2,1)}, u32[]{:S(2)}, u32[]{:S(2)}) async-start(bf16[16,128,384]{2,0,1:T(8,128)(2,1)} %copy.103), calls=%async_computation.7 | async-start | bytes 3145728 | tf_op jit(solution)/shard_map/all_to_all | solution.py:17
  202.5 1.8 fusion.66
  204.2 2.9 copy.87
  207.1 15.4 %all-to-all-done.7 = bf16[16,128,384]{2,0,1:T(8,128)(2,1)} async-done(((bf16[16,128,384]{2,0,1:T(8,128)(2,1)}), bf16[16,128,384]{2,0,1:T(8,128)(2,1)}, u32[]{:S(2)}, u32[]{:S(2)}) %all-to-all-start.7) | async-done | bytes 1572896 | tf_op jit(solution)/shard_map/all_to_all | solution.py:17
  222.6 4.4 %all-to-all-start.3 = ((bf16[16,128,384]{2,0,1:T(8,128)(2,1)}), bf16[16,128,384]{2,0,1:T(8,128)(2,1)}, u32[]{:S(2)}, u32[]{:S(2)}) async-start(bf16[16,128,384]{2,0,1:T(8,128)(2,1)} %copy.87), calls=%async_computation.3 | async-start | bytes 3145728 | tf_op jit(solution)/shard_map/all_to_all | solution.py:17
  228.7 7.1 %fusion.56 = bf16[64,32,384]{2,0,1:T(8,128)(2,1)} fusion(bf16[64,32,384]{2,0,1:T(8,128)(2,1)S(1)} %bitcast.304, bf16[1,32,64,256]{3,2,1,0:T(8,128)(2,1)S(1)} %copy-done, bf16[1,32,64,256]{3,2,1,0:T(8,128)(2,1)} %param.12), kind=kOutput, calls=%fused_computation.79 | convolution fusion | flops 834404352 | bytes 5242880 | tf_op jit(solution)/shard_map/ifr,inf->nir/dot_general | solution.py:31
  235.7 3.5 copy.107
  239.2 7.9 %all-to-all-done.3 = bf16[16,128,384]{2,0,1:T(8,128)(2,1)} async-done(((bf16[16,128,384]{2,0,1:T(8,128)(2,1)}), bf16[16,128,384]{2,0,1:T(8,128)(2,1)}, u32[]{:S(2)}, u32[]{:S(2)}) %all-to-all-start.3) | async-done | bytes 1572896 | tf_op jit(solution)/shard_map/all_to_all | solution.py:17
  247.1 4.5 %all-to-all-start.8 = ((bf16[64,32,384]{2,1,0:T(8,128)(2,1)}), bf16[64,32,384]{2,1,0:T(8,128)(2,1)}, u32[]{:S(2)}, u32[]{:S(2)}) async-start(bf16[64,32,384]{2,1,0:T(8,128)(2,1)} %copy.107), calls=%async_computation.8 | async-start | bytes 3145728 | tf_op jit(solution)/shard_map/all_to_all | solution.py:21
  251.6 5.2 %fusion.64 = bf16[64,32,384]{2,0,1:T(8,128)(2,1)S(1)} fusion(bf16[32,256,384]{1,2,0:T(8,128)(2,1)} %get-tuple-element.36, bf16[1,32,64,256]{3,2,1,0:T(8,128)(2,1)} %param.12), kind=kOutput, calls=%fused_computation.83 | convolution fusion | flops 403439616 | bytes 8912896 | tf_op jit(solution)/shard_map/ifr,inf->nir/dot_general | solution.py:31
  256.9 2.1 copy.118
  259.0 2.6 fusion.113
  264.4 6.4 %fusion.76 = f32[32,384,256]{2,1,0:T(8,128)} fusion(bf16[64,32,384]{2,0,1:T(8,128)(2,1)S(1)} %bitcast.286, bf16[1,32,64,256]{3,2,1,0:T(8,128)(2,1)S(1)} %copy-done), kind=kOutput, calls=%fused_computation.96 | convolution fusion | flops 402653184 | bytes 15204352 | tf_op jit(solution)/shard_map/nir,inf->ifr/dot_general | solution.py:29
  271.7 4.0 all-to-all-start.10
  275.7 9.1 %fusion.65 = bf16[64,32,384]{2,0,1:T(8,128)(2,1)S(1)} fusion(bf16[1,32,64,256]{3,2,1,0:T(8,128)(2,1)} %param.12, f32[32,384,256]{2,1,0:T(8,128)} %fusion.76), kind=kOutput, calls=%fused_computation.84 | convolution fusion | flops 431751168 | bytes 15204352 | tf_op jit(solution)/shard_map/ifr,inf->nir/dot_general | solution.py:31
  284.8 2.1 copy.121
  286.9 2.9 copy.89
  292.1 3.3 fusion.47
  295.3 2.5 collective-permute-start.2
  297.8 4.5 %all-to-all-start.11 = ((bf16[64,32,384]{2,1,0:T(8,128)(2,1)}), bf16[64,32,384]{2,1,0:T(8,128)(2,1)}, u32[]{:S(2)}, u32[]{:S(2)}) async-start(bf16[64,32,384]{2,1,0:T(8,128)(2,1)} %copy.121), calls=%async_computation.11 | async-start | bytes 3145728 | tf_op jit(solution)/shard_map/all_to_all | solution.py:21
  302.3 13.3 %fusion.13 = bf16[32,256,384]{1,2,0:T(8,128)(2,1)S(1)} fusion(f32[32,384,256]{2,1,0:T(8,128)} %fusion.76, bf16[64,32,384]{2,0,1:T(8,128)(2,1)} %bitcast.301, bf16[1,32,64,256]{3,2,1,0:T(8,128)(2,1)} %param.12), kind=kOutput, calls=%fused_computation.19 | convolution fusion | flops 465567744 | bytes 21495808 | tf_op jit(solution)/shard_map/nir,inf->ifr/dot_general | solution.py:51
  315.7 2.1 fusion.63
  318.4 17.8 %collective-permute-done.2 = bf16[2048,384]{1,0:T(8,128)(2,1)} collective-permute-done((bf16[2048,384]{1,0:T(8,128)(2,1)}, bf16[2048,384]{1,0:T(8,128)(2,1)}, u32[]{:S(2)}, u32[]{:S(2)}) %collective-permute-start.2) | collective-permute-done | bytes 1572896 | tf_op jit(solution)/shard_map/ppermute | solution.py:9
  336.2 2.1 copy.110
  338.3 4.3 %all-to-all-start.9 = ((bf16[64,32,384]{2,1,0:T(8,128)(2,1)}), bf16[64,32,384]{2,1,0:T(8,128)(2,1)}, u32[]{:S(2)}, u32[]{:S(2)}) async-start(bf16[64,32,384]{2,1,0:T(8,128)(2,1)} %copy.110), calls=%async_computation.9 | async-start | bytes 3145728 | tf_op jit(solution)/shard_map/all_to_all | solution.py:21
  342.7 5.5 %fusion.112 = f32[32,64,256]{2,1,0:T(8,128)} fusion(bf16[64,32,384]{2,0,1:T(8,128)(2,1)S(1)} %bitcast.291, bf16[32,256,384]{1,2,0:T(8,128)(2,1)} %copy-done.1), kind=kOutput, calls=%fused_computation.130 | convolution fusion | flops 402653184 | bytes 9961472 | tf_op jit(solution)/shard_map/nir,ifr->inf/dot_general | solution.py:56
  354.3 1.8 fusion.69
  356.0 6.7 %all-to-all-done.9 = bf16[64,32,384]{2,1,0:T(8,128)(2,1)} async-done(((bf16[64,32,384]{2,1,0:T(8,128)(2,1)}), bf16[64,32,384]{2,1,0:T(8,128)(2,1)}, u32[]{:S(2)}, u32[]{:S(2)}) %all-to-all-start.9) | async-done | bytes 1572896 | tf_op jit(solution)/shard_map/all_to_all | solution.py:21
  366.6 1.9 collective-permute-start.3
  368.5 9.9 %add_bitcast_fusion = f32[1,32,64,256]{3,2,1,0:T(8,128)} fusion(f32[32,64,256]{2,1,0:T(8,128)S(1)} %copy-done.32, bf16[64,32,384]{2,0,1:T(8,128)(2,1)S(1)} %bitcast.302, f32[32,384,256]{2,1,0:T(8,128)} %fusion.76), kind=kOutput, calls=%fused_computation.62 | convolution fusion | flops 431489024 | bytes 18350080 | tf_op jit(solution)/shard_map/ifr,nir->inf/dot_general | solution.py:48
  378.4 2.6 add_bitcast_fusion.1
  381.0 3.4 bitcast_convert_fusion.1
  386.5 16.5 %collective-permute-done.3 = bf16[2048,384]{1,0:T(8,128)(2,1)} collective-permute-done((bf16[2048,384]{1,0:T(8,128)(2,1)}, bf16[2048,384]{1,0:T(8,128)(2,1)}, u32[]{:S(2)}, u32[]{:S(2)}) %collective-permute-start.3) | collective-permute-done | bytes 1572896 | tf_op jit(solution)/shard_map/ppermute | solution.py:9
  403.0 3.3 bitcast_convert_fusion
  (110 shorter events, 40.3 us)
Async XLA Ops:
  0.6 62.6 %copy-start = (bf16[1,32,64,256]{3,2,1,0:T(8,128)(2,1)S(1)}, bf16[1,32,64,256]{3,2,1,0:T(8,128)(2,1)}, u32[]{:S(2)}) copy-start(bf16[1,32,64,256]{3,2,1,0:T(8,128)(2,1)} %param.11) | copy-start | bytes 3145732
  0.6 2.2 copy-start.3
  5.5 24.3 %all-to-all-start.5 = ((bf16[16,128,384]{2,0,1:T(8,128)(2,1)}), bf16[16,128,384]{2,0,1:T(8,128)(2,1)S(1)}, u32[]{:S(2)}, u32[]{:S(2)}) async-start(bf16[16,128,384]{2,0,1:T(8,128)(2,1)} %copy.96), calls=%async_computation.5 | async-start | bytes 3145728 | tf_op jit(solution)/shard_map/all_to_all | solution.py:17
  9.7 3.3 copy-start.19
  11.9 1.1 copy-start.7
  29.8 1.1 copy-start.30
  31.0 24.5 %all-to-all-start = ((bf16[16,128,384]{2,0,1:T(8,128)(2,1)}), bf16[16,128,384]{2,0,1:T(8,128)(2,1)}, u32[]{:S(2)}, u32[]{:S(2)}) async-start(bf16[16,128,384]{2,0,1:T(8,128)(2,1)} %copy.78), calls=%async_computation | async-start | bytes 3145728 | tf_op jit(solution)/shard_map/all_to_all | solution.py:17
  37.5 1.2 copy-start.9
  37.6 104.4 %copy-start.5 = (bf16[2048,384]{1,0:T(8,128)(2,1)}, bf16[2048,384]{1,0:T(8,128)(2,1)S(1)}, u32[]{:S(2)}) copy-start(bf16[2048,384]{1,0:T(8,128)(2,1)S(1)} %get-tuple-element.12) | copy-start | bytes 4718596
  55.5 25.0 %all-to-all-start.1 = ((bf16[16,128,384]{2,0,1:T(8,128)(2,1)}), bf16[16,128,384]{2,0,1:T(8,128)(2,1)}, u32[]{:S(2)}, u32[]{:S(2)}) async-start(bf16[16,128,384]{2,0,1:T(8,128)(2,1)} %copy.81), calls=%async_computation.1 | async-start | bytes 3145728 | tf_op jit(solution)/shard_map/all_to_all | solution.py:17
  80.5 31.4 %all-to-all-start.6 = ((bf16[64,32,384]{2,1,0:T(8,128)(2,1)}), bf16[64,32,384]{2,1,0:T(8,128)(2,1)}, u32[]{:S(2)}, u32[]{:S(2)}) async-start(bf16[64,32,384]{2,1,0:T(8,128)(2,1)} %copy.99), calls=%async_computation.6 | async-start | bytes 3145728 | tf_op jit(solution)/shard_map/all_to_all | solution.py:21
  86.7 8.8 %copy-start.24 = (bf16[16,4,32,384]{3,0,1,2:T(8,128)(2,1)}, bf16[16,4,32,384]{3,0,1,2:T(8,128)(2,1)S(1)}, u32[]{:S(2)}) copy-start(bf16[16,4,32,384]{3,0,1,2:T(8,128)(2,1)S(1)} %copy.82) | copy-start | bytes 4718596
  86.7 8.7 %copy-start.26 = (bf16[16,4,32,384]{3,0,1,2:T(8,128)(2,1)S(1)}, bf16[16,4,32,384]{3,0,1,2:T(8,128)(2,1)}, u32[]{:S(2)}) copy-start(bf16[16,4,32,384]{3,0,1,2:T(8,128)(2,1)} %copy.79) | copy-start | bytes 4718596
  86.7 8.7 %copy-start.34 = (bf16[1,32,64,256]{3,2,1,0:T(8,128)(2,1)S(1)}, bf16[1,32,64,256]{3,2,1,0:T(8,128)(2,1)}, u32[]{:S(2)}) copy-start(bf16[1,32,64,256]{3,2,1,0:T(8,128)(2,1)} %param.12) | copy-start | bytes 3145732
  107.1 2.7 copy-start.1
  111.9 24.5 %all-to-all-start.2 = ((bf16[64,32,384]{2,1,0:T(8,128)(2,1)}), bf16[64,32,384]{2,1,0:T(8,128)(2,1)}, u32[]{:S(2)}, u32[]{:S(2)}) async-start(bf16[64,32,384]{2,1,0:T(8,128)(2,1)} %copy.84), calls=%async_computation.2 | async-start | bytes 3145728 | tf_op jit(solution)/shard_map/all_to_all | solution.py:21
  116.2 1.8 copy-start.20
  118.0 1.9 copy-start.17
  121.3 70.6 %collective-permute-start.1 = (bf16[2048,384]{1,0:T(8,128)(2,1)}, bf16[2048,384]{1,0:T(8,128)(2,1)}, u32[]{:S(2)}, u32[]{:S(2)}) collective-permute-start(bf16[2048,384]{1,0:T(8,128)(2,1)} %fusion.48), channel_id=1, source_target_pairs={{0,4},{4,8},{8,12},{12,16},{16,20},{20,24},{24,28},{28,0},{1,5},{5... | collective-permute-start | bytes 4718600 | tf_op jit(solution)/shard_map/ppermute | solution.py:9
  138.0 1.2 copy-start.13
  138.0 2.5 copy-start.18
  146.6 51.4 %all-to-all-start.4 = ((bf16[16,128,384]{2,0,1:T(8,128)(2,1)}), bf16[16,128,384]{2,0,1:T(8,128)(2,1)}, u32[]{:S(2)}, u32[]{:S(2)}) async-start(bf16[16,128,384]{2,0,1:T(8,128)(2,1)} %copy.91), calls=%async_computation.4 | async-start | bytes 3145728 | tf_op jit(solution)/shard_map/all_to_all | solution.py:17
  151.0 51.5 %collective-permute-start = (bf16[2048,384]{1,0:T(8,128)(2,1)}, bf16[2048,384]{1,0:T(8,128)(2,1)S(1)}, u32[]{:S(2)}, u32[]{:S(2)}) collective-permute-start(bf16[2048,384]{1,0:T(8,128)(2,1)} %fusion.49), channel_id=1, source_target_pairs={{0,28},{4,0},{8,4},{12,8},{16,12},{20,16},{24,20},{28,24},{1,29},{... | collective-permute-start | bytes 4718600 | tf_op jit(solution)/shard_map/ppermute | solution.py:9
  195.1 7.3 %copy-start.21 = (bf16[1,16,128,128]{3,2,1,0:T(8,128)(2,1)S(1)}, bf16[1,16,128,128]{3,2,1,0:T(8,128)(2,1)}, u32[]{:S(2)}) copy-start(bf16[1,16,128,128]{3,2,1,0:T(8,128)(2,1)} %param.13) | copy-start | bytes 1572868
  198.1 24.5 %all-to-all-start.7 = ((bf16[16,128,384]{2,0,1:T(8,128)(2,1)}), bf16[16,128,384]{2,0,1:T(8,128)(2,1)}, u32[]{:S(2)}, u32[]{:S(2)}) async-start(bf16[16,128,384]{2,0,1:T(8,128)(2,1)} %copy.103), calls=%async_computation.7 | async-start | bytes 3145728 | tf_op jit(solution)/shard_map/all_to_all | solution.py:17
  202.4 4.7 %copy-start.11 = (bf16[2048,384]{1,0:T(8,128)(2,1)}, bf16[2048,384]{1,0:T(8,128)(2,1)S(1)}, u32[]{:S(2)}) copy-start(bf16[2048,384]{1,0:T(8,128)(2,1)S(1)} %collective-permute-done) | copy-start | bytes 4718596
  222.6 24.5 %all-to-all-start.3 = ((bf16[16,128,384]{2,0,1:T(8,128)(2,1)}), bf16[16,128,384]{2,0,1:T(8,128)(2,1)}, u32[]{:S(2)}, u32[]{:S(2)}) async-start(bf16[16,128,384]{2,0,1:T(8,128)(2,1)} %copy.87), calls=%async_computation.3 | async-start | bytes 3145728 | tf_op jit(solution)/shard_map/all_to_all | solution.py:17
  247.1 11.8 %slice-start = ((s8[6291456]{0:T(1024)(128)(4,1)}), s8[2097152]{0:T(1024)(128)(4,1)S(1)}, s32[]{:S(2)}) async-start(s8[6291456]{0:T(1024)(128)(4,1)} %bitcast.272), calls=%async_computation.12 | async-start | bytes 4194304
  247.1 24.6 %all-to-all-start.8 = ((bf16[64,32,384]{2,1,0:T(8,128)(2,1)}), bf16[64,32,384]{2,1,0:T(8,128)(2,1)}, u32[]{:S(2)}, u32[]{:S(2)}) async-start(bf16[64,32,384]{2,1,0:T(8,128)(2,1)} %copy.107), calls=%async_computation.8 | async-start | bytes 3145728 | tf_op jit(solution)/shard_map/all_to_all | solution.py:21
  251.6 7.3 %slice-start.1 = ((s8[6291456]{0:T(1024)(128)(4,1)}), s8[4194304]{0:T(1024)(128)(4,1)S(1)}, s32[]{:S(2)}) async-start(s8[6291456]{0:T(1024)(128)(4,1)} %bitcast.272), calls=%async_computation.13 | async-start | bytes 8388608
  256.9 2.1 copy-start.27
  263.3 1.2 copy-start.15
  271.7 26.1 %all-to-all-start.10 = ((bf16[64,32,384]{2,1,0:T(8,128)(2,1)}), bf16[64,32,384]{2,1,0:T(8,128)(2,1)S(1)}, u32[]{:S(2)}, u32[]{:S(2)}) async-start(bf16[64,32,384]{2,1,0:T(8,128)(2,1)} %copy.118), calls=%async_computation.10 | async-start | bytes 3145728 | tf_op jit(solution)/shard_map/all_to_all | solution.py:21
  286.9 4.6 %copy-start.22 = (bf16[1,16,128,128]{3,2,1,0:T(8,128)(2,1)S(1)}, bf16[1,16,128,128]{3,2,1,0:T(8,128)(2,1)}, u32[]{:S(2)}) copy-start(bf16[1,16,128,128]{3,2,1,0:T(8,128)(2,1)} %param.13) | copy-start | bytes 1572868
  295.3 40.9 %collective-permute-start.2 = (bf16[2048,384]{1,0:T(8,128)(2,1)}, bf16[2048,384]{1,0:T(8,128)(2,1)}, u32[]{:S(2)}, u32[]{:S(2)}) collective-permute-start(bf16[2048,384]{1,0:T(8,128)(2,1)} %fusion.47), channel_id=1, source_target_pairs={{0,4},{4,8},{8,12},{12,16},{16,20},{20,24},{24,28},{28,0},{1,5},{5... | collective-permute-start | bytes 4718600 | tf_op jit(solution)/shard_map/ppermute | solution.py:9
  297.8 17.8 %copy-start.28 = (bf16[64,32,384]{2,1,0:T(8,128)(2,1)}, bf16[64,32,384]{2,1,0:T(8,128)(2,1)S(1)}, u32[]{:S(2)}) copy-start(bf16[64,32,384]{2,1,0:T(8,128)(2,1)S(1)} %all-to-all-done.10) | copy-start | bytes 4718596
  297.8 40.4 %all-to-all-start.11 = ((bf16[64,32,384]{2,1,0:T(8,128)(2,1)}), bf16[64,32,384]{2,1,0:T(8,128)(2,1)}, u32[]{:S(2)}, u32[]{:S(2)}) async-start(bf16[64,32,384]{2,1,0:T(8,128)(2,1)} %copy.121), calls=%async_computation.11 | async-start | bytes 3145728 | tf_op jit(solution)/shard_map/all_to_all | solution.py:21
  315.7 2.7 copy-start.2
  318.4 24.2 %copy-start.25 = (bf16[16,4,32,384]{3,0,1,2:T(8,128)(2,1)S(1)}, bf16[16,4,32,384]{3,0,1,2:T(8,128)(2,1)}, u32[]{:S(2)}) copy-start(bf16[16,4,32,384]{3,0,1,2:T(8,128)(2,1)} %copy-done.24) | copy-start | bytes 4718596
  338.3 24.5 %all-to-all-start.9 = ((bf16[64,32,384]{2,1,0:T(8,128)(2,1)}), bf16[64,32,384]{2,1,0:T(8,128)(2,1)}, u32[]{:S(2)}, u32[]{:S(2)}) async-start(bf16[64,32,384]{2,1,0:T(8,128)(2,1)} %copy.110), calls=%async_computation.9 | async-start | bytes 3145728 | tf_op jit(solution)/shard_map/all_to_all | solution.py:21
  342.6 5.5 %copy-start.29 = (bf16[64,32,384]{2,1,0:T(8,128)(2,1)S(1)}, bf16[64,32,384]{2,1,0:T(8,128)(2,1)}, u32[]{:S(2)}) copy-start(bf16[64,32,384]{2,1,0:T(8,128)(2,1)} %copy-done.28) | copy-start | bytes 4718596
  348.1 1.4 copy-start.10
  348.1 1.9 copy-start.14
  348.1 3.6 copy-start.8
  351.8 2.5 copy-start.12
  354.2 10.2 %copy-start.4 = (bf16[1,16,128,128]{3,2,1,0:T(8,128)(2,1)S(1)}, bf16[1,16,128,128]{3,2,1,0:T(8,128)(2,1)}, u32[]{:S(2)}) copy-start(bf16[1,16,128,128]{3,2,1,0:T(8,128)(2,1)} %param.10) | copy-start | bytes 1572868
  364.4 4.1 %copy-start.33 = (bf16[4,16,32,384]{3,1,0,2:T(8,128)(2,1)S(1)}, bf16[4,16,32,384]{3,1,0,2:T(8,128)(2,1)}, u32[]{:S(2)}) copy-start(bf16[4,16,32,384]{3,1,0,2:T(8,128)(2,1)} %copy.89) | copy-start | bytes 4718596
  365.0 3.5 copy-start.32
  365.0 13.3 %slice-start.2 = ((s8[6291456]{0:T(1024)(128)(4,1)}), s8[4194304]{0:T(1024)(128)(4,1)S(1)}, s32[]{:S(2)}) async-start(s8[6291456]{0:T(1024)(128)(4,1)} %bitcast.274), calls=%async_computation.14 | async-start | bytes 8388608
  366.6 11.8 %slice-start.3 = ((s8[6291456]{0:T(1024)(128)(4,1)}), s8[2097152]{0:T(1024)(128)(4,1)S(1)}, s32[]{:S(2)}) async-start(s8[6291456]{0:T(1024)(128)(4,1)} %bitcast.274), calls=%async_computation.15 | async-start | bytes 4194304
  366.6 11.8 %copy-start.16 = (bf16[4,16,32,384]{3,1,0,2:T(8,128)(2,1)S(1)}, bf16[4,16,32,384]{3,1,0,2:T(8,128)(2,1)}, u32[]{:S(2)}) copy-start(bf16[4,16,32,384]{3,1,0,2:T(8,128)(2,1)} %copy-done.15) | copy-start | bytes 4718596
  366.6 11.8 %copy-start.23 = (f32[32,64,256]{2,1,0:T(8,128)S(1)}, f32[32,64,256]{2,1,0:T(8,128)}, u32[]{:S(2)}) copy-start(f32[32,64,256]{2,1,0:T(8,128)} %fusion.112) | copy-start | bytes 6291460
  366.6 36.5 %collective-permute-start.3 = (bf16[2048,384]{1,0:T(8,128)(2,1)}, bf16[2048,384]{1,0:T(8,128)(2,1)}, u32[]{:S(2)}, u32[]{:S(2)}) collective-permute-start(bf16[2048,384]{1,0:T(8,128)(2,1)} %fusion.46), channel_id=1, source_target_pairs={{0,28},{4,0},{8,4},{12,8},{16,12},{20,16},{24,20},{28,24},{1,29},{... | collective-permute-start | bytes 4718600 | tf_op jit(solution)/shard_map/ppermute | solution.py:9
  381.0 3.4 copy-start.6
  381.0 3.4 copy-start.31

commit v2 on v0

--- a/solution.py
+++ b/solution.py
@@ -98,8 +98,8 @@
         stored, cotangent, up_first, up_second, down_first, down_second, behind
     )
     sent_back = (cotangent + grad_step).astype(jnp.bfloat16)
+    near_activation, sent_back = lax.optimization_barrier((near_activation, sent_back))
     near_cotangent = shifted(sent_back, "pipe", -1)
-    near_activation, sent_back = lax.optimization_barrier((near_activation, sent_back))
 
     folded_ahead = front(near_activation.reshape(blocks, width, rows), up_first, up_second, down_first)[3]
     output = near_activation.astype(jnp.float32) + jnp.einsum(

time: 408 us -> 399 us (0.978)
  starting transfers between devices: 64.9 us -> 56.9 us
    ppermute x4, waiting for transfers between devices: 72.2 us -> 53.9 us  [shifted(): lax.ppermute(value, axis, [(i, (i + by) % count) for i in range(count)])]
    all_to_all x6, waiting for transfers between devices: 45.6 us -> 59.6 us  [to_columns(): lax.all_to_all(value, 'tensor', split_axis=1, concat_axis=0, tiled=True)]
    ppermute x4, starting transfers between devices: 12.1 us -> 4.33 us  [shifted(): lax.ppermute(value, axis, [(i, (i + by) % count) for i in range(count)])]
  transfers between devices with their start and end apart: 16 -> 16, of which waited for: 12 -> 14; matrix products, arithmetic and copies ran while one was open for 43% -> 42% of each run, Pallas kernels for 0% -> 0%
where the time goes in v2:
time: 399 us; the launch traced here: 393 us
  waiting for transfers between devices  141 us (35%)
  matrix products  109 us (27%)
  local copies, waits for them, and re-layouts  65.3 us (16%)
  starting transfers between devices  56.9 us (14%)
  other arithmetic  18.8 us (5%)
    all_to_all x6, waiting for transfers between devices, to_columns(): lax.all_to_all(value, 'tensor', split_axis=1, concat_axis=0, tiled=True)  59.6 us
    ppermute x4, waiting for transfers between devices, shifted(): lax.ppermute(value, axis, [(i, (i + by) % count) for i in range(count)])  53.9 us
    dot_general x4, matrix products, front(): jnp.einsum('ifr,inf->nir', hidden, first_down, preferred_element_type=jnp...  29.6 us
    all_to_all x6, waiting for transfers between devices, to_rows(): lax.all_to_all(value, 'tensor', split_axis=0, concat_axis=1, tiled=True)  27.5 us
    all_to_all x6, starting transfers between devices, to_columns(): lax.all_to_all(value, 'tensor', split_axis=1, concat_axis=0, tiled=True)  26.9 us
    all_to_all x6, starting transfers between devices, to_rows(): lax.all_to_all(value, 'tensor', split_axis=0, concat_axis=1, tiled=True)  25.7 us
    dot_general x2, matrix products, backward(): jnp.einsum('nir,inf->ifr', grad_folded, first_down, preferred_element_typ...  24.9 us
    dot_general x2, matrix products, front(): jnp.einsum('nir,inf->ifr', spread, second_up, preferred_element_type=jnp....  15.1 us
  transfers between devices with their start and end apart: 16, of which 14 were waited for; matrix products, arithmetic and copies ran while one was open for 42% of the time, Pallas kernels for 0%

profile of v2, /device:TPU:0, one launch (start us, length us, event | category | flops | bytes accessed | tf_op | source)
XLA Modules:
  0.0 392.9 jit_solution(3026370957238205804)
XLA Ops:
  0.7 2.2 convert_element_type.112
  3.5 2.1 copy.76
  5.5 4.2 %all-to-all-start = ((bf16[16,128,384]{2,0,1:T(8,128)(2,1)}), bf16[16,128,384]{2,0,1:T(8,128)(2,1)S(1)}, u32[]{:S(2)}, u32[]{:S(2)}) async-start(bf16[16,128,384]{2,0,1:T(8,128)(2,1)} %copy.76), calls=%async_computation | async-start | bytes 3145728 | tf_op jit(solution)/shard_map/all_to_all | solution.py:17
  9.8 2.1 convert_element_type.119
  13.6 2.1 copy.82
  15.7 14.1 %all-to-all-done = bf16[16,128,384]{2,0,1:T(8,128)(2,1)S(1)} async-done(((bf16[16,128,384]{2,0,1:T(8,128)(2,1)}), bf16[16,128,384]{2,0,1:T(8,128)(2,1)S(1)}, u32[]{:S(2)}, u32[]{:S(2)}) %all-to-all-start) | async-done | bytes 1572896 | tf_op jit(solution)/shard_map/all_to_all | solution.py:17
  31.0 4.4 %all-to-all-start.2 = ((bf16[16,128,384]{2,0,1:T(8,128)(2,1)}), bf16[16,128,384]{2,0,1:T(8,128)(2,1)}, u32[]{:S(2)}, u32[]{:S(2)}) async-start(bf16[16,128,384]{2,0,1:T(8,128)(2,1)} %copy.82), calls=%async_computation.2 | async-start | bytes 3145728 | tf_op jit(solution)/shard_map/all_to_all | solution.py:17
  35.4 2.2 fusion.110
  39.4 2.1 copy.85
  41.4 14.1 %all-to-all-done.2 = bf16[16,128,384]{2,0,1:T(8,128)(2,1)} async-done(((bf16[16,128,384]{2,0,1:T(8,128)(2,1)}), bf16[16,128,384]{2,0,1:T(8,128)(2,1)}, u32[]{:S(2)}, u32[]{:S(2)}) %all-to-all-start.2) | async-done | bytes 1572896 | tf_op jit(solution)/shard_map/all_to_all | solution.py:17
  55.5 4.5 %all-to-all-start.3 = ((bf16[16,128,384]{2,0,1:T(8,128)(2,1)}), bf16[16,128,384]{2,0,1:T(8,128)(2,1)}, u32[]{:S(2)}, u32[]{:S(2)}) async-start(bf16[16,128,384]{2,0,1:T(8,128)(2,1)} %copy.85), calls=%async_computation.3 | async-start | bytes 3145728 | tf_op jit(solution)/shard_map/all_to_all | solution.py:17
  60.0 2.8 copy.77
  62.9 7.6 %fusion.59 = bf16[64,32,384]{2,0,1:T(8,128)(2,1)} fusion(bf16[64,32,384]{2,0,1:T(8,128)(2,1)} %bitcast.299, bf16[1,32,64,256]{3,2,1,0:T(8,128)(2,1)} %param.12, bf16[1,32,64,256]{3,2,1,0:T(8,128)(2,1)S(1)} %copy-done), kind=kOutput, calls=%fused_computation.79 | convolution fusion | flops 834404352 | bytes 5242880 | tf_op jit(solution)/shard_map/ifr,inf->nir/dot_general | solution.py:31
  70.5 3.5 copy.79
  74.0 2.8 copy.83
  76.8 3.3 all-to-all-done.3
  80.2 4.6 %all-to-all-start.1 = ((bf16[64,32,384]{2,1,0:T(8,128)(2,1)}), bf16[64,32,384]{2,1,0:T(8,128)(2,1)}, u32[]{:S(2)}, u32[]{:S(2)}) async-start(bf16[64,32,384]{2,1,0:T(8,128)(2,1)} %copy.79), calls=%async_computation.1 | async-start | bytes 3145728 | tf_op jit(solution)/shard_map/all_to_all | solution.py:21
  86.4 8.7 %fusion.34 = (bf16[32,256,384]{1,2,0:T(8,128)(2,1)}, f32[32,384,256]{2,1,0:T(8,128)}) fusion(bf16[64,32,384]{2,0,1:T(8,128)(2,1)S(1)} %bitcast.286, bf16[1,32,64,256]{3,2,1,0:T(8,128)(2,1)S(1)} %copy-done), kind=kOutput, calls=%fused_computation.45 | convolution fusion | flops 430964736 | bytes 21495808 | tf_op jit(solution)/shard_map/nir,inf->ifr/dot_general | solution.py:29
  95.1 11.6 %fusion.6 = bf16[32,256,384]{1,2,0:T(8,128)(2,1)S(1)} fusion(f32[32,384,256]{2,1,0:T(8,128)} %get-tuple-element.35, bf16[64,32,384]{2,0,1:T(8,128)(2,1)S(1)} %bitcast.288, bf16[1,32,64,256]{3,2,1,0:T(8,128)(2,1)S(1)} %copy-done.34), kind=kOutput, calls=%fused_computation.12 | convolution fusion | flops 465567744 | bytes 21495808 | tf_op jit(solution)/shard_map/nir,inf->ifr/dot_general | solution.py:51
  106.8 2.1 fusion.62
  109.4 2.1 copy.88
  111.4 4.4 %all-to-all-start.4 = ((bf16[64,32,384]{2,1,0:T(8,128)(2,1)}), bf16[64,32,384]{2,1,0:T(8,128)(2,1)}, u32[]{:S(2)}, u32[]{:S(2)}) async-start(bf16[64,32,384]{2,1,0:T(8,128)(2,1)} %copy.88), calls=%async_computation.4 | async-start | bytes 3145728 | tf_op jit(solution)/shard_map/all_to_all | solution.py:21
  120.9 2.3 collective-permute-start
  123.2 12.7 %all-to-all-done.4 = bf16[64,32,384]{2,1,0:T(8,128)(2,1)} async-done(((bf16[64,32,384]{2,1,0:T(8,128)(2,1)}), bf16[64,32,384]{2,1,0:T(8,128)(2,1)}, u32[]{:S(2)}, u32[]{:S(2)}) %all-to-all-start.4) | async-done | bytes 1572896 | tf_op jit(solution)/shard_map/all_to_all | solution.py:21
  141.6 20.0 %collective-permute-done = bf16[2048,384]{1,0:T(8,128)(2,1)} collective-permute-done((bf16[2048,384]{1,0:T(8,128)(2,1)}, bf16[2048,384]{1,0:T(8,128)(2,1)}, u32[]{:S(2)}, u32[]{:S(2)}) %collective-permute-start) | collective-permute-done | bytes 1572896 | tf_op jit(solution)/shard_map/ppermute | solution.py:9
  161.6 3.2 fusion.67
  164.8 2.9 copy.99
  167.7 4.8 %all-to-all-start.7 = ((bf16[16,128,384]{2,0,1:T(8,128)(2,1)}), bf16[16,128,384]{2,0,1:T(8,128)(2,1)}, u32[]{:S(2)}, u32[]{:S(2)}) async-start(bf16[16,128,384]{2,0,1:T(8,128)(2,1)} %copy.99), calls=%async_computation.7 | async-start | bytes 3145728 | tf_op jit(solution)/shard_map/all_to_all | solution.py:17
  173.1 2.1 copy.95
  175.1 17.4 %all-to-all-done.7 = bf16[16,128,384]{2,0,1:T(8,128)(2,1)} async-done(((bf16[16,128,384]{2,0,1:T(8,128)(2,1)}), bf16[16,128,384]{2,0,1:T(8,128)(2,1)}, u32[]{:S(2)}, u32[]{:S(2)}) %all-to-all-start.7) | async-done | bytes 1572896 | tf_op jit(solution)/shard_map/all_to_all | solution.py:17
  192.6 4.3 %all-to-all-start.6 = ((bf16[16,128,384]{2,0,1:T(8,128)(2,1)}), bf16[16,128,384]{2,0,1:T(8,128)(2,1)}, u32[]{:S(2)}, u32[]{:S(2)}) async-start(bf16[16,128,384]{2,0,1:T(8,128)(2,1)} %copy.95), calls=%async_computation.6 | async-start | bytes 3145728 | tf_op jit(solution)/shard_map/all_to_all | solution.py:17
  198.7 2.8 copy.101
  201.6 7.6 %fusion.56 = bf16[64,32,384]{2,0,1:T(8,128)(2,1)} fusion(bf16[64,32,384]{2,0,1:T(8,128)(2,1)} %bitcast.300, bf16[1,32,64,256]{3,2,1,0:T(8,128)(2,1)} %param.12, bf16[1,32,64,256]{3,2,1,0:T(8,128)(2,1)S(1)} %copy-done), kind=kOutput, calls=%fused_computation.78 | convolution fusion | flops 834404352 | bytes 5242880 | tf_op jit(solution)/shard_map/ifr,inf->nir/dot_general | solution.py:31
  209.2 3.5 copy.103
  212.7 4.4 %all-to-all-done.6 = bf16[16,128,384]{2,0,1:T(8,128)(2,1)} async-done(((bf16[16,128,384]{2,0,1:T(8,128)(2,1)}), bf16[16,128,384]{2,0,1:T(8,128)(2,1)}, u32[]{:S(2)}, u32[]{:S(2)}) %all-to-all-start.6) | async-done | bytes 1572896 | tf_op jit(solution)/shard_map/all_to_all | solution.py:17
  217.1 4.3 %all-to-all-start.8 = ((bf16[64,32,384]{2,1,0:T(8,128)(2,1)}), bf16[64,32,384]{2,1,0:T(8,128)(2,1)}, u32[]{:S(2)}, u32[]{:S(2)}) async-start(bf16[64,32,384]{2,1,0:T(8,128)(2,1)} %copy.103), calls=%async_computation.8 | async-start | bytes 3145728 | tf_op jit(solution)/shard_map/all_to_all | solution.py:21
  223.1 6.4 %fusion.79 = f32[32,384,256]{2,1,0:T(8,128)} fusion(bf16[64,32,384]{2,0,1:T(8,128)(2,1)S(1)} %bitcast.282, bf16[1,32,64,256]{3,2,1,0:T(8,128)(2,1)S(1)} %copy-done), kind=kOutput, calls=%fused_computation.98 | convolution fusion | flops 402653184 | bytes 15204352 | tf_op jit(solution)/shard_map/nir,inf->ifr/dot_general | solution.py:29
  229.5 4.4 %collective-permute-done.1 = bf16[2048,384]{1,0:T(8,128)(2,1)S(1)} collective-permute-done((bf16[2048,384]{1,0:T(8,128)(2,1)}, bf16[2048,384]{1,0:T(8,128)(2,1)S(1)}, u32[]{:S(2)}, u32[]{:S(2)}) %collective-permute-start.1) | collective-permute-done | bytes 1572896 | tf_op jit(solution)/shard_map/ppermute | solution.py:9
  235.7 2.9 copy.91
  238.6 2.9 all-to-all-done.8
  241.5 4.7 %all-to-all-start.5 = ((bf16[16,128,384]{2,0,1:T(8,128)(2,1)}), bf16[16,128,384]{2,0,1:T(8,128)(2,1)}, u32[]{:S(2)}, u32[]{:S(2)}) async-start(bf16[16,128,384]{2,0,1:T(8,128)(2,1)} %copy.91), calls=%async_computation.5 | async-start | bytes 3145728 | tf_op jit(solution)/shard_map/all_to_all | solution.py:17
  246.2 9.2 %fusion.65 = bf16[64,32,384]{2,0,1:T(8,128)(2,1)S(1)} fusion(bf16[1,32,64,256]{3,2,1,0:T(8,128)(2,1)} %param.12, f32[32,384,256]{2,1,0:T(8,128)} %fusion.79), kind=kOutput, calls=%fused_computation.83 | convolution fusion | flops 431751168 | bytes 15204352 | tf_op jit(solution)/shard_map/ifr,inf->nir/dot_general | solution.py:31
  255.5 2.0 copy.116
  257.5 2.6 fusion.113
  260.1 6.2 %all-to-all-done.5 = bf16[16,128,384]{2,0,1:T(8,128)(2,1)} async-done(((bf16[16,128,384]{2,0,1:T(8,128)(2,1)}), bf16[16,128,384]{2,0,1:T(8,128)(2,1)}, u32[]{:S(2)}, u32[]{:S(2)}) %all-to-all-start.5) | async-done | bytes 1572896 | tf_op jit(solution)/shard_map/all_to_all | solution.py:17
  266.3 3.6 all-to-all-start.11
  269.9 5.1 %fusion.64 = bf16[64,32,384]{2,0,1:T(8,128)(2,1)S(1)} fusion(bf16[32,256,384]{1,2,0:T(8,128)(2,1)} %get-tuple-element.34, bf16[1,32,64,256]{3,2,1,0:T(8,128)(2,1)} %param.12), kind=kOutput, calls=%fused_computation.82 | convolution fusion | flops 403439616 | bytes 8912896 | tf_op jit(solution)/shard_map/ifr,inf->nir/dot_general | solution.py:31
  275.0 2.1 copy.113
  279.4 3.3 fusion.47
  282.7 2.8 copy.93
  285.5 4.5 %all-to-all-done.11 = bf16[64,32,384]{2,1,0:T(8,128)(2,1)S(1)} async-done(((bf16[64,32,384]{2,1,0:T(8,128)(2,1)}), bf16[64,32,384]{2,1,0:T(8,128)(2,1)S(1)}, u32[]{:S(2)}, u32[]{:S(2)}) %all-to-all-start.11) | async-done | bytes 1572896 | tf_op jit(solution)/shard_map/all_to_all | solution.py:21
  290.0 4.6 %all-to-all-start.10 = ((bf16[64,32,384]{2,1,0:T(8,128)(2,1)}), bf16[64,32,384]{2,1,0:T(8,128)(2,1)}, u32[]{:S(2)}, u32[]{:S(2)}) async-start(bf16[64,32,384]{2,1,0:T(8,128)(2,1)} %copy.113), calls=%async_computation.10 | async-start | bytes 3145728 | tf_op jit(solution)/shard_map/all_to_all | solution.py:21
  294.5 13.3 %fusion.13 = bf16[32,256,384]{1,2,0:T(8,128)(2,1)S(1)} fusion(f32[32,384,256]{2,1,0:T(8,128)} %fusion.79, bf16[64,32,384]{2,0,1:T(8,128)(2,1)} %bitcast.297, bf16[1,32,64,256]{3,2,1,0:T(8,128)(2,1)} %param.12), kind=kOutput, calls=%fused_computation.19 | convolution fusion | flops 465567744 | bytes 21495808 | tf_op jit(solution)/shard_map/nir,inf->ifr/dot_general | solution.py:51
  307.9 2.1 fusion.63
  310.6 11.9 %collective-permute-done.2 = bf16[2048,384]{1,0:T(8,128)(2,1)} collective-permute-done((bf16[2048,384]{1,0:T(8,128)(2,1)}, bf16[2048,384]{1,0:T(8,128)(2,1)}, u32[]{:S(2)}, u32[]{:S(2)}) %collective-permute-start.2) | collective-permute-done | bytes 1572896 | tf_op jit(solution)/shard_map/ppermute | solution.py:9
  322.4 2.1 copy.106
  324.5 4.3 %all-to-all-start.9 = ((bf16[64,32,384]{2,1,0:T(8,128)(2,1)}), bf16[64,32,384]{2,1,0:T(8,128)(2,1)}, u32[]{:S(2)}, u32[]{:S(2)}) async-start(bf16[64,32,384]{2,1,0:T(8,128)(2,1)} %copy.106), calls=%async_computation.9 | async-start | bytes 3145728 | tf_op jit(solution)/shard_map/all_to_all | solution.py:21
  328.9 5.5 %fusion.112 = f32[32,64,256]{2,1,0:T(8,128)} fusion(bf16[64,32,384]{2,0,1:T(8,128)(2,1)S(1)} %bitcast.287, bf16[32,256,384]{1,2,0:T(8,128)(2,1)} %copy-done.1), kind=kOutput, calls=%fused_computation.128 | convolution fusion | flops 402653184 | bytes 9961472 | tf_op jit(solution)/shard_map/nir,ifr->inf/dot_general | solution.py:56
  341.6 7.3 %all-to-all-done.9 = bf16[64,32,384]{2,1,0:T(8,128)(2,1)} async-done(((bf16[64,32,384]{2,1,0:T(8,128)(2,1)}), bf16[64,32,384]{2,1,0:T(8,128)(2,1)}, u32[]{:S(2)}, u32[]{:S(2)}) %all-to-all-start.9) | async-done | bytes 1572896 | tf_op jit(solution)/shard_map/all_to_all | solution.py:21
  353.5 10.1 %add_bitcast_fusion = f32[1,32,64,256]{3,2,1,0:T(8,128)} fusion(f32[32,64,256]{2,1,0:T(8,128)S(1)} %copy-done.32, bf16[64,32,384]{2,0,1:T(8,128)(2,1)S(1)} %bitcast.298, f32[32,384,256]{2,1,0:T(8,128)} %fusion.79), kind=kOutput, calls=%fused_computation.62 | convolution fusion | flops 431489024 | bytes 18350080 | tf_op jit(solution)/shard_map/ifr,nir->inf/dot_general | solution.py:48
  363.6 2.6 add_bitcast_fusion.1
  366.2 3.4 bitcast_convert_fusion.1
  371.7 17.6 %collective-permute-done.3 = bf16[2048,384]{1,0:T(8,128)(2,1)} collective-permute-done((bf16[2048,384]{1,0:T(8,128)(2,1)}, bf16[2048,384]{1,0:T(8,128)(2,1)}, u32[]{:S(2)}, u32[]{:S(2)}) %collective-permute-start.3) | collective-permute-done | bytes 1572896 | tf_op jit(solution)/shard_map/ppermute | solution.py:9
  389.3 3.3 bitcast_convert_fusion
  (110 shorter events, 40.8 us)
Async XLA Ops:
  0.6 62.2 %copy-start = (bf16[1,32,64,256]{3,2,1,0:T(8,128)(2,1)S(1)}, bf16[1,32,64,256]{3,2,1,0:T(8,128)(2,1)}, u32[]{:S(2)}) copy-start(bf16[1,32,64,256]{3,2,1,0:T(8,128)(2,1)} %param.11) | copy-start | bytes 3145732
  0.6 2.2 copy-start.3
  5.5 24.3 %all-to-all-start = ((bf16[16,128,384]{2,0,1:T(8,128)(2,1)}), bf16[16,128,384]{2,0,1:T(8,128)(2,1)S(1)}, u32[]{:S(2)}, u32[]{:S(2)}) async-start(bf16[16,128,384]{2,0,1:T(8,128)(2,1)} %copy.76), calls=%async_computation | async-start | bytes 3145728 | tf_op jit(solution)/shard_map/all_to_all | solution.py:17
  9.7 3.3 copy-start.19
  11.9 1.2 copy-start.7
  29.8 1.1 copy-start.30
  31.0 24.5 %all-to-all-start.2 = ((bf16[16,128,384]{2,0,1:T(8,128)(2,1)}), bf16[16,128,384]{2,0,1:T(8,128)(2,1)}, u32[]{:S(2)}, u32[]{:S(2)}) async-start(bf16[16,128,384]{2,0,1:T(8,128)(2,1)} %copy.82), calls=%async_computation.2 | async-start | bytes 3145728 | tf_op jit(solution)/shard_map/all_to_all | solution.py:17
  37.6 1.2 copy-start.9
  37.6 134.9 %copy-start.5 = (bf16[1,1,2048,384]{3,2,1,0:T(8,128)(2,1)}, bf16[1,1,2048,384]{3,2,1,0:T(8,128)(2,1)S(1)}, u32[]{:S(2)}) copy-start(bf16[1,1,2048,384]{3,2,1,0:T(8,128)(2,1)S(1)} %get-tuple-element.33) | copy-start | bytes 4718596
  55.5 24.7 %all-to-all-start.3 = ((bf16[16,128,384]{2,0,1:T(8,128)(2,1)}), bf16[16,128,384]{2,0,1:T(8,128)(2,1)}, u32[]{:S(2)}, u32[]{:S(2)}) async-start(bf16[16,128,384]{2,0,1:T(8,128)(2,1)} %copy.85), calls=%async_computation.3 | async-start | bytes 3145728 | tf_op jit(solution)/shard_map/all_to_all | solution.py:17
  80.2 31.3 %all-to-all-start.1 = ((bf16[64,32,384]{2,1,0:T(8,128)(2,1)}), bf16[64,32,384]{2,1,0:T(8,128)(2,1)}, u32[]{:S(2)}, u32[]{:S(2)}) async-start(bf16[64,32,384]{2,1,0:T(8,128)(2,1)} %copy.79), calls=%async_computation.1 | async-start | bytes 3145728 | tf_op jit(solution)/shard_map/all_to_all | solution.py:21
  86.4 8.7 %copy-start.24 = (bf16[16,4,32,384]{3,0,1,2:T(8,128)(2,1)}, bf16[16,4,32,384]{3,0,1,2:T(8,128)(2,1)S(1)}, u32[]{:S(2)}) copy-start(bf16[16,4,32,384]{3,0,1,2:T(8,128)(2,1)S(1)} %copy.86) | copy-start | bytes 4718596
  86.4 8.7 %copy-start.26 = (bf16[16,4,32,384]{3,0,1,2:T(8,128)(2,1)S(1)}, bf16[16,4,32,384]{3,0,1,2:T(8,128)(2,1)}, u32[]{:S(2)}) copy-start(bf16[16,4,32,384]{3,0,1,2:T(8,128)(2,1)} %copy.83) | copy-start | bytes 4718596
  86.4 8.7 %copy-start.34 = (bf16[1,32,64,256]{3,2,1,0:T(8,128)(2,1)S(1)}, bf16[1,32,64,256]{3,2,1,0:T(8,128)(2,1)}, u32[]{:S(2)}) copy-start(bf16[1,32,64,256]{3,2,1,0:T(8,128)(2,1)} %param.12) | copy-start | bytes 3145732
  106.8 2.6 copy-start.1
  111.4 24.5 %all-to-all-start.4 = ((bf16[64,32,384]{2,1,0:T(8,128)(2,1)}), bf16[64,32,384]{2,1,0:T(8,128)(2,1)}, u32[]{:S(2)}, u32[]{:S(2)}) async-start(bf16[64,32,384]{2,1,0:T(8,128)(2,1)} %copy.88), calls=%async_computation.4 | async-start | bytes 3145728 | tf_op jit(solution)/shard_map/all_to_all | solution.py:21
  115.8 1.8 copy-start.20
  117.6 1.9 copy-start.17
  120.9 40.7 %collective-permute-start = (bf16[2048,384]{1,0:T(8,128)(2,1)}, bf16[2048,384]{1,0:T(8,128)(2,1)}, u32[]{:S(2)}, u32[]{:S(2)}) collective-permute-start(bf16[2048,384]{1,0:T(8,128)(2,1)} %fusion.49), channel_id=1, source_target_pairs={{0,4},{4,8},{8,12},{12,16},{16,20},{20,24},{24,28},{28,0},{1,5},{5... | collective-permute-start | bytes 4718600 | tf_op jit(solution)/shard_map/ppermute | solution.py:9
  137.6 1.2 copy-start.13
  137.6 2.5 copy-start.18
  167.7 24.9 %all-to-all-start.7 = ((bf16[16,128,384]{2,0,1:T(8,128)(2,1)}), bf16[16,128,384]{2,0,1:T(8,128)(2,1)}, u32[]{:S(2)}, u32[]{:S(2)}) async-start(bf16[16,128,384]{2,0,1:T(8,128)(2,1)} %copy.99), calls=%async_computation.7 | async-start | bytes 3145728 | tf_op jit(solution)/shard_map/all_to_all | solution.py:17
  192.6 24.5 %all-to-all-start.6 = ((bf16[16,128,384]{2,0,1:T(8,128)(2,1)}), bf16[16,128,384]{2,0,1:T(8,128)(2,1)}, u32[]{:S(2)}, u32[]{:S(2)}) async-start(bf16[16,128,384]{2,0,1:T(8,128)(2,1)} %copy.95), calls=%async_computation.6 | async-start | bytes 3145728 | tf_op jit(solution)/shard_map/all_to_all | solution.py:17
  196.9 37.0 %collective-permute-start.1 = (bf16[2048,384]{1,0:T(8,128)(2,1)}, bf16[2048,384]{1,0:T(8,128)(2,1)S(1)}, u32[]{:S(2)}, u32[]{:S(2)}) collective-permute-start(bf16[2048,384]{1,0:T(8,128)(2,1)} %fusion.48), channel_id=1, source_target_pairs={{0,28},{4,0},{8,4},{12,8},{16,12},{20,16},{24,20},{28,24},{1,29},{... | collective-permute-start | bytes 4718600 | tf_op jit(solution)/shard_map/ppermute | solution.py:9
  217.1 24.5 %all-to-all-start.8 = ((bf16[64,32,384]{2,1,0:T(8,128)(2,1)}), bf16[64,32,384]{2,1,0:T(8,128)(2,1)}, u32[]{:S(2)}, u32[]{:S(2)}) async-start(bf16[64,32,384]{2,1,0:T(8,128)(2,1)} %copy.103), calls=%async_computation.8 | async-start | bytes 3145728 | tf_op jit(solution)/shard_map/all_to_all | solution.py:21
  223.1 6.4 %copy-start.15 = (bf16[16,4,32,384]{3,0,1,2:T(8,128)(2,1)}, bf16[16,4,32,384]{3,0,1,2:T(8,128)(2,1)S(1)}, u32[]{:S(2)}) copy-start(bf16[16,4,32,384]{3,0,1,2:T(8,128)(2,1)S(1)} %copy.96) | copy-start | bytes 4718596
  223.1 10.8 %copy-start.21 = (bf16[1,16,128,128]{3,2,1,0:T(8,128)(2,1)S(1)}, bf16[1,16,128,128]{3,2,1,0:T(8,128)(2,1)}, u32[]{:S(2)}) copy-start(bf16[1,16,128,128]{3,2,1,0:T(8,128)(2,1)} %param.13) | copy-start | bytes 1572868
  233.9 4.7 %copy-start.11 = (bf16[2048,384]{1,0:T(8,128)(2,1)}, bf16[2048,384]{1,0:T(8,128)(2,1)S(1)}, u32[]{:S(2)}) copy-start(bf16[2048,384]{1,0:T(8,128)(2,1)S(1)} %collective-permute-done.1) | copy-start | bytes 4718596
  241.5 16.0 %slice-start = ((s8[6291456]{0:T(1024)(128)(4,1)}), s8[2097152]{0:T(1024)(128)(4,1)S(1)}, s32[]{:S(2)}) async-start(s8[6291456]{0:T(1024)(128)(4,1)} %bitcast.268), calls=%async_computation.12 | async-start | bytes 4194304
  241.5 24.8 %all-to-all-start.5 = ((bf16[16,128,384]{2,0,1:T(8,128)(2,1)}), bf16[16,128,384]{2,0,1:T(8,128)(2,1)}, u32[]{:S(2)}, u32[]{:S(2)}) async-start(bf16[16,128,384]{2,0,1:T(8,128)(2,1)} %copy.91), calls=%async_computation.5 | async-start | bytes 3145728 | tf_op jit(solution)/shard_map/all_to_all | solution.py:17
  246.2 11.3 %slice-start.1 = ((s8[6291456]{0:T(1024)(128)(4,1)}), s8[4194304]{0:T(1024)(128)(4,1)S(1)}, s32[]{:S(2)}) async-start(s8[6291456]{0:T(1024)(128)(4,1)} %bitcast.268), calls=%async_computation.13 | async-start | bytes 8388608
  255.4 2.1 copy-start.27
  266.3 23.6 %all-to-all-start.11 = ((bf16[64,32,384]{2,1,0:T(8,128)(2,1)}), bf16[64,32,384]{2,1,0:T(8,128)(2,1)S(1)}, u32[]{:S(2)}, u32[]{:S(2)}) async-start(bf16[64,32,384]{2,1,0:T(8,128)(2,1)} %copy.116), calls=%async_computation.11 | async-start | bytes 3145728 | tf_op jit(solution)/shard_map/all_to_all | solution.py:21
  275.0 3.7 copy-start.22
  282.7 39.8 %collective-permute-start.2 = (bf16[2048,384]{1,0:T(8,128)(2,1)}, bf16[2048,384]{1,0:T(8,128)(2,1)}, u32[]{:S(2)}, u32[]{:S(2)}) collective-permute-start(bf16[2048,384]{1,0:T(8,128)(2,1)} %fusion.47), channel_id=1, source_target_pairs={{0,4},{4,8},{8,12},{12,16},{16,20},{20,24},{24,28},{28,0},{1,5},{5... | collective-permute-start | bytes 4718600 | tf_op jit(solution)/shard_map/ppermute | solution.py:9
  290.0 17.9 %copy-start.28 = (bf16[64,32,384]{2,1,0:T(8,128)(2,1)}, bf16[64,32,384]{2,1,0:T(8,128)(2,1)S(1)}, u32[]{:S(2)}) copy-start(bf16[64,32,384]{2,1,0:T(8,128)(2,1)S(1)} %all-to-all-done.11) | copy-start | bytes 4718596
  290.0 34.5 %all-to-all-start.10 = ((bf16[64,32,384]{2,1,0:T(8,128)(2,1)}), bf16[64,32,384]{2,1,0:T(8,128)(2,1)}, u32[]{:S(2)}, u32[]{:S(2)}) async-start(bf16[64,32,384]{2,1,0:T(8,128)(2,1)} %copy.113), calls=%async_computation.10 | async-start | bytes 3145728 | tf_op jit(solution)/shard_map/all_to_all | solution.py:21
  307.9 2.7 copy-start.2
  310.5 18.3 %copy-start.25 = (bf16[16,4,32,384]{3,0,1,2:T(8,128)(2,1)S(1)}, bf16[16,4,32,384]{3,0,1,2:T(8,128)(2,1)}, u32[]{:S(2)}) copy-start(bf16[16,4,32,384]{3,0,1,2:T(8,128)(2,1)} %copy-done.24) | copy-start | bytes 4718596
  324.5 24.5 %all-to-all-start.9 = ((bf16[64,32,384]{2,1,0:T(8,128)(2,1)}), bf16[64,32,384]{2,1,0:T(8,128)(2,1)}, u32[]{:S(2)}, u32[]{:S(2)}) async-start(bf16[64,32,384]{2,1,0:T(8,128)(2,1)} %copy.106), calls=%async_computation.9 | async-start | bytes 3145728 | tf_op jit(solution)/shard_map/all_to_all | solution.py:21
  328.9 5.5 %copy-start.29 = (bf16[64,32,384]{2,1,0:T(8,128)(2,1)S(1)}, bf16[64,32,384]{2,1,0:T(8,128)(2,1)}, u32[]{:S(2)}) copy-start(bf16[64,32,384]{2,1,0:T(8,128)(2,1)} %copy-done.28) | copy-start | bytes 4718596
  334.3 2.1 copy-start.10
  334.3 2.4 copy-start.14
  334.6 3.8 copy-start.8
  338.4 1.4 copy-start.12
  339.9 10.8 %copy-start.4 = (bf16[1,16,128,128]{3,2,1,0:T(8,128)(2,1)S(1)}, bf16[1,16,128,128]{3,2,1,0:T(8,128)(2,1)}, u32[]{:S(2)}) copy-start(bf16[1,16,128,128]{3,2,1,0:T(8,128)(2,1)} %param.10) | copy-start | bytes 1572868
  350.6 2.4 copy-start.33
  351.2 2.3 copy-start.32
  351.2 12.3 %slice-start.2 = ((s8[6291456]{0:T(1024)(128)(4,1)}), s8[4194304]{0:T(1024)(128)(4,1)S(1)}, s32[]{:S(2)}) async-start(s8[6291456]{0:T(1024)(128)(4,1)} %bitcast.270), calls=%async_computation.14 | async-start | bytes 8388608
  352.8 10.8 %slice-start.3 = ((s8[6291456]{0:T(1024)(128)(4,1)}), s8[2097152]{0:T(1024)(128)(4,1)S(1)}, s32[]{:S(2)}) async-start(s8[6291456]{0:T(1024)(128)(4,1)} %bitcast.270), calls=%async_computation.15 | async-start | bytes 4194304
  352.8 10.8 %copy-start.16 = (bf16[16,4,32,384]{3,0,1,2:T(8,128)(2,1)S(1)}, bf16[16,4,32,384]{3,0,1,2:T(8,128)(2,1)}, u32[]{:S(2)}) copy-start(bf16[16,4,32,384]{3,0,1,2:T(8,128)(2,1)} %copy-done.15) | copy-start | bytes 4718596
  352.8 10.8 %copy-start.23 = (f32[32,64,256]{2,1,0:T(8,128)S(1)}, f32[32,64,256]{2,1,0:T(8,128)}, u32[]{:S(2)}) copy-start(f32[32,64,256]{2,1,0:T(8,128)} %fusion.112) | copy-start | bytes 6291460
  352.8 36.5 %collective-permute-start.3 = (bf16[2048,384]{1,0:T(8,128)(2,1)}, bf16[2048,384]{1,0:T(8,128)(2,1)}, u32[]{:S(2)}, u32[]{:S(2)}) collective-permute-start(bf16[2048,384]{1,0:T(8,128)(2,1)} %fusion.46), channel_id=1, source_target_pairs={{0,28},{4,0},{8,4},{12,8},{16,12},{20,16},{24,20},{28,24},{1,29},{... | collective-permute-start | bytes 4718600 | tf_op jit(solution)/shard_map/ppermute | solution.py:9
  366.2 3.4 copy-start.6
  366.2 3.4 copy-start.31

commit v3 on v2

--- a/solution.py
+++ b/solution.py
@@ -59,9 +59,9 @@
     column_grad = jnp.einsum(
         "ifr,inf->nir", grad_pre, second_up, preferred_element_type=jnp.float32
     ).astype(jnp.bfloat16)
+    grad_first = to_rows(column_grad)
     if held is not None:
-        column_grad, held = lax.optimization_barrier((column_grad, held))
-    grad_first = to_rows(column_grad)
+        grad_first, held = lax.optimization_barrier((grad_first, held))
     grad_first_up = jnp.einsum(
         "njr,nir->nji", narrow_in, grad_first, preferred_element_type=jnp.float32
     )

time: 399 us -> 389 us (0.975)
  waiting for transfers between devices: 141 us -> 130 us
    ppermute x4, waiting for transfers between devices: 53.9 us -> 41.1 us  [shifted(): lax.ppermute(value, axis, [(i, (i + by) % count) for i in range(count)])]
  transfers between devices with their start and end apart: 16 -> 16, of which waited for: 14 -> 14; matrix products, arithmetic and copies ran while one was open for 42% -> 44% of each run, Pallas kernels for 0% -> 0%
where the time goes in v3:
time: 389 us; the launch traced here: 383 us
  waiting for transfers between devices  130 us (33%)
  matrix products  109 us (28%)
  local copies, waits for them, and re-layouts  64.9 us (17%)
  starting transfers between devices  58.7 us (15%)
  other arithmetic  18.6 us (5%)
    all_to_all x6, waiting for transfers between devices, to_columns(): lax.all_to_all(value, 'tensor', split_axis=1, concat_axis=0, tiled=True)  59.6 us
    ppermute x4, waiting for transfers between devices, shifted(): lax.ppermute(value, axis, [(i, (i + by) % count) for i in range(count)])  41.1 us
    dot_general x4, matrix products, front(): jnp.einsum('ifr,inf->nir', hidden, first_down, preferred_element_type=jnp...  29.6 us
    all_to_all x6, waiting for transfers between devices, to_rows(): lax.all_to_all(value, 'tensor', split_axis=0, concat_axis=1, tiled=True)  29.5 us
    all_to_all x6, starting transfers between devices, to_columns(): lax.all_to_all(value, 'tensor', split_axis=1, concat_axis=0, tiled=True)  26.9 us
    all_to_all x6, starting transfers between devices, to_rows(): lax.all_to_all(value, 'tensor', split_axis=0, concat_axis=1, tiled=True)  25.7 us
    dot_general x2, matrix products, backward(): jnp.einsum('nir,inf->ifr', grad_folded, first_down, preferred_element_typ...  24.9 us
    dot_general x2, matrix products, front(): jnp.einsum('nir,inf->ifr', spread, second_up, preferred_element_type=jnp....  15.1 us
  transfers between devices with their start and end apart: 16, of which 14 were waited for; matrix products, arithmetic and copies ran while one was open for 44% of the time, Pallas kernels for 0%

profile of v3, /device:TPU:0, one launch (start us, length us, event | category | flops | bytes accessed | tf_op | source)
XLA Modules:
  0.0 383.0 jit_solution(12138659443807794390)
XLA Ops:
  0.7 2.2 convert_element_type.112
  3.5 2.1 copy.76
  5.5 4.2 %all-to-all-start = ((bf16[16,128,384]{2,0,1:T(8,128)(2,1)}), bf16[16,128,384]{2,0,1:T(8,128)(2,1)S(1)}, u32[]{:S(2)}, u32[]{:S(2)}) async-start(bf16[16,128,384]{2,0,1:T(8,128)(2,1)} %copy.76), calls=%async_computation | async-start | bytes 3145728 | tf_op jit(solution)/shard_map/all_to_all | solution.py:17
  9.8 2.1 convert_element_type.119
  13.6 2.1 copy.82
  15.7 14.1 %all-to-all-done = bf16[16,128,384]{2,0,1:T(8,128)(2,1)S(1)} async-done(((bf16[16,128,384]{2,0,1:T(8,128)(2,1)}), bf16[16,128,384]{2,0,1:T(8,128)(2,1)S(1)}, u32[]{:S(2)}, u32[]{:S(2)}) %all-to-all-start) | async-done | bytes 1572896 | tf_op jit(solution)/shard_map/all_to_all | solution.py:17
  31.0 4.4 %all-to-all-start.2 = ((bf16[16,128,384]{2,0,1:T(8,128)(2,1)}), bf16[16,128,384]{2,0,1:T(8,128)(2,1)}, u32[]{:S(2)}, u32[]{:S(2)}) async-start(bf16[16,128,384]{2,0,1:T(8,128)(2,1)} %copy.82), calls=%async_computation.2 | async-start | bytes 3145728 | tf_op jit(solution)/shard_map/all_to_all | solution.py:17
  35.4 2.2 fusion.110
  39.4 2.1 copy.85
  41.4 14.1 %all-to-all-done.2 = bf16[16,128,384]{2,0,1:T(8,128)(2,1)} async-done(((bf16[16,128,384]{2,0,1:T(8,128)(2,1)}), bf16[16,128,384]{2,0,1:T(8,128)(2,1)}, u32[]{:S(2)}, u32[]{:S(2)}) %all-to-all-start.2) | async-done | bytes 1572896 | tf_op jit(solution)/shard_map/all_to_all | solution.py:17
  55.5 4.5 %all-to-all-start.3 = ((bf16[16,128,384]{2,0,1:T(8,128)(2,1)}), bf16[16,128,384]{2,0,1:T(8,128)(2,1)}, u32[]{:S(2)}, u32[]{:S(2)}) async-start(bf16[16,128,384]{2,0,1:T(8,128)(2,1)} %copy.85), calls=%async_computation.3 | async-start | bytes 3145728 | tf_op jit(solution)/shard_map/all_to_all | solution.py:17
  60.0 2.8 copy.77
  62.9 7.6 %fusion.59 = bf16[64,32,384]{2,0,1:T(8,128)(2,1)} fusion(bf16[64,32,384]{2,0,1:T(8,128)(2,1)} %bitcast.299, bf16[1,32,64,256]{3,2,1,0:T(8,128)(2,1)} %param.12, bf16[1,32,64,256]{3,2,1,0:T(8,128)(2,1)S(1)} %copy-done), kind=kOutput, calls=%fused_computation.79 | convolution fusion | flops 834404352 | bytes 5242880 | tf_op jit(solution)/shard_map/ifr,inf->nir/dot_general | solution.py:31
  70.5 3.5 copy.79
  74.0 2.8 copy.83
  76.8 3.3 all-to-all-done.3
  80.2 4.6 %all-to-all-start.1 = ((bf16[64,32,384]{2,1,0:T(8,128)(2,1)}), bf16[64,32,384]{2,1,0:T(8,128)(2,1)}, u32[]{:S(2)}, u32[]{:S(2)}) async-start(bf16[64,32,384]{2,1,0:T(8,128)(2,1)} %copy.79), calls=%async_computation.1 | async-start | bytes 3145728 | tf_op jit(solution)/shard_map/all_to_all | solution.py:21
  86.4 8.7 %fusion.34 = (bf16[32,256,384]{1,2,0:T(8,128)(2,1)}, f32[32,384,256]{2,1,0:T(8,128)}) fusion(bf16[64,32,384]{2,0,1:T(8,128)(2,1)S(1)} %bitcast.286, bf16[1,32,64,256]{3,2,1,0:T(8,128)(2,1)S(1)} %copy-done), kind=kOutput, calls=%fused_computation.45 | convolution fusion | flops 430964736 | bytes 21495808 | tf_op jit(solution)/shard_map/nir,inf->ifr/dot_general | solution.py:29
  95.1 11.6 %fusion.6 = bf16[32,256,384]{1,2,0:T(8,128)(2,1)S(1)} fusion(f32[32,384,256]{2,1,0:T(8,128)} %get-tuple-element.35, bf16[64,32,384]{2,0,1:T(8,128)(2,1)S(1)} %bitcast.288, bf16[1,32,64,256]{3,2,1,0:T(8,128)(2,1)S(1)} %copy-done.34), kind=kOutput, calls=%fused_computation.12 | convolution fusion | flops 465567744 | bytes 21495808 | tf_op jit(solution)/shard_map/nir,inf->ifr/dot_general | solution.py:51
  106.8 2.1 fusion.62
  109.4 2.1 copy.88
  111.4 4.4 %all-to-all-start.4 = ((bf16[64,32,384]{2,1,0:T(8,128)(2,1)}), bf16[64,32,384]{2,1,0:T(8,128)(2,1)}, u32[]{:S(2)}, u32[]{:S(2)}) async-start(bf16[64,32,384]{2,1,0:T(8,128)(2,1)} %copy.88), calls=%async_computation.4 | async-start | bytes 3145728 | tf_op jit(solution)/shard_map/all_to_all | solution.py:21
  120.9 2.3 collective-permute-start
  123.2 12.7 %all-to-all-done.4 = bf16[64,32,384]{2,1,0:T(8,128)(2,1)} async-done(((bf16[64,32,384]{2,1,0:T(8,128)(2,1)}), bf16[64,32,384]{2,1,0:T(8,128)(2,1)}, u32[]{:S(2)}, u32[]{:S(2)}) %all-to-all-start.4) | async-done | bytes 1572896 | tf_op jit(solution)/shard_map/all_to_all | solution.py:21
  141.6 20.0 %collective-permute-done = bf16[2048,384]{1,0:T(8,128)(2,1)} collective-permute-done((bf16[2048,384]{1,0:T(8,128)(2,1)}, bf16[2048,384]{1,0:T(8,128)(2,1)}, u32[]{:S(2)}, u32[]{:S(2)}) %collective-permute-start) | collective-permute-done | bytes 1572896 | tf_op jit(solution)/shard_map/ppermute | solution.py:9
  161.6 3.2 fusion.67
  164.8 2.9 copy.101
  167.7 4.8 %all-to-all-start.8 = ((bf16[16,128,384]{2,0,1:T(8,128)(2,1)}), bf16[16,128,384]{2,0,1:T(8,128)(2,1)}, u32[]{:S(2)}, u32[]{:S(2)}) async-start(bf16[16,128,384]{2,0,1:T(8,128)(2,1)} %copy.101), calls=%async_computation.8 | async-start | bytes 3145728 | tf_op jit(solution)/shard_map/all_to_all | solution.py:17
  173.1 2.1 copy.95
  175.1 17.4 %all-to-all-done.8 = bf16[16,128,384]{2,0,1:T(8,128)(2,1)} async-done(((bf16[16,128,384]{2,0,1:T(8,128)(2,1)}), bf16[16,128,384]{2,0,1:T(8,128)(2,1)}, u32[]{:S(2)}, u32[]{:S(2)}) %all-to-all-start.8) | async-done | bytes 1572896 | tf_op jit(solution)/shard_map/all_to_all | solution.py:17
  192.6 4.3 %all-to-all-start.6 = ((bf16[16,128,384]{2,0,1:T(8,128)(2,1)}), bf16[16,128,384]{2,0,1:T(8,128)(2,1)}, u32[]{:S(2)}, u32[]{:S(2)}) async-start(bf16[16,128,384]{2,0,1:T(8,128)(2,1)} %copy.95), calls=%async_computation.6 | async-start | bytes 3145728 | tf_op jit(solution)/shard_map/all_to_all | solution.py:17
  198.7 2.8 copy.103
  201.6 7.6 %fusion.56 = bf16[64,32,384]{2,0,1:T(8,128)(2,1)} fusion(bf16[64,32,384]{2,0,1:T(8,128)(2,1)} %bitcast.300, bf16[1,32,64,256]{3,2,1,0:T(8,128)(2,1)} %param.12, bf16[1,32,64,256]{3,2,1,0:T(8,128)(2,1)S(1)} %copy-done), kind=kOutput, calls=%fused_computation.78 | convolution fusion | flops 834404352 | bytes 5242880 | tf_op jit(solution)/shard_map/ifr,inf->nir/dot_general | solution.py:31
  209.2 3.5 copy.105
  212.7 4.4 %all-to-all-done.6 = bf16[16,128,384]{2,0,1:T(8,128)(2,1)} async-done(((bf16[16,128,384]{2,0,1:T(8,128)(2,1)}), bf16[16,128,384]{2,0,1:T(8,128)(2,1)}, u32[]{:S(2)}, u32[]{:S(2)}) %all-to-all-start.6) | async-done | bytes 1572896 | tf_op jit(solution)/shard_map/all_to_all | solution.py:17
  217.1 4.3 %all-to-all-start.9 = ((bf16[64,32,384]{2,1,0:T(8,128)(2,1)}), bf16[64,32,384]{2,1,0:T(8,128)(2,1)}, u32[]{:S(2)}, u32[]{:S(2)}) async-start(bf16[64,32,384]{2,1,0:T(8,128)(2,1)} %copy.105), calls=%async_computation.9 | async-start | bytes 3145728 | tf_op jit(solution)/shard_map/all_to_all | solution.py:21
  223.1 6.4 %fusion.79 = f32[32,384,256]{2,1,0:T(8,128)} fusion(bf16[64,32,384]{2,0,1:T(8,128)(2,1)S(1)} %bitcast.282, bf16[1,32,64,256]{3,2,1,0:T(8,128)(2,1)S(1)} %copy-done), kind=kOutput, calls=%fused_computation.98 | convolution fusion | flops 402653184 | bytes 15204352 | tf_op jit(solution)/shard_map/nir,inf->ifr/dot_general | solution.py:29
  229.5 4.4 %collective-permute-done.1 = bf16[2048,384]{1,0:T(8,128)(2,1)S(1)} collective-permute-done((bf16[2048,384]{1,0:T(8,128)(2,1)}, bf16[2048,384]{1,0:T(8,128)(2,1)S(1)}, u32[]{:S(2)}, u32[]{:S(2)}) %collective-permute-start.1) | collective-permute-done | bytes 1572896 | tf_op jit(solution)/shard_map/ppermute | solution.py:9
  235.7 2.9 copy.91
  238.6 2.9 all-to-all-done.9
  241.5 4.7 %all-to-all-start.5 = ((bf16[16,128,384]{2,0,1:T(8,128)(2,1)}), bf16[16,128,384]{2,0,1:T(8,128)(2,1)}, u32[]{:S(2)}, u32[]{:S(2)}) async-start(bf16[16,128,384]{2,0,1:T(8,128)(2,1)} %copy.91), calls=%async_computation.5 | async-start | bytes 3145728 | tf_op jit(solution)/shard_map/all_to_all | solution.py:17
  246.2 9.2 %fusion.65 = bf16[64,32,384]{2,0,1:T(8,128)(2,1)S(1)} fusion(bf16[1,32,64,256]{3,2,1,0:T(8,128)(2,1)} %param.12, f32[32,384,256]{2,1,0:T(8,128)} %fusion.79), kind=kOutput, calls=%fused_computation.83 | convolution fusion | flops 431751168 | bytes 15204352 | tf_op jit(solution)/shard_map/ifr,inf->nir/dot_general | solution.py:31
  255.4 2.1 copy.116
  257.5 2.6 fusion.113
  260.1 6.2 %all-to-all-done.5 = bf16[16,128,384]{2,0,1:T(8,128)(2,1)} async-done(((bf16[16,128,384]{2,0,1:T(8,128)(2,1)}), bf16[16,128,384]{2,0,1:T(8,128)(2,1)}, u32[]{:S(2)}, u32[]{:S(2)}) %all-to-all-start.5) | async-done | bytes 1572896 | tf_op jit(solution)/shard_map/all_to_all | solution.py:17
  266.3 3.6 all-to-all-start.11
  269.9 5.1 %fusion.64 = bf16[64,32,384]{2,0,1:T(8,128)(2,1)S(1)} fusion(bf16[32,256,384]{1,2,0:T(8,128)(2,1)} %get-tuple-element.34, bf16[1,32,64,256]{3,2,1,0:T(8,128)(2,1)} %param.12), kind=kOutput, calls=%fused_computation.82 | convolution fusion | flops 403439616 | bytes 8912896 | tf_op jit(solution)/shard_map/ifr,inf->nir/dot_general | solution.py:31
  275.0 2.1 copy.113
  279.4 3.3 fusion.47
  282.7 2.8 copy.93
  285.5 4.5 %all-to-all-done.11 = bf16[64,32,384]{2,1,0:T(8,128)(2,1)S(1)} async-done(((bf16[64,32,384]{2,1,0:T(8,128)(2,1)}), bf16[64,32,384]{2,1,0:T(8,128)(2,1)S(1)}, u32[]{:S(2)}, u32[]{:S(2)}) %all-to-all-start.11) | async-done | bytes 1572896 | tf_op jit(solution)/shard_map/all_to_all | solution.py:21
  289.9 4.6 %all-to-all-start.10 = ((bf16[64,32,384]{2,1,0:T(8,128)(2,1)}), bf16[64,32,384]{2,1,0:T(8,128)(2,1)}, u32[]{:S(2)}, u32[]{:S(2)}) async-start(bf16[64,32,384]{2,1,0:T(8,128)(2,1)} %copy.113), calls=%async_computation.10 | async-start | bytes 3145728 | tf_op jit(solution)/shard_map/all_to_all | solution.py:21
  294.5 13.3 %fusion.13 = bf16[32,256,384]{1,2,0:T(8,128)(2,1)S(1)} fusion(f32[32,384,256]{2,1,0:T(8,128)} %fusion.79, bf16[64,32,384]{2,0,1:T(8,128)(2,1)} %bitcast.297, bf16[1,32,64,256]{3,2,1,0:T(8,128)(2,1)} %param.12), kind=kOutput, calls=%fused_computation.19 | convolution fusion | flops 465567744 | bytes 21495808 | tf_op jit(solution)/shard_map/nir,inf->ifr/dot_general | solution.py:51
  307.9 2.1 fusion.63
  310.5 2.1 copy.98
  312.6 2.0 all-to-all-done.10
  314.7 4.3 %all-to-all-start.7 = ((bf16[64,32,384]{2,1,0:T(8,128)(2,1)}), bf16[64,32,384]{2,1,0:T(8,128)(2,1)}, u32[]{:S(2)}, u32[]{:S(2)}) async-start(bf16[64,32,384]{2,1,0:T(8,128)(2,1)} %copy.98), calls=%async_computation.7 | async-start | bytes 3145728 | tf_op jit(solution)/shard_map/all_to_all | solution.py:21
  319.0 5.5 %fusion.112 = f32[32,64,256]{2,1,0:T(8,128)} fusion(bf16[64,32,384]{2,0,1:T(8,128)(2,1)S(1)} %bitcast.287, bf16[32,256,384]{1,2,0:T(8,128)(2,1)} %copy-done.1), kind=kOutput, calls=%fused_computation.128 | convolution fusion | flops 402653184 | bytes 9961472 | tf_op jit(solution)/shard_map/nir,ifr->inf/dot_general | solution.py:56
  331.8 7.3 %all-to-all-done.7 = bf16[64,32,384]{2,1,0:T(8,128)(2,1)} async-done(((bf16[64,32,384]{2,1,0:T(8,128)(2,1)}), bf16[64,32,384]{2,1,0:T(8,128)(2,1)}, u32[]{:S(2)}, u32[]{:S(2)}) %all-to-all-start.7) | async-done | bytes 1572896 | tf_op jit(solution)/shard_map/all_to_all | solution.py:21
  344.9 9.8 %add_bitcast_fusion = f32[1,32,64,256]{3,2,1,0:T(8,128)} fusion(f32[32,64,256]{2,1,0:T(8,128)S(1)} %copy-done.32, bf16[64,32,384]{2,0,1:T(8,128)(2,1)S(1)} %bitcast.298, f32[32,384,256]{2,1,0:T(8,128)} %fusion.79), kind=kOutput, calls=%fused_computation.62 | convolution fusion | flops 431489024 | bytes 18350080 | tf_op jit(solution)/shard_map/ifr,nir->inf/dot_general | solution.py:48
  354.8 2.6 add_bitcast_fusion.1
  359.5 3.3 bitcast_convert_fusion.1
  362.7 16.7 %collective-permute-done.3 = bf16[2048,384]{1,0:T(8,128)(2,1)} collective-permute-done((bf16[2048,384]{1,0:T(8,128)(2,1)}, bf16[2048,384]{1,0:T(8,128)(2,1)}, u32[]{:S(2)}, u32[]{:S(2)}) %collective-permute-start.3) | collective-permute-done | bytes 1572896 | tf_op jit(solution)/shard_map/ppermute | solution.py:9
  379.4 3.3 bitcast_convert_fusion
  (110 shorter events, 42.1 us)
Async XLA Ops:
  0.6 62.2 %copy-start = (bf16[1,32,64,256]{3,2,1,0:T(8,128)(2,1)S(1)}, bf16[1,32,64,256]{3,2,1,0:T(8,128)(2,1)}, u32[]{:S(2)}) copy-start(bf16[1,32,64,256]{3,2,1,0:T(8,128)(2,1)} %param.11) | copy-start | bytes 3145732
  0.6 2.2 copy-start.3
  5.5 24.3 %all-to-all-start = ((bf16[16,128,384]{2,0,1:T(8,128)(2,1)}), bf16[16,128,384]{2,0,1:T(8,128)(2,1)S(1)}, u32[]{:S(2)}, u32[]{:S(2)}) async-start(bf16[16,128,384]{2,0,1:T(8,128)(2,1)} %copy.76), calls=%async_computation | async-start | bytes 3145728 | tf_op jit(solution)/shard_map/all_to_all | solution.py:17
  9.7 3.3 copy-start.19
  11.9 1.2 copy-start.7
  29.8 1.1 copy-start.30
  31.0 24.5 %all-to-all-start.2 = ((bf16[16,128,384]{2,0,1:T(8,128)(2,1)}), bf16[16,128,384]{2,0,1:T(8,128)(2,1)}, u32[]{:S(2)}, u32[]{:S(2)}) async-start(bf16[16,128,384]{2,0,1:T(8,128)(2,1)} %copy.82), calls=%async_computation.2 | async-start | bytes 3145728 | tf_op jit(solution)/shard_map/all_to_all | solution.py:17
  37.6 1.2 copy-start.9
  37.6 134.9 %copy-start.5 = (bf16[1,1,2048,384]{3,2,1,0:T(8,128)(2,1)}, bf16[1,1,2048,384]{3,2,1,0:T(8,128)(2,1)S(1)}, u32[]{:S(2)}) copy-start(bf16[1,1,2048,384]{3,2,1,0:T(8,128)(2,1)S(1)} %get-tuple-element.33) | copy-start | bytes 4718596
  55.5 24.7 %all-to-all-start.3 = ((bf16[16,128,384]{2,0,1:T(8,128)(2,1)}), bf16[16,128,384]{2,0,1:T(8,128)(2,1)}, u32[]{:S(2)}, u32[]{:S(2)}) async-start(bf16[16,128,384]{2,0,1:T(8,128)(2,1)} %copy.85), calls=%async_computation.3 | async-start | bytes 3145728 | tf_op jit(solution)/shard_map/all_to_all | solution.py:17
  80.2 31.3 %all-to-all-start.1 = ((bf16[64,32,384]{2,1,0:T(8,128)(2,1)}), bf16[64,32,384]{2,1,0:T(8,128)(2,1)}, u32[]{:S(2)}, u32[]{:S(2)}) async-start(bf16[64,32,384]{2,1,0:T(8,128)(2,1)} %copy.79), calls=%async_computation.1 | async-start | bytes 3145728 | tf_op jit(solution)/shard_map/all_to_all | solution.py:21
  86.4 8.7 %copy-start.24 = (bf16[16,4,32,384]{3,0,1,2:T(8,128)(2,1)}, bf16[16,4,32,384]{3,0,1,2:T(8,128)(2,1)S(1)}, u32[]{:S(2)}) copy-start(bf16[16,4,32,384]{3,0,1,2:T(8,128)(2,1)S(1)} %copy.86) | copy-start | bytes 4718596
  86.4 8.7 %copy-start.26 = (bf16[16,4,32,384]{3,0,1,2:T(8,128)(2,1)S(1)}, bf16[16,4,32,384]{3,0,1,2:T(8,128)(2,1)}, u32[]{:S(2)}) copy-start(bf16[16,4,32,384]{3,0,1,2:T(8,128)(2,1)} %copy.83) | copy-start | bytes 4718596
  86.4 8.7 %copy-start.34 = (bf16[1,32,64,256]{3,2,1,0:T(8,128)(2,1)S(1)}, bf16[1,32,64,256]{3,2,1,0:T(8,128)(2,1)}, u32[]{:S(2)}) copy-start(bf16[1,32,64,256]{3,2,1,0:T(8,128)(2,1)} %param.12) | copy-start | bytes 3145732
  106.8 2.6 copy-start.1
  111.4 24.5 %all-to-all-start.4 = ((bf16[64,32,384]{2,1,0:T(8,128)(2,1)}), bf16[64,32,384]{2,1,0:T(8,128)(2,1)}, u32[]{:S(2)}, u32[]{:S(2)}) async-start(bf16[64,32,384]{2,1,0:T(8,128)(2,1)} %copy.88), calls=%async_computation.4 | async-start | bytes 3145728 | tf_op jit(solution)/shard_map/all_to_all | solution.py:21
  115.8 1.8 copy-start.20
  117.6 1.9 copy-start.17
  120.9 40.7 %collective-permute-start = (bf16[2048,384]{1,0:T(8,128)(2,1)}, bf16[2048,384]{1,0:T(8,128)(2,1)}, u32[]{:S(2)}, u32[]{:S(2)}) collective-permute-start(bf16[2048,384]{1,0:T(8,128)(2,1)} %fusion.49), channel_id=1, source_target_pairs={{0,4},{4,8},{8,12},{12,16},{16,20},{20,24},{24,28},{28,0},{1,5},{5... | collective-permute-start | bytes 4718600 | tf_op jit(solution)/shard_map/ppermute | solution.py:9
  137.6 1.2 copy-start.13
  137.6 2.5 copy-start.18
  167.7 24.9 %all-to-all-start.8 = ((bf16[16,128,384]{2,0,1:T(8,128)(2,1)}), bf16[16,128,384]{2,0,1:T(8,128)(2,1)}, u32[]{:S(2)}, u32[]{:S(2)}) async-start(bf16[16,128,384]{2,0,1:T(8,128)(2,1)} %copy.101), calls=%async_computation.8 | async-start | bytes 3145728 | tf_op jit(solution)/shard_map/all_to_all | solution.py:17
  192.6 24.5 %all-to-all-start.6 = ((bf16[16,128,384]{2,0,1:T(8,128)(2,1)}), bf16[16,128,384]{2,0,1:T(8,128)(2,1)}, u32[]{:S(2)}, u32[]{:S(2)}) async-start(bf16[16,128,384]{2,0,1:T(8,128)(2,1)} %copy.95), calls=%async_computation.6 | async-start | bytes 3145728 | tf_op jit(solution)/shard_map/all_to_all | solution.py:17
  196.9 37.0 %collective-permute-start.1 = (bf16[2048,384]{1,0:T(8,128)(2,1)}, bf16[2048,384]{1,0:T(8,128)(2,1)S(1)}, u32[]{:S(2)}, u32[]{:S(2)}) collective-permute-start(bf16[2048,384]{1,0:T(8,128)(2,1)} %fusion.48), channel_id=1, source_target_pairs={{0,28},{4,0},{8,4},{12,8},{16,12},{20,16},{24,20},{28,24},{1,29},{... | collective-permute-start | bytes 4718600 | tf_op jit(solution)/shard_map/ppermute | solution.py:9
  217.1 24.5 %all-to-all-start.9 = ((bf16[64,32,384]{2,1,0:T(8,128)(2,1)}), bf16[64,32,384]{2,1,0:T(8,128)(2,1)}, u32[]{:S(2)}, u32[]{:S(2)}) async-start(bf16[64,32,384]{2,1,0:T(8,128)(2,1)} %copy.105), calls=%async_computation.9 | async-start | bytes 3145728 | tf_op jit(solution)/shard_map/all_to_all | solution.py:21
  223.1 6.4 %copy-start.15 = (bf16[16,4,32,384]{3,0,1,2:T(8,128)(2,1)}, bf16[16,4,32,384]{3,0,1,2:T(8,128)(2,1)S(1)}, u32[]{:S(2)}) copy-start(bf16[16,4,32,384]{3,0,1,2:T(8,128)(2,1)S(1)} %copy.96) | copy-start | bytes 4718596
  223.1 10.8 %copy-start.21 = (bf16[1,16,128,128]{3,2,1,0:T(8,128)(2,1)S(1)}, bf16[1,16,128,128]{3,2,1,0:T(8,128)(2,1)}, u32[]{:S(2)}) copy-start(bf16[1,16,128,128]{3,2,1,0:T(8,128)(2,1)} %param.13) | copy-start | bytes 1572868
  233.9 4.7 %copy-start.11 = (bf16[2048,384]{1,0:T(8,128)(2,1)}, bf16[2048,384]{1,0:T(8,128)(2,1)S(1)}, u32[]{:S(2)}) copy-start(bf16[2048,384]{1,0:T(8,128)(2,1)S(1)} %collective-permute-done.1) | copy-start | bytes 4718596
  241.5 16.0 %slice-start = ((s8[6291456]{0:T(1024)(128)(4,1)}), s8[2097152]{0:T(1024)(128)(4,1)S(1)}, s32[]{:S(2)}) async-start(s8[6291456]{0:T(1024)(128)(4,1)} %bitcast.268), calls=%async_computation.12 | async-start | bytes 4194304
  241.5 24.8 %all-to-all-start.5 = ((bf16[16,128,384]{2,0,1:T(8,128)(2,1)}), bf16[16,128,384]{2,0,1:T(8,128)(2,1)}, u32[]{:S(2)}, u32[]{:S(2)}) async-start(bf16[16,128,384]{2,0,1:T(8,128)(2,1)} %copy.91), calls=%async_computation.5 | async-start | bytes 3145728 | tf_op jit(solution)/shard_map/all_to_all | solution.py:17
  246.2 11.3 %slice-start.1 = ((s8[6291456]{0:T(1024)(128)(4,1)}), s8[4194304]{0:T(1024)(128)(4,1)S(1)}, s32[]{:S(2)}) async-start(s8[6291456]{0:T(1024)(128)(4,1)} %bitcast.268), calls=%async_computation.13 | async-start | bytes 8388608
  255.4 2.1 copy-start.27
  266.3 23.6 %all-to-all-start.11 = ((bf16[64,32,384]{2,1,0:T(8,128)(2,1)}), bf16[64,32,384]{2,1,0:T(8,128)(2,1)S(1)}, u32[]{:S(2)}, u32[]{:S(2)}) async-start(bf16[64,32,384]{2,1,0:T(8,128)(2,1)} %copy.116), calls=%async_computation.11 | async-start | bytes 3145728 | tf_op jit(solution)/shard_map/all_to_all | solution.py:21
  275.0 3.7 copy-start.22
  282.6 58.1 %collective-permute-start.2 = (bf16[2048,384]{1,0:T(8,128)(2,1)}, bf16[2048,384]{1,0:T(8,128)(2,1)}, u32[]{:S(2)}, u32[]{:S(2)}) collective-permute-start(bf16[2048,384]{1,0:T(8,128)(2,1)} %fusion.47), channel_id=1, source_target_pairs={{0,4},{4,8},{8,12},{12,16},{16,20},{20,24},{24,28},{28,0},{1,5},{5... | collective-permute-start | bytes 4718600 | tf_op jit(solution)/shard_map/ppermute | solution.py:9
  289.9 17.9 %copy-start.28 = (bf16[64,32,384]{2,1,0:T(8,128)(2,1)}, bf16[64,32,384]{2,1,0:T(8,128)(2,1)S(1)}, u32[]{:S(2)}) copy-start(bf16[64,32,384]{2,1,0:T(8,128)(2,1)S(1)} %all-to-all-done.11) | copy-start | bytes 4718596
  289.9 24.7 %all-to-all-start.10 = ((bf16[64,32,384]{2,1,0:T(8,128)(2,1)}), bf16[64,32,384]{2,1,0:T(8,128)(2,1)}, u32[]{:S(2)}, u32[]{:S(2)}) async-start(bf16[64,32,384]{2,1,0:T(8,128)(2,1)} %copy.113), calls=%async_computation.10 | async-start | bytes 3145728 | tf_op jit(solution)/shard_map/all_to_all | solution.py:21
  307.8 2.7 copy-start.2
  310.5 8.5 %copy-start.25 = (bf16[16,4,32,384]{3,0,1,2:T(8,128)(2,1)S(1)}, bf16[16,4,32,384]{3,0,1,2:T(8,128)(2,1)}, u32[]{:S(2)}) copy-start(bf16[16,4,32,384]{3,0,1,2:T(8,128)(2,1)} %copy-done.24) | copy-start | bytes 4718596
  314.7 24.5 %all-to-all-start.7 = ((bf16[64,32,384]{2,1,0:T(8,128)(2,1)}), bf16[64,32,384]{2,1,0:T(8,128)(2,1)}, u32[]{:S(2)}, u32[]{:S(2)}) async-start(bf16[64,32,384]{2,1,0:T(8,128)(2,1)} %copy.98), calls=%async_computation.7 | async-start | bytes 3145728 | tf_op jit(solution)/shard_map/all_to_all | solution.py:21
  319.0 5.5 %copy-start.29 = (bf16[64,32,384]{2,1,0:T(8,128)(2,1)S(1)}, bf16[64,32,384]{2,1,0:T(8,128)(2,1)}, u32[]{:S(2)}) copy-start(bf16[64,32,384]{2,1,0:T(8,128)(2,1)} %copy-done.28) | copy-start | bytes 4718596
  324.5 2.1 copy-start.10
  324.5 2.4 copy-start.14
  324.7 3.8 %copy-start.8 = (bf16[1,2048,384]{2,1,0:T(8,128)(2,1)S(1)}, bf16[1,2048,384]{2,1,0:T(8,128)(2,1)}, u32[]{:S(2)}) copy-start(bf16[1,2048,384]{2,1,0:T(8,128)(2,1)} %copy-done.7) | copy-start | bytes 4718596
  328.6 1.4 copy-start.12
  330.0 10.8 %copy-start.4 = (bf16[1,16,128,128]{3,2,1,0:T(8,128)(2,1)S(1)}, bf16[1,16,128,128]{3,2,1,0:T(8,128)(2,1)}, u32[]{:S(2)}) copy-start(bf16[1,16,128,128]{3,2,1,0:T(8,128)(2,1)} %param.10) | copy-start | bytes 1572868
  340.8 4.1 %copy-start.33 = (bf16[4,16,32,384]{3,1,0,2:T(8,128)(2,1)S(1)}, bf16[4,16,32,384]{3,1,0,2:T(8,128)(2,1)}, u32[]{:S(2)}) copy-start(bf16[4,16,32,384]{3,1,0,2:T(8,128)(2,1)} %copy.93) | copy-start | bytes 4718596
  341.4 3.5 copy-start.32
  341.4 13.3 %slice-start.2 = ((s8[6291456]{0:T(1024)(128)(4,1)}), s8[4194304]{0:T(1024)(128)(4,1)S(1)}, s32[]{:S(2)}) async-start(s8[6291456]{0:T(1024)(128)(4,1)} %bitcast.270), calls=%async_computation.14 | async-start | bytes 8388608
  342.9 11.8 %slice-start.3 = ((s8[6291456]{0:T(1024)(128)(4,1)}), s8[2097152]{0:T(1024)(128)(4,1)S(1)}, s32[]{:S(2)}) async-start(s8[6291456]{0:T(1024)(128)(4,1)} %bitcast.270), calls=%async_computation.15 | async-start | bytes 4194304
  342.9 11.8 %copy-start.16 = (bf16[16,4,32,384]{3,0,1,2:T(8,128)(2,1)S(1)}, bf16[16,4,32,384]{3,0,1,2:T(8,128)(2,1)}, u32[]{:S(2)}) copy-start(bf16[16,4,32,384]{3,0,1,2:T(8,128)(2,1)} %copy-done.15) | copy-start | bytes 4718596
  342.9 11.8 %copy-start.23 = (f32[32,64,256]{2,1,0:T(8,128)S(1)}, f32[32,64,256]{2,1,0:T(8,128)}, u32[]{:S(2)}) copy-start(f32[32,64,256]{2,1,0:T(8,128)} %fusion.112) | copy-start | bytes 6291460
  342.9 36.5 %collective-permute-start.3 = (bf16[2048,384]{1,0:T(8,128)(2,1)}, bf16[2048,384]{1,0:T(8,128)(2,1)}, u32[]{:S(2)}, u32[]{:S(2)}) collective-permute-start(bf16[2048,384]{1,0:T(8,128)(2,1)} %fusion.46), channel_id=1, source_target_pairs={{0,28},{4,0},{8,4},{12,8},{16,12},{20,16},{24,20},{28,24},{1,29},{... | collective-permute-start | bytes 4718600 | tf_op jit(solution)/shard_map/ppermute | solution.py:9
  354.8 2.6 copy-start.6
  354.8 2.6 copy-start.31

commit v4 on v3

--- a/solution.py
+++ b/solution.py
@@ -21,17 +21,48 @@
     return lax.all_to_all(value, "tensor", split_axis=0, concat_axis=1, tiled=True)
 
 
-def front(narrow_in, first_up, second_up, first_down):
+def swapped(pieces):
+    count = lax.axis_size("tensor")
+    me = lax.axis_index("tensor")
+    arrived = []
+    for shift in range(count):
+        piece = lax.dynamic_index_in_dim(pieces, (me + shift) % count, 0, keepdims=False)
+        if shift:
+            piece = lax.ppermute(
+                piece, "tensor", [(i, (i + shift) % count) for i in range(count)]
+            )
+        arrived.append(piece)
+    order = (me - jnp.arange(count)) % count
+    return jnp.take(jnp.stack(arrived), order, axis=0)
+
+
+def to_columns_by_permutes(value):
+    count = lax.axis_size("tensor")
+    pieces = value.reshape(value.shape[0], count, -1, value.shape[2]).swapaxes(0, 1)
+    out = swapped(pieces)
+    return out.reshape((-1,) + out.shape[2:])
+
+
+def to_rows_by_permutes(value):
+    count = lax.axis_size("tensor")
+    out = swapped(value.reshape((count, -1) + value.shape[1:]))
+    out = out.swapaxes(0, 1)
+    return out.reshape(out.shape[0], -1, out.shape[3])
+
+
+def front(narrow_in, first_up, second_up, first_down, columns=None, rows=None):
+    columns = columns or to_columns
+    rows = rows or to_rows
     first_out = jnp.einsum(
         "njr,nji->nir", narrow_in, first_up, preferred_element_type=jnp.float32
     ).astype(jnp.bfloat16)
-    spread = to_columns(first_out)
+    spread = columns(first_out)
     hidden_pre = jnp.einsum("nir,inf->ifr", spread, second_up, preferred_element_type=jnp.float32)
     hidden = smooth(hidden_pre).astype(jnp.bfloat16)
     local_fold = jnp.einsum(
         "ifr,inf->nir", hidden, first_down, preferred_element_type=jnp.float32
     ).astype(jnp.bfloat16)
-    folded = to_rows(local_fold)
+    folded = rows(local_fold)
     return (spread, hidden_pre, hidden, folded)
 
 
@@ -93,7 +124,10 @@
     near_activation = shifted(sent, "pipe", 1)
 
     stored = stash[0, 0].reshape(blocks, width, rows)
-    behind = front(stored, up_first, up_second, down_first)
+    behind = front(
+        stored, up_first, up_second, down_first,
+        to_columns_by_permutes, to_rows_by_permutes,
+    )
     grad_step, totals = backward(
         stored, cotangent, up_first, up_second, down_first, down_second, behind
     )
@@ -109,7 +143,10 @@
     last_activation = shifted(sent, "pipe", 1)
 
     stored = stash[1, 0].reshape(blocks, width, rows)
-    behind = front(stored, up_first, up_second, down_first)
+    behind = front(
+        stored, up_first, up_second, down_first,
+        to_columns_by_permutes, to_rows_by_permutes,
+    )
     grad_step, terms, last_activation = backward(
         stored, near_cotangent, up_first, up_second, down_first, down_second, behind,
         last_activation,

time: 389 us -> 385 us (0.990)
  waiting for transfers between devices: 130 us -> 100 us
  other arithmetic: 18.6 us -> 35.2 us
  local copies, waits for them, and re-layouts: 64.9 us -> 71.7 us
    all_to_all x6 -> x4, waiting for transfers between devices: 59.6 us -> 20.3 us  [to_columns(): lax.all_to_all(value, 'tensor', split_axis=1, concat_axis=0, tiled=True)]
    ppermute x0 -> x12, waiting for transfers between devices: none -> 27 us  [swapped(): lax.ppermute(piece, 'tensor', [(i, (i + shift) % count) for i in range(co...]
    all_to_all x6 -> x4, waiting for transfers between devices: 29.5 us -> 15.6 us  [to_rows(): lax.all_to_all(value, 'tensor', split_axis=0, concat_axis=1, tiled=True)]
    gather x0 -> x4, local copies, waits for them, and re-layouts: none -> 13.4 us  [swapped(): return jnp.take(jnp.stack(arrived), order, axis=0)]
    ppermute x0 -> x12, starting transfers between devices: none -> 12 us  [swapped(): lax.ppermute(piece, 'tensor', [(i, (i + shift) % count) for i in range(co...]
    another operation x0 -> x4, other arithmetic: none -> 10.5 us  [swapped(): return jnp.take(jnp.stack(arrived), order, axis=0)]
    all_to_all x6 -> x4, starting transfers between devices: 26.9 us -> 17.6 us  [to_columns(): lax.all_to_all(value, 'tensor', split_axis=1, concat_axis=0, tiled=True)]
    all_to_all x6 -> x4, starting transfers between devices: 25.7 us -> 17.9 us  [to_rows(): lax.all_to_all(value, 'tensor', split_axis=0, concat_axis=1, tiled=True)]
  transfers between devices with their start and end apart: 16 -> 24, of which waited for: 14 -> 12; matrix products, arithmetic and copies ran while one was open for 44% -> 53% of each run, Pallas kernels for 0% -> 0%
where the time goes in v4:
time: 385 us; the launch traced here: 377 us
  matrix products  112 us (29%)
  waiting for transfers between devices  100 us (26%)
  local copies, waits for them, and re-layouts  71.7 us (19%)
  starting transfers between devices  56.2 us (15%)
  other arithmetic  35.2 us (9%)
    ppermute x4, waiting for transfers between devices, shifted(): lax.ppermute(value, axis, [(i, (i + by) % count) for i in range(count)])  37.5 us
    ppermute x12, waiting for transfers between devices, swapped(): lax.ppermute(piece, 'tensor', [(i, (i + shift) % count) for i in range(co...  27 us
    dot_general x4, matrix products, front(): jnp.einsum('ifr,inf->nir', hidden, first_down, preferred_element_type=jnp...  26.4 us
    dot_general x2, matrix products, backward(): jnp.einsum('nir,inf->ifr', grad_folded, first_down, preferred_element_typ...  25.5 us
    all_to_all x4, waiting for transfers between devices, to_columns(): lax.all_to_all(value, 'tensor', split_axis=1, concat_axis=0, tiled=True)  20.3 us
    all_to_all x4, starting transfers between devices, to_rows(): lax.all_to_all(value, 'tensor', split_axis=0, concat_axis=1, tiled=True)  17.9 us
    all_to_all x4, starting transfers between devices, to_columns(): lax.all_to_all(value, 'tensor', split_axis=1, concat_axis=0, tiled=True)  17.6 us
    dot_general x2, matrix products, front(): jnp.einsum('nir,inf->ifr', spread, second_up, preferred_element_type=jnp....  16.4 us
  transfers between devices with their start and end apart: 24, of which 12 were waited for; matrix products, arithmetic and copies ran while one was open for 53% of the time, Pallas kernels for 0%

profile of v4, /device:TPU:0, one launch (start us, length us, event | category | flops | bytes accessed | tf_op | source)
XLA Modules:
  0.0 377.2 jit_solution(490159385808464334)
XLA Ops:
  0.7 3.4 fusion.114
  6.8 2.5 collective-permute-start.6
  14.7 2.1 copy.82
  16.8 4.3 %all-to-all-start.2 = ((bf16[16,128,384]{2,0,1:T(8,128)(2,1)}), bf16[16,128,384]{2,0,1:T(8,128)(2,1)}, u32[]{:S(2)}, u32[]{:S(2)}) async-start(bf16[16,128,384]{2,0,1:T(8,128)(2,1)} %copy.82), calls=%async_computation.2 | async-start | bytes 3145728 | tf_op jit(solution)/shard_map/all_to_all | solution.py:17
  21.2 2.1 convert_element_type.112
  25.7 2.1 copy.76
  27.8 2.6 pad_maximum_fusion.1
  30.4 3.4 gather_fusion.1
  36.4 24.3 %collective-permute-done.3 = bf16[16,32,384]{2,1,0:T(8,128)(2,1)} collective-permute-done((bf16[16,32,384]{2,1,0:T(8,128)(2,1)}, bf16[16,32,384]{2,1,0:T(8,128)(2,1)}, u32[]{:S(2)}, u32[]{:S(2)}) %collective-permute-start.3) | collective-permute-done | bytes 393248 | tf_op jit(solution)/shard_map/ppermute | solution.py:31
  60.7 2.6 pad_maximum_fusion
  63.3 3.3 gather_fusion
  66.7 3.9 %broadcast_select_fusion.1 = (bf16[4,16,32,384]{3,2,1,0:T(8,128)(2,1)}, bf16[4,16,32,384]{3,2,1,0:T(8,128)(2,1)}) fusion(bf16[4,16,32,384]{3,2,1,0:T(8,128)(2,1)} %gather_fusion, pred[4]{0:T(512)(128)(4,1)S(1)} %compare_and_fusion, bf16[4,16,32,384]{3,2,1,0:T(8,128)(2,1)} %gather_fusion.1), kind=kLoop, calls=%fused_computation.89 | loop fusion | flops 1572864 | bytes 6291460 | tf_op jit(solution)/shard_map/jit(_take)/select_n | solution.py:36
  70.6 4.6 %all-to-all-start = ((bf16[16,128,384]{2,0,1:T(8,128)(2,1)}), bf16[16,128,384]{2,0,1:T(8,128)(2,1)}, u32[]{:S(2)}, u32[]{:S(2)}) async-start(bf16[16,128,384]{2,0,1:T(8,128)(2,1)} %copy.76), calls=%async_computation | async-start | bytes 3145728 | tf_op jit(solution)/shard_map/all_to_all | solution.py:17
  75.2 10.0 %fusion.34 = (bf16[32,256,384]{1,2,0:T(8,128)(2,1)S(1)}, f32[32,384,256]{2,1,0:T(8,128)}) fusion(bf16[1,32,64,256]{3,2,1,0:T(8,128)(2,1)S(1)} %copy-done, bf16[64,32,384]{2,1,0:T(8,128)(2,1)} %bitcast.316), kind=kOutput, calls=%fused_computation.49 | convolution fusion | flops 430964736 | bytes 21495808 | tf_op jit(solution)/shard_map/nir,inf->ifr/dot_general | solution.py:60
  85.2 2.0 convolution_convert_fusion.7
  92.3 2.9 copy.83
  95.8 2.8 copy.77
  98.6 7.6 %fusion.59 = bf16[64,32,384]{2,0,1:T(8,128)(2,1)} fusion(bf16[64,32,384]{2,0,1:T(8,128)(2,1)} %bitcast.331, bf16[1,32,64,256]{3,2,1,0:T(8,128)(2,1)} %param.14, bf16[1,32,64,256]{3,2,1,0:T(8,128)(2,1)S(1)} %copy-done), kind=kOutput, calls=%fused_computation.91 | convolution fusion | flops 834404352 | bytes 5242880 | tf_op jit(solution)/shard_map/ifr,inf->nir/dot_general | solution.py:62
  106.2 3.5 copy.79
  109.7 4.7 %all-to-all-start.1 = ((bf16[64,32,384]{2,1,0:T(8,128)(2,1)}), bf16[64,32,384]{2,1,0:T(8,128)(2,1)}, u32[]{:S(2)}, u32[]{:S(2)}) async-start(bf16[64,32,384]{2,1,0:T(8,128)(2,1)} %copy.79), calls=%async_computation.1 | async-start | bytes 3145728 | tf_op jit(solution)/shard_map/all_to_all | solution.py:21
  114.4 13.3 %fusion.6 = bf16[32,256,384]{1,2,0:T(8,128)(2,1)S(1)} fusion(f32[32,384,256]{2,1,0:T(8,128)} %get-tuple-element.56, bf16[64,32,384]{2,0,1:T(8,128)(2,1)} %bitcast.318, bf16[1,32,64,256]{3,2,1,0:T(8,128)(2,1)} %param.14), kind=kOutput, calls=%fused_computation.16 | convolution fusion | flops 465567744 | bytes 21495808 | tf_op jit(solution)/shard_map/nir,inf->ifr/dot_general | solution.py:82
  127.8 2.1 fusion.62
  130.5 2.1 copy.87
  132.5 2.0 all-to-all-done.1
  134.6 4.3 %all-to-all-start.3 = ((bf16[64,32,384]{2,1,0:T(8,128)(2,1)}), bf16[64,32,384]{2,1,0:T(8,128)(2,1)}, u32[]{:S(2)}, u32[]{:S(2)}) async-start(bf16[64,32,384]{2,1,0:T(8,128)(2,1)} %copy.87), calls=%async_computation.3 | async-start | bytes 3145728 | tf_op jit(solution)/shard_map/all_to_all | solution.py:21
  145.7 6.4 %fusion.67 = f32[32,384,256]{2,1,0:T(8,128)} fusion(bf16[64,32,384]{2,1,0:T(8,128)(2,1)S(1)} %bitcast.314, bf16[1,32,64,256]{3,2,1,0:T(8,128)(2,1)S(1)} %copy-done), kind=kOutput, calls=%fused_computation.97 | convolution fusion | flops 402653184 | bytes 15204352 | tf_op jit(solution)/shard_map/nir,inf->ifr/dot_general | solution.py:60
  152.2 6.9 %all-to-all-done.3 = bf16[64,32,384]{2,1,0:T(8,128)(2,1)} async-done(((bf16[64,32,384]{2,1,0:T(8,128)(2,1)}), bf16[64,32,384]{2,1,0:T(8,128)(2,1)}, u32[]{:S(2)}, u32[]{:S(2)}) %all-to-all-start.3) | async-done | bytes 1572896 | tf_op jit(solution)/shard_map/all_to_all | solution.py:21
  165.2 18.9 %collective-permute-done = bf16[2048,384]{1,0:T(8,128)(2,1)} collective-permute-done((bf16[2048,384]{1,0:T(8,128)(2,1)}, bf16[2048,384]{1,0:T(8,128)(2,1)}, u32[]{:S(2)}, u32[]{:S(2)}) %collective-permute-start) | collective-permute-done | bytes 1572896 | tf_op jit(solution)/shard_map/ppermute | solution.py:9
  184.1 3.2 fusion.65
  187.3 2.9 copy.99
  190.2 4.3 %all-to-all-start.6 = ((bf16[16,128,384]{2,0,1:T(8,128)(2,1)}), bf16[16,128,384]{2,0,1:T(8,128)(2,1)}, u32[]{:S(2)}, u32[]{:S(2)}) async-start(bf16[16,128,384]{2,0,1:T(8,128)(2,1)} %copy.99), calls=%async_computation.6 | async-start | bytes 3145728 | tf_op jit(solution)/shard_map/all_to_all | solution.py:17
  194.5 9.1 %convolution_convert_fusion.6 = bf16[32,384,64]{1,2,0:T(8,128)(2,1)S(1)} fusion(bf16[1,32,64,256]{3,2,1,0:T(8,128)(2,1)} %param.14, f32[32,384,256]{2,1,0:T(8,128)} %fusion.67), kind=kOutput, calls=%fused_computation.76 | convolution fusion | flops 431751168 | bytes 15204352 | tf_op jit(solution)/shard_map/ifr,inf->nir/dot_general | solution.py:62
  206.6 8.5 %all-to-all-done.6 = bf16[16,128,384]{2,0,1:T(8,128)(2,1)} async-done(((bf16[16,128,384]{2,0,1:T(8,128)(2,1)}), bf16[16,128,384]{2,0,1:T(8,128)(2,1)}, u32[]{:S(2)}, u32[]{:S(2)}) %all-to-all-start.6) | async-done | bytes 1572896 | tf_op jit(solution)/shard_map/all_to_all | solution.py:17
  215.1 2.8 copy.101
  220.0 7.6 %fusion.56 = bf16[64,32,384]{2,0,1:T(8,128)(2,1)} fusion(bf16[64,32,384]{2,0,1:T(8,128)(2,1)} %bitcast.330, bf16[1,32,64,256]{3,2,1,0:T(8,128)(2,1)} %param.14, bf16[1,32,64,256]{3,2,1,0:T(8,128)(2,1)S(1)} %copy-done), kind=kOutput, calls=%fused_computation.90 | convolution fusion | flops 834404352 | bytes 5242880 | tf_op jit(solution)/shard_map/ifr,inf->nir/dot_general | solution.py:62
  227.6 3.5 copy.103
  231.1 4.3 %all-to-all-start.7 = ((bf16[64,32,384]{2,1,0:T(8,128)(2,1)}), bf16[64,32,384]{2,1,0:T(8,128)(2,1)}, u32[]{:S(2)}, u32[]{:S(2)}) async-start(bf16[64,32,384]{2,1,0:T(8,128)(2,1)} %copy.103), calls=%async_computation.7 | async-start | bytes 3145728 | tf_op jit(solution)/shard_map/all_to_all | solution.py:21
  235.5 2.6 pad_maximum_fusion.2
  238.1 3.3 gather_fusion.2
  241.4 2.6 pad_maximum_fusion.3
  244.0 3.3 gather_fusion.3
  247.4 2.3 select_bitcast_fusion
  252.7 2.3 collective-permute-done.4
  255.0 3.2 fusion.64
  258.2 3.0 copy.90
  261.1 4.4 %all-to-all-start.4 = ((bf16[16,128,384]{2,0,1:T(8,128)(2,1)}), bf16[16,128,384]{2,0,1:T(8,128)(2,1)}, u32[]{:S(2)}, u32[]{:S(2)}) async-start(bf16[16,128,384]{2,0,1:T(8,128)(2,1)} %copy.90), calls=%async_computation.4 | async-start | bytes 3145728 | tf_op jit(solution)/shard_map/all_to_all | solution.py:17
  265.5 3.2 fusion.117
  271.0 3.3 fusion.47
  274.5 11.1 %all-to-all-done.4 = bf16[16,128,384]{2,0,1:T(8,128)(2,1)} async-done(((bf16[16,128,384]{2,0,1:T(8,128)(2,1)}), bf16[16,128,384]{2,0,1:T(8,128)(2,1)}, u32[]{:S(2)}, u32[]{:S(2)}) %all-to-all-start.4) | async-done | bytes 1572896 | tf_op jit(solution)/shard_map/all_to_all | solution.py:17
  287.5 12.2 %fusion.13 = bf16[32,256,384]{1,2,0:T(8,128)(2,1)S(1)} fusion(f32[32,384,256]{2,1,0:T(8,128)} %fusion.67, bf16[64,32,384]{2,0,1:T(8,128)(2,1)S(1)} %bitcast.328, bf16[1,32,64,256]{3,2,1,0:T(8,128)(2,1)S(1)} %copy-done.29), kind=kOutput, calls=%fused_computation.23 | convolution fusion | flops 465567744 | bytes 21495808 | tf_op jit(solution)/shard_map/nir,inf->ifr/dot_general | solution.py:82
  299.7 2.1 fusion.63
  302.4 2.1 copy.96
  304.5 4.5 %all-to-all-start.5 = ((bf16[64,32,384]{2,1,0:T(8,128)(2,1)}), bf16[64,32,384]{2,1,0:T(8,128)(2,1)}, u32[]{:S(2)}, u32[]{:S(2)}) async-start(bf16[64,32,384]{2,1,0:T(8,128)(2,1)} %copy.96), calls=%async_computation.5 | async-start | bytes 3145728 | tf_op jit(solution)/shard_map/all_to_all | solution.py:21
  309.0 6.0 %fusion.116 = f32[32,64,256]{2,1,0:T(8,128)} fusion(bf16[64,32,384]{2,0,1:T(8,128)(2,1)} %bitcast.319, bf16[32,256,384]{1,2,0:T(8,128)(2,1)} %copy-done.1), kind=kOutput, calls=%fused_computation.166 | convolution fusion | flops 402653184 | bytes 9961472 | tf_op jit(solution)/shard_map/ifr,nir->inf/dot_general | solution.py:79
  315.0 2.6 fusion.69
  319.3 3.2 fusion.73
  322.5 6.7 %all-to-all-done.5 = bf16[64,32,384]{2,1,0:T(8,128)(2,1)} async-done(((bf16[64,32,384]{2,1,0:T(8,128)(2,1)}), bf16[64,32,384]{2,1,0:T(8,128)(2,1)}, u32[]{:S(2)}, u32[]{:S(2)}) %all-to-all-start.5) | async-done | bytes 1572896 | tf_op jit(solution)/shard_map/all_to_all | solution.py:21
  331.5 3.5 fusion.46
  334.9 4.7 %collective-permute-start.9 = (bf16[2048,384]{1,0:T(8,128)(2,1)}, bf16[2048,384]{1,0:T(8,128)(2,1)}, u32[]{:S(2)}, u32[]{:S(2)}) collective-permute-start(bf16[2048,384]{1,0:T(8,128)(2,1)} %fusion.46), channel_id=1, source_target_pairs={{0,28},{4,0},{8,4},{12,8},{16,12},{20,16},{24,20},{28,24},{1,29},{... | collective-permute-start | bytes 4718600 | tf_op jit(solution)/shard_map/ppermute | solution.py:9
  339.6 9.3 %add_bitcast_fusion = f32[1,32,64,256]{3,2,1,0:T(8,128)} fusion(f32[32,64,256]{2,1,0:T(8,128)S(1)} %copy-done.24, bf16[64,32,384]{2,0,1:T(8,128)(2,1)S(1)} %bitcast.329, f32[32,384,256]{2,1,0:T(8,128)} %fusion.67), kind=kOutput, calls=%fused_computation.66 | convolution fusion | flops 431489024 | bytes 18350080 | tf_op jit(solution)/shard_map/ifr,nir->inf/dot_general | solution.py:79
  349.0 2.7 add_bitcast_fusion.1
  353.8 3.3 bitcast_convert_fusion.1
  357.0 16.4 %collective-permute-done.9 = bf16[2048,384]{1,0:T(8,128)(2,1)} collective-permute-done((bf16[2048,384]{1,0:T(8,128)(2,1)}, bf16[2048,384]{1,0:T(8,128)(2,1)}, u32[]{:S(2)}, u32[]{:S(2)}) %collective-permute-start.9) | collective-permute-done | bytes 1572896 | tf_op jit(solution)/shard_map/ppermute | solution.py:9
  373.4 3.3 bitcast_convert_fusion
  (127 shorter events, 51.5 us)
Async XLA Ops:
  0.6 74.5 %copy-start = (bf16[1,32,64,256]{3,2,1,0:T(8,128)(2,1)S(1)}, bf16[1,32,64,256]{3,2,1,0:T(8,128)(2,1)}, u32[]{:S(2)}) copy-start(bf16[1,32,64,256]{3,2,1,0:T(8,128)(2,1)} %param.13) | copy-start | bytes 3145732
  0.7 3.5 copy-start.4
  4.2 1.2 copy-start.6
  5.3 5.5 %copy-start.8 = (bf16[1,1,2048,384]{3,2,1,0:T(8,128)(2,1)S(1)}, bf16[1,1,2048,384]{3,2,1,0:T(8,128)(2,1)}, u32[]{:S(2)}) copy-start(bf16[1,1,2048,384]{3,2,1,0:T(8,128)(2,1)} %get-tuple-element.33) | copy-start | bytes 4718596
  6.4 17.5 %collective-permute-start.5 = (bf16[16,32,384]{2,1,0:T(8,128)(2,1)}, bf16[16,32,384]{2,1,0:T(8,128)(2,1)}, u32[]{:S(2)}, u32[]{:S(2)}) collective-permute-start(bf16[16,32,384]{2,1,0:T(8,128)(2,1)} %get-tuple-element.50), channel_id=1, source_target_pairs={{0,1},{1,2},{2,3},{3,0},{4,5},{5,6},{6,7},{7,4},{8,9},{9,10},{10,1... | collective-permute-start | bytes 1179656 | tf_op jit(solution)/shard_map/ppermute | solution.py:31
  6.8 20.9 %collective-permute-start.6 = (bf16[16,32,384]{2,1,0:T(8,128)(2,1)}, bf16[16,32,384]{2,1,0:T(8,128)(2,1)}, u32[]{:S(2)}, u32[]{:S(2)}) collective-permute-start(bf16[16,32,384]{2,1,0:T(8,128)(2,1)} %get-tuple-element.49), channel_id=1, source_target_pairs={{0,2},{1,3},{2,0},{3,1},{4,6},{5,7},{6,4},{7,5},{8,10},{9,11},{10,... | collective-permute-start | bytes 1179656 | tf_op jit(solution)/shard_map/ppermute | solution.py:31
  9.4 18.4 %collective-permute-start.7 = (bf16[16,32,384]{2,1,0:T(8,128)(2,1)}, bf16[16,32,384]{2,1,0:T(8,128)(2,1)}, u32[]{:S(2)}, u32[]{:S(2)}) collective-permute-start(bf16[16,32,384]{2,1,0:T(8,128)(2,1)} %get-tuple-element.48), channel_id=1, source_target_pairs={{0,3},{1,0},{2,1},{3,2},{4,7},{5,4},{6,5},{7,6},{8,11},{9,8},{10,9... | collective-permute-start | bytes 1179656 | tf_op jit(solution)/shard_map/ppermute | solution.py:31
  11.4 2.5 copy-start.15
  12.7 22.1 %collective-permute-start.1 = (bf16[16,32,384]{2,1,0:T(8,128)(2,1)}, bf16[16,32,384]{2,1,0:T(8,128)(2,1)}, u32[]{:S(2)}, u32[]{:S(2)}) collective-permute-start(bf16[16,32,384]{2,1,0:T(8,128)(2,1)} %get-tuple-element.46), channel_id=1, source_target_pairs={{0,1},{1,2},{2,3},{3,0},{4,5},{5,6},{6,7},{7,4},{8,9},{9,10},{10,1... | collective-permute-start | bytes 1179656 | tf_op jit(solution)/shard_map/ppermute | solution.py:31
  12.7 1.5 copy-start.17
  12.7 23.8 %collective-permute-start.2 = (bf16[16,32,384]{2,1,0:T(8,128)(2,1)}, bf16[16,32,384]{2,1,0:T(8,128)(2,1)}, u32[]{:S(2)}, u32[]{:S(2)}) collective-permute-start(bf16[16,32,384]{2,1,0:T(8,128)(2,1)} %get-tuple-element.45), channel_id=1, source_target_pairs={{0,2},{1,3},{2,0},{3,1},{4,6},{5,7},{6,4},{7,5},{8,10},{9,11},{10,... | collective-permute-start | bytes 1179656 | tf_op jit(solution)/shard_map/ppermute | solution.py:31
  16.8 53.8 %all-to-all-start.2 = ((bf16[16,128,384]{2,0,1:T(8,128)(2,1)}), bf16[16,128,384]{2,0,1:T(8,128)(2,1)}, u32[]{:S(2)}, u32[]{:S(2)}) async-start(bf16[16,128,384]{2,0,1:T(8,128)(2,1)} %copy.82), calls=%async_computation.2 | async-start | bytes 3145728 | tf_op jit(solution)/shard_map/all_to_all | solution.py:17
  23.9 36.8 %collective-permute-start.3 = (bf16[16,32,384]{2,1,0:T(8,128)(2,1)}, bf16[16,32,384]{2,1,0:T(8,128)(2,1)}, u32[]{:S(2)}, u32[]{:S(2)}) collective-permute-start(bf16[16,32,384]{2,1,0:T(8,128)(2,1)} %get-tuple-element.44), channel_id=1, source_target_pairs={{0,3},{1,0},{2,1},{3,2},{4,7},{5,4},{6,5},{7,6},{8,11},{9,8},{10,9... | collective-permute-start | bytes 1179656 | tf_op jit(solution)/shard_map/ppermute | solution.py:31
  30.4 30.3 %copy-start.27 = (bf16[1,16,32,384]{3,2,1,0:T(8,128)(2,1)S(1)}, bf16[1,16,32,384]{3,2,1,0:T(8,128)(2,1)}, u32[]{:S(2)}) copy-start(bf16[1,16,32,384]{3,2,1,0:T(8,128)(2,1)} %get-tuple-element.43) | copy-start | bytes 1179652
  70.6 25.2 %all-to-all-start = ((bf16[16,128,384]{2,0,1:T(8,128)(2,1)}), bf16[16,128,384]{2,0,1:T(8,128)(2,1)}, u32[]{:S(2)}, u32[]{:S(2)}) async-start(bf16[16,128,384]{2,0,1:T(8,128)(2,1)} %copy.76), calls=%async_computation | async-start | bytes 3145728 | tf_op jit(solution)/shard_map/all_to_all | solution.py:17
  75.2 10.0 %copy-start.28 = (bf16[1,32,64,256]{3,2,1,0:T(8,128)(2,1)S(1)}, bf16[1,32,64,256]{3,2,1,0:T(8,128)(2,1)}, u32[]{:S(2)}) copy-start(bf16[1,32,64,256]{3,2,1,0:T(8,128)(2,1)} %param.14) | copy-start | bytes 3145732
  85.2 2.6 copy-start.1
  88.8 129.2 %collective-permute-start.10 = (bf16[16,32,384]{2,0,1:T(8,128)(2,1)}, bf16[16,32,384]{2,0,1:T(8,128)(2,1)}, u32[]{:S(2)}, u32[]{:S(2)}) collective-permute-start(bf16[16,32,384]{2,0,1:T(8,128)(2,1)} %get-tuple-element.42), channel_id=1, source_target_pairs={{0,1},{1,2},{2,3},{3,0},{4,5},{5,6},{6,7},{7,4},{8,9},{9,10},{10,1... | collective-permute-start | bytes 1179656 | tf_op jit(solution)/shard_map/ppermute | solution.py:31
  89.3 128.7 %collective-permute-start.11 = (bf16[16,32,384]{2,0,1:T(8,128)(2,1)}, bf16[16,32,384]{2,0,1:T(8,128)(2,1)}, u32[]{:S(2)}, u32[]{:S(2)}) collective-permute-start(bf16[16,32,384]{2,0,1:T(8,128)(2,1)} %get-tuple-element.41), channel_id=1, source_target_pairs={{0,2},{1,3},{2,0},{3,1},{4,6},{5,7},{6,4},{7,5},{8,10},{9,11},{10,... | collective-permute-start | bytes 1179656 | tf_op jit(solution)/shard_map/ppermute | solution.py:31
  91.1 144.4 %collective-permute-start.12 = (bf16[16,32,384]{2,0,1:T(8,128)(2,1)}, bf16[16,32,384]{2,0,1:T(8,128)(2,1)}, u32[]{:S(2)}, u32[]{:S(2)}) collective-permute-start(bf16[16,32,384]{2,0,1:T(8,128)(2,1)} %get-tuple-element.40), channel_id=1, source_target_pairs={{0,3},{1,0},{2,1},{3,2},{4,7},{5,4},{6,5},{7,6},{8,11},{9,8},{10,9... | collective-permute-start | bytes 1179656 | tf_op jit(solution)/shard_map/ppermute | solution.py:31
  109.7 24.9 %all-to-all-start.1 = ((bf16[64,32,384]{2,1,0:T(8,128)(2,1)}), bf16[64,32,384]{2,1,0:T(8,128)(2,1)}, u32[]{:S(2)}, u32[]{:S(2)}) async-start(bf16[64,32,384]{2,1,0:T(8,128)(2,1)} %copy.79), calls=%async_computation.1 | async-start | bytes 3145728 | tf_op jit(solution)/shard_map/all_to_all | solution.py:21
  127.8 2.7 copy-start.2
  134.6 24.5 %all-to-all-start.3 = ((bf16[64,32,384]{2,1,0:T(8,128)(2,1)}), bf16[64,32,384]{2,1,0:T(8,128)(2,1)}, u32[]{:S(2)}, u32[]{:S(2)}) async-start(bf16[64,32,384]{2,1,0:T(8,128)(2,1)} %copy.87), calls=%async_computation.3 | async-start | bytes 3145728 | tf_op jit(solution)/shard_map/all_to_all | solution.py:21
  138.9 1.7 copy-start.18
  140.7 1.9 copy-start.14
  142.6 3.2 copy-start.12
  144.1 40.0 %collective-permute-start = (bf16[2048,384]{1,0:T(8,128)(2,1)}, bf16[2048,384]{1,0:T(8,128)(2,1)}, u32[]{:S(2)}, u32[]{:S(2)}) collective-permute-start(bf16[2048,384]{1,0:T(8,128)(2,1)} %fusion.49), channel_id=1, source_target_pairs={{0,4},{4,8},{8,12},{12,16},{16,20},{20,24},{24,28},{28,0},{1,5},{5... | collective-permute-start | bytes 4718600 | tf_op jit(solution)/shard_map/ppermute | solution.py:9
  160.7 1.1 copy-start.10
  161.9 1.9 copy-start.16
  190.2 25.0 %all-to-all-start.6 = ((bf16[16,128,384]{2,0,1:T(8,128)(2,1)}), bf16[16,128,384]{2,0,1:T(8,128)(2,1)}, u32[]{:S(2)}, u32[]{:S(2)}) async-start(bf16[16,128,384]{2,0,1:T(8,128)(2,1)} %copy.99), calls=%async_computation.6 | async-start | bytes 3145728 | tf_op jit(solution)/shard_map/all_to_all | solution.py:17
  204.7 36.7 %collective-permute-start.14 = (bf16[16,32,384]{2,0,1:T(8,128)(2,1)}, bf16[16,32,384]{2,0,1:T(8,128)(2,1)}, u32[]{:S(2)}, u32[]{:S(2)}) collective-permute-start(bf16[16,32,384]{2,0,1:T(8,128)(2,1)} %get-tuple-element.37), channel_id=1, source_target_pairs={{0,2},{1,3},{2,0},{3,1},{4,6},{5,7},{6,4},{7,5},{8,10},{9,11},{10,... | collective-permute-start | bytes 1179656 | tf_op jit(solution)/shard_map/ppermute | solution.py:31
  206.6 34.8 %collective-permute-start.15 = (bf16[16,32,384]{2,0,1:T(8,128)(2,1)}, bf16[16,32,384]{2,0,1:T(8,128)(2,1)}, u32[]{:S(2)}, u32[]{:S(2)}) collective-permute-start(bf16[16,32,384]{2,0,1:T(8,128)(2,1)} %get-tuple-element.36), channel_id=1, source_target_pairs={{0,3},{1,0},{2,1},{3,2},{4,7},{5,4},{6,5},{7,6},{8,11},{9,8},{10,9... | collective-permute-start | bytes 1179656 | tf_op jit(solution)/shard_map/ppermute | solution.py:31
  218.0 23.4 %collective-permute-start.13 = (bf16[16,32,384]{2,0,1:T(8,128)(2,1)}, bf16[16,32,384]{2,0,1:T(8,128)(2,1)}, u32[]{:S(2)}, u32[]{:S(2)}) collective-permute-start(bf16[16,32,384]{2,0,1:T(8,128)(2,1)} %get-tuple-element.38), channel_id=1, source_target_pairs={{0,1},{1,2},{2,3},{3,0},{4,5},{5,6},{6,7},{7,4},{8,9},{9,10},{10,1... | collective-permute-start | bytes 1179656 | tf_op jit(solution)/shard_map/ppermute | solution.py:31
  218.0 37.0 %collective-permute-start.4 = (bf16[2048,384]{1,0:T(8,128)(2,1)}, bf16[2048,384]{1,0:T(8,128)(2,1)}, u32[]{:S(2)}, u32[]{:S(2)}) collective-permute-start(bf16[2048,384]{1,0:T(8,128)(2,1)} %fusion.48), channel_id=1, source_target_pairs={{0,28},{4,0},{8,4},{12,8},{16,12},{20,16},{24,20},{28,24},{1,29},{... | collective-permute-start | bytes 4718600 | tf_op jit(solution)/shard_map/ppermute | solution.py:9
  231.1 30.1 %all-to-all-start.7 = ((bf16[64,32,384]{2,1,0:T(8,128)(2,1)}), bf16[64,32,384]{2,1,0:T(8,128)(2,1)}, u32[]{:S(2)}, u32[]{:S(2)}) async-start(bf16[64,32,384]{2,1,0:T(8,128)(2,1)} %copy.103), calls=%async_computation.7 | async-start | bytes 3145728 | tf_op jit(solution)/shard_map/all_to_all | solution.py:21
  251.2 3.8 %copy-start.19 = (bf16[1,16,128,128]{3,2,1,0:T(8,128)(2,1)S(1)}, bf16[1,16,128,128]{3,2,1,0:T(8,128)(2,1)}, u32[]{:S(2)}) copy-start(bf16[1,16,128,128]{3,2,1,0:T(8,128)(2,1)} %param.15) | copy-start | bytes 1572868
  261.1 24.5 %all-to-all-start.4 = ((bf16[16,128,384]{2,0,1:T(8,128)(2,1)}), bf16[16,128,384]{2,0,1:T(8,128)(2,1)}, u32[]{:S(2)}, u32[]{:S(2)}) async-start(bf16[16,128,384]{2,0,1:T(8,128)(2,1)} %copy.90), calls=%async_computation.4 | async-start | bytes 3145728 | tf_op jit(solution)/shard_map/all_to_all | solution.py:17
  274.3 56.6 %collective-permute-start.8 = (bf16[2048,384]{1,0:T(8,128)(2,1)}, bf16[2048,384]{1,0:T(8,128)(2,1)}, u32[]{:S(2)}, u32[]{:S(2)}) collective-permute-start(bf16[2048,384]{1,0:T(8,128)(2,1)} %fusion.47), channel_id=1, source_target_pairs={{0,4},{4,8},{8,12},{12,16},{16,20},{20,24},{24,28},{28,0},{1,5},{5... | collective-permute-start | bytes 4718600 | tf_op jit(solution)/shard_map/ppermute | solution.py:9
  285.7 1.8 copy-start.29
  287.5 12.2 %copy-start.25 = (bf16[4,16,32,384]{3,1,0,2:T(8,128)(2,1)}, bf16[4,16,32,384]{3,1,0,2:T(8,128)(2,1)S(1)}, u32[]{:S(2)}) copy-start(bf16[4,16,32,384]{3,1,0,2:T(8,128)(2,1)S(1)} %copy.92) | copy-start | bytes 4718596
  299.7 2.7 copy-start.3
  304.5 10.5 %slice-start = ((s8[6291456]{0:T(1024)(128)(4,1)}), s8[2097152]{0:T(1024)(128)(4,1)S(1)}, s32[]{:S(2)}) async-start(s8[6291456]{0:T(1024)(128)(4,1)} %bitcast.300), calls=%async_computation.8 | async-start | bytes 4194304
  304.5 24.6 %all-to-all-start.5 = ((bf16[64,32,384]{2,1,0:T(8,128)(2,1)}), bf16[64,32,384]{2,1,0:T(8,128)(2,1)}, u32[]{:S(2)}, u32[]{:S(2)}) async-start(bf16[64,32,384]{2,1,0:T(8,128)(2,1)} %copy.96), calls=%async_computation.5 | async-start | bytes 3145728 | tf_op jit(solution)/shard_map/all_to_all | solution.py:21
  309.0 6.0 %slice-start.1 = ((s8[6291456]{0:T(1024)(128)(4,1)}), s8[4194304]{0:T(1024)(128)(4,1)S(1)}, s32[]{:S(2)}) async-start(s8[6291456]{0:T(1024)(128)(4,1)} %bitcast.300), calls=%async_computation.9 | async-start | bytes 8388608
  309.0 6.0 %copy-start.21 = (bf16[4,16,32,384]{3,2,1,0:T(8,128)(2,1)S(1)}, bf16[4,16,32,384]{3,2,1,0:T(8,128)(2,1)}, u32[]{:S(2)}) copy-start(bf16[4,16,32,384]{3,2,1,0:T(8,128)(2,1)} %get-tuple-element.53) | copy-start | bytes 4718596
  315.0 2.6 copy-start.9
  315.0 2.6 copy-start.11
  317.6 1.4 copy-start.22
  317.6 1.7 copy-start.23
  329.1 1.7 copy-start.5
  330.8 8.8 %copy-start.26 = (bf16[4,16,32,384]{3,1,0,2:T(8,128)(2,1)S(1)}, bf16[4,16,32,384]{3,1,0,2:T(8,128)(2,1)}, u32[]{:S(2)}) copy-start(bf16[4,16,32,384]{3,1,0,2:T(8,128)(2,1)} %copy-done.25) | copy-start | bytes 4718596
  331.4 8.2 %copy-start.24 = (f32[32,64,256]{2,1,0:T(8,128)S(1)}, f32[32,64,256]{2,1,0:T(8,128)}, u32[]{:S(2)}) copy-start(f32[32,64,256]{2,1,0:T(8,128)} %fusion.116) | copy-start | bytes 6291460
  331.4 17.5 %slice-start.2 = ((s8[6291456]{0:T(1024)(128)(4,1)}), s8[4194304]{0:T(1024)(128)(4,1)S(1)}, s32[]{:S(2)}) async-start(s8[6291456]{0:T(1024)(128)(4,1)} %bitcast.302), calls=%async_computation.10 | async-start | bytes 8388608
  334.9 14.0 %slice-start.3 = ((s8[6291456]{0:T(1024)(128)(4,1)}), s8[2097152]{0:T(1024)(128)(4,1)S(1)}, s32[]{:S(2)}) async-start(s8[6291456]{0:T(1024)(128)(4,1)} %bitcast.302), calls=%async_computation.11 | async-start | bytes 4194304
  334.9 14.0 %copy-start.13 = (bf16[4,16,32,384]{3,2,1,0:T(8,128)(2,1)S(1)}, bf16[4,16,32,384]{3,2,1,0:T(8,128)(2,1)}, u32[]{:S(2)}) copy-start(bf16[4,16,32,384]{3,2,1,0:T(8,128)(2,1)} %get-tuple-element.54) | copy-start | bytes 4718596
  334.9 14.0 %copy-start.20 = (f32[32,64,256]{2,1,0:T(8,128)S(1)}, f32[32,64,256]{2,1,0:T(8,128)}, u32[]{:S(2)}) copy-start(f32[32,64,256]{2,1,0:T(8,128)} %fusion.69) | copy-start | bytes 6291460
  334.9 38.5 %collective-permute-start.9 = (bf16[2048,384]{1,0:T(8,128)(2,1)}, bf16[2048,384]{1,0:T(8,128)(2,1)}, u32[]{:S(2)}, u32[]{:S(2)}) collective-permute-start(bf16[2048,384]{1,0:T(8,128)(2,1)} %fusion.46), channel_id=1, source_target_pairs={{0,28},{4,0},{8,4},{12,8},{16,12},{20,16},{24,20},{28,24},{1,29},{... | collective-permute-start | bytes 4718600 | tf_op jit(solution)/shard_map/ppermute | solution.py:9
  349.0 2.7 copy-start.7

commit v5 on v4

--- a/solution.py
+++ b/solution.py
@@ -14,11 +14,11 @@
 
 
 def to_columns(value):
-    return lax.all_to_all(value, "tensor", split_axis=1, concat_axis=0, tiled=True)
+    return to_columns_by_permutes(value)
 
 
 def to_rows(value):
-    return lax.all_to_all(value, "tensor", split_axis=0, concat_axis=1, tiled=True)
+    return to_rows_by_permutes(value)
 
 
 def swapped(pieces):

time: 385 us -> 446 us (1.16)
  waiting for transfers between devices: 100 us -> 172 us
  matrix products: 112 us -> 90 us
  other arithmetic: 35.2 us -> 49.8 us
    ppermute x4, waiting for transfers between devices: 37.5 us -> 111 us  [shifted(): lax.ppermute(value, axis, [(i, (i + by) % count) for i in range(count)])]
    all_to_all x8 -> x0, waiting for transfers between devices: 35.8 us -> none  [the longest x4 20.3 us: to_columns(): lax.all_to_all(value, 'tensor', split_axis=1, concat_axis=0, tiled=True)]
    all_to_all x8 -> x0, starting transfers between devices: 35.5 us -> none  [the longest x4 17.9 us: to_rows(): lax.all_to_all(value, 'tensor', split_axis=0, concat_axis=1, tiled=True)]
    ppermute x12 -> x36, starting transfers between devices: 12 us -> 47.2 us  [swapped(): lax.ppermute(piece, 'tensor', [(i, (i + shift) % count) for i in range(co...]
    ppermute x12 -> x36, waiting for transfers between devices: 27 us -> 60.4 us  [swapped(): lax.ppermute(piece, 'tensor', [(i, (i + shift) % count) for i in range(co...]
    gather x4 -> x12, local copies, waits for them, and re-layouts: 13.4 us -> 34.6 us  [swapped(): return jnp.take(jnp.stack(arrived), order, axis=0)]
    convert_element_type x8 -> x0, local copies, waits for them, and re-layouts: 21.1 us -> none  [the longest x2 6.93 us: front(): local_fold = jnp.einsum('ifr,inf->nir', hidden, first_down, preferred_ele...]
    all_to_all x8 -> x0, local copies, waits for them, and re-layouts: 17 us -> none  [the longest x4 10.3 us: to_columns(): lax.all_to_all(value, 'tensor', split_axis=1, concat_axis=0, tiled=True)]
  transfers between devices with their start and end apart: 24 -> 40, of which waited for: 12 -> 21; matrix products, arithmetic and copies ran while one was open for 53% -> 27% of each run, Pallas kernels for 0% -> 0%
where the time goes in v5:
time: 446 us; the launch traced here: 441 us
  waiting for transfers between devices  172 us (39%)
  matrix products  90 us (20%)
  local copies, waits for them, and re-layouts  74.6 us (17%)
  starting transfers between devices  53.1 us (12%)
  other arithmetic  49.8 us (11%)
    ppermute x4, waiting for transfers between devices, shifted(): lax.ppermute(value, axis, [(i, (i + by) % count) for i in range(count)])  111 us
    ppermute x36, waiting for transfers between devices, swapped(): lax.ppermute(piece, 'tensor', [(i, (i + shift) % count) for i in range(co...  60.4 us
    ppermute x36, starting transfers between devices, swapped(): lax.ppermute(piece, 'tensor', [(i, (i + shift) % count) for i in range(co...  47.2 us
    gather x12, local copies, waits for them, and re-layouts, swapped(): return jnp.take(jnp.stack(arrived), order, axis=0)  34.6 us
    dot_general x4, matrix products, front(): jnp.einsum('ifr,inf->nir', hidden, first_down, preferred_element_type=jnp...  26 us
    another operation x12, other arithmetic, swapped(): return jnp.take(jnp.stack(arrived), order, axis=0)  24.3 us
    dot_general x2, matrix products, backward(): jnp.einsum('nir,inf->ifr', grad_folded, first_down, preferred_element_typ...  24 us
    unnamed x115, local copies, waits for them, and re-layouts  20.9 us
  transfers between devices with their start and end apart: 40, of which 21 were waited for; matrix products, arithmetic and copies ran while one was open for 27% of the time, Pallas kernels for 0%

profile of v5, /device:TPU:0, one launch (start us, length us, event | category | flops | bytes accessed | tf_op | source)
XLA Modules:
  0.0 440.7 jit_solution(16832283921482433664)
XLA Ops:
  0.7 3.4 fusion.113
  6.0 2.6 collective-permute-start.21
  18.5 8.6 %collective-permute-start.2 = (bf16[16,32,384]{2,1,0:T(8,128)(2,1)S(1)}, bf16[16,32,384]{2,1,0:T(8,128)(2,1)S(1)}, u32[]{:S(2)}, u32[]{:S(2)}) collective-permute-start(bf16[16,32,384]{2,1,0:T(8,128)(2,1)S(1)} %get-tuple-element.70), channel_id=1, source_target_pairs={{0,3},{1,0},{2,1},{3,2},{4,7},{5,4},{6,5},{7,6},{8,11},{9,8},{10,9... | collective-permute-start | bytes 1179656 | tf_op jit(solution)/shard_map/ppermute | solution.py:31
  28.4 5.1 %collective-permute-done.10 = bf16[16,32,384]{2,1,0:T(8,128)(2,1)S(1)} collective-permute-done((bf16[16,32,384]{2,1,0:T(8,128)(2,1)S(1)}, bf16[16,32,384]{2,1,0:T(8,128)(2,1)S(1)}, u32[]{:S(2)}, u32[]{:S(2)}) %collective-permute-start.10) | collective-permute-done | bytes 393248 | tf_op jit(solution)/shard_map/ppermute | solution.py:31
  33.5 2.6 collective-permute-start.1
  36.2 6.0 %collective-permute-start.7 = (bf16[16,32,384]{2,1,0:T(8,128)(2,1)}, bf16[16,32,384]{2,1,0:T(8,128)(2,1)}, u32[]{:S(2)}, u32[]{:S(2)}) collective-permute-start(bf16[16,32,384]{2,1,0:T(8,128)(2,1)} %get-tuple-element.60), channel_id=1, source_target_pairs={{0,1},{1,2},{2,3},{3,0},{4,5},{5,6},{6,7},{7,4},{8,9},{9,10},{10,1... | collective-permute-start | bytes 1179656 | tf_op jit(solution)/shard_map/ppermute | solution.py:31
  44.4 7.3 %collective-permute-done.2 = bf16[16,32,384]{2,1,0:T(8,128)(2,1)S(1)} collective-permute-done((bf16[16,32,384]{2,1,0:T(8,128)(2,1)S(1)}, bf16[16,32,384]{2,1,0:T(8,128)(2,1)S(1)}, u32[]{:S(2)}, u32[]{:S(2)}) %collective-permute-start.2) | collective-permute-done | bytes 393248 | tf_op jit(solution)/shard_map/ppermute | solution.py:31
  51.7 2.1 collective-permute-start.9
  54.1 1.9 gather_fusion.6
  57.5 1.9 gather_fusion.3
  62.2 1.9 gather_fusion
  64.2 3.2 collective-permute-done.7
  67.3 1.8 collective-permute-done.8
  69.2 7.3 %collective-permute-done.9 = bf16[16,32,384]{2,1,0:T(8,128)(2,1)} collective-permute-done((bf16[16,32,384]{2,1,0:T(8,128)(2,1)}, bf16[16,32,384]{2,1,0:T(8,128)(2,1)}, u32[]{:S(2)}, u32[]{:S(2)}) %collective-permute-start.9) | collective-permute-done | bytes 393248 | tf_op jit(solution)/shard_map/ppermute | solution.py:31
  78.0 1.9 gather_fusion.2
  79.9 4.8 %broadcast_select_fusion.3 = (bf16[4,16,32,384]{3,2,1,0:T(8,128)(2,1)S(1)}, bf16[4,16,32,384]{3,2,1,0:T(8,128)(2,1)}, bf16[4,16,32,384]{3,2,1,0:T(8,128)(2,1)S(1)}, bf16[4,16,32,384]{3,2,1,0:T(8,128)(2,1)S(1)}) fusion(bf16[4,16,32,384]{3,2,1,0:T(8,128)(2,1)} %gather_fusion.2, pred[4]{0:T(512)(128)(4,1)S(1)} %compare_and_fusion, ...), kind=kLoop, calls=%fused_computation.113 | loop fusion | flops 3145728 | bytes 12582916 | tf_op jit(solution)/shard_map/jit(_take)/select_n | solution.py:36
  84.7 7.6 %fusion.34 = (bf16[32,256,384]{1,2,0:T(8,128)(2,1)S(1)}, f32[32,384,256]{2,1,0:T(8,128)}) fusion(bf16[1,32,64,256]{3,2,1,0:T(8,128)(2,1)S(1)} %copy-done, bf16[64,32,384]{2,1,0:T(8,128)(2,1)S(1)} %bitcast.384), kind=kOutput, calls=%fused_computation.57 | convolution fusion | flops 430964736 | bytes 21495808 | tf_op jit(solution)/shard_map/nir,inf->ifr/dot_general | solution.py:60
  92.3 2.0 convolution_convert_fusion.7
  96.0 2.3 collective-permute-start.35
  98.3 11.7 %fusion.6 = bf16[32,256,384]{1,2,0:T(8,128)(2,1)S(1)} fusion(f32[32,384,256]{2,1,0:T(8,128)} %get-tuple-element.90, bf16[64,32,384]{2,1,0:T(8,128)(2,1)S(1)} %bitcast.386, bf16[1,32,64,256]{3,2,1,0:T(8,128)(2,1)S(1)} %copy-done.38), kind=kOutput, calls=%fused_computation.24 | convolution fusion | flops 465567744 | bytes 21495808 | tf_op jit(solution)/shard_map/nir,inf->ifr/dot_general | solution.py:82
  110.0 2.1 convolution_convert_fusion.9
  115.5 8.0 %fusion.50 = bf16[32,384,64]{1,2,0:T(8,128)(2,1)} fusion(bf16[64,32,384]{2,1,0:T(8,128)(2,1)} %bitcast.403, bf16[1,32,64,256]{3,2,1,0:T(8,128)(2,1)} %param.14, bf16[1,32,64,256]{3,2,1,0:T(8,128)(2,1)S(1)} %copy-done), kind=kOutput, calls=%fused_computation.82 | convolution fusion | flops 834404352 | bytes 5242880 | tf_op jit(solution)/shard_map/ifr,inf->nir/dot_general | solution.py:62
  123.5 2.4 constant_dynamic-slice_fusion.5
  125.9 6.4 %fusion.61 = f32[32,384,256]{2,1,0:T(8,128)} fusion(bf16[64,32,384]{2,1,0:T(8,128)(2,1)S(1)} %bitcast.374, bf16[1,32,64,256]{3,2,1,0:T(8,128)(2,1)S(1)} %copy-done), kind=kOutput, calls=%fused_computation.117 | convolution fusion | flops 402653184 | bytes 15204352 | tf_op jit(solution)/shard_map/nir,inf->ifr/dot_general | solution.py:60
  133.7 7.9 %convolution_convert_fusion.6 = bf16[32,384,64]{1,2,0:T(8,128)(2,1)S(1)} fusion(bf16[1,32,64,256]{3,2,1,0:T(8,128)(2,1)S(1)} %copy-done.39, f32[32,384,256]{2,1,0:T(8,128)} %fusion.61), kind=kOutput, calls=%fused_computation.84 | convolution fusion | flops 431751168 | bytes 15204352 | tf_op jit(solution)/shard_map/ifr,inf->nir/dot_general | solution.py:62
  148.3 2.6 pad_maximum_fusion.10
  150.9 3.4 gather_fusion.10
  154.3 2.6 pad_maximum_fusion.4
  156.9 3.5 gather_fusion.4
  160.3 2.6 pad_maximum_fusion.1
  163.0 3.4 gather_fusion.1
  166.3 4.4 collective-permute-done.38
  170.7 2.6 collective-permute-done.39
  173.3 2.6 pad_maximum_fusion.11
  175.9 3.3 gather_fusion.11
  179.2 5.3 %select_bitcast_fusion = (bf16[16,4,32,384]{3,0,2,1:T(8,128)(2,1)}, bf16[16,4,32,384]{3,0,2,1:T(8,128)(2,1)S(1)}, bf16[16,4,32,384]{3,0,2,1:T(8,128)(2,1)S(1)}, bf16[16,4,32,384]{3,0,2,1:T(8,128)(2,1)}) fusion(bf16[4,16,32,384]{3,1,2,0:T(8,128)(2,1)} %gather_fusion.11, pred[4]{0:T(512)(128)(4,1)S(1)} %compare_and_fusion, ...), kind=kLoop, calls=%fused_computation.104 | loop fusion | flops 3145728 | bytes 12582916 | tf_op jit(solution)/shard_map/transpose | solution.py:49
  193.2 34.1 %collective-permute-done.6 = bf16[2048,384]{1,0:T(8,128)(2,1)S(1)} collective-permute-done((bf16[2048,384]{1,0:T(8,128)(2,1)S(1)}, bf16[2048,384]{1,0:T(8,128)(2,1)S(1)}, u32[]{:S(2)}, u32[]{:S(2)}) %collective-permute-start.6) | collective-permute-done | bytes 1572896 | tf_op jit(solution)/shard_map/ppermute | solution.py:9
  227.3 2.0 collective-permute-start.16
  233.0 30.9 %collective-permute-done.16 = bf16[2048,384]{1,0:T(8,128)(2,1)S(1)} collective-permute-done((bf16[2048,384]{1,0:T(8,128)(2,1)S(1)}, bf16[2048,384]{1,0:T(8,128)(2,1)S(1)}, u32[]{:S(2)}, u32[]{:S(2)}) %collective-permute-start.16) | collective-permute-done | bytes 1572896 | tf_op jit(solution)/shard_map/ppermute | solution.py:9
  270.3 3.3 gather_fusion.8
  273.7 3.7 collective-permute-done.17
  278.5 6.6 %collective-permute-done.19 = bf16[16,32,384]{2,1,0:T(8,128)(2,1)} collective-permute-done((bf16[16,32,384]{2,1,0:T(8,128)(2,1)}, bf16[16,32,384]{2,1,0:T(8,128)(2,1)}, u32[]{:S(2)}, u32[]{:S(2)}) %collective-permute-start.19) | collective-permute-done | bytes 393248 | tf_op jit(solution)/shard_map/ppermute | solution.py:31
  285.0 2.6 pad_maximum_fusion.5
  287.6 3.4 gather_fusion.5
  291.0 3.5 broadcast_select_fusion
  294.6 12.3 %fusion.13 = bf16[32,256,384]{1,2,0:T(8,128)(2,1)S(1)} fusion(f32[32,384,256]{2,1,0:T(8,128)} %fusion.61, bf16[64,32,384]{2,1,0:T(8,128)(2,1)S(1)} %bitcast.404, bf16[1,32,64,256]{3,2,1,0:T(8,128)(2,1)S(1)} %copy-done.40), kind=kOutput, calls=%fused_computation.31 | convolution fusion | flops 465567744 | bytes 21495808 | tf_op jit(solution)/shard_map/nir,inf->ifr/dot_general | solution.py:82
  306.8 2.1 convolution_convert_fusion.8
  313.0 8.0 %fusion.53 = bf16[32,384,64]{1,2,0:T(8,128)(2,1)} fusion(bf16[64,32,384]{2,1,0:T(8,128)(2,1)} %bitcast.406, bf16[1,32,64,256]{3,2,1,0:T(8,128)(2,1)} %param.14, bf16[1,32,64,256]{3,2,1,0:T(8,128)(2,1)S(1)} %copy-done), kind=kOutput, calls=%fused_computation.83 | convolution fusion | flops 834404352 | bytes 5242880 | tf_op jit(solution)/shard_map/ifr,inf->nir/dot_general | solution.py:62
  321.0 2.5 constant_dynamic-slice_fusion.2
  326.4 4.7 %collective-permute-done.25 = bf16[16,32,384]{2,0,1:T(8,128)(2,1)} collective-permute-done((bf16[16,32,384]{2,0,1:T(8,128)(2,1)}, bf16[16,32,384]{2,0,1:T(8,128)(2,1)}, u32[]{:S(2)}, u32[]{:S(2)}) %collective-permute-start.25) | collective-permute-done | bytes 393248 | tf_op jit(solution)/shard_map/ppermute | solution.py:31
  331.1 2.6 pad_maximum_fusion.7
  333.7 3.4 gather_fusion.7
  337.6 3.2 collective-permute-done.30
  340.9 5.2 %collective-permute-done.31 = bf16[16,32,384]{2,0,1:T(8,128)(2,1)} collective-permute-done((bf16[16,32,384]{2,0,1:T(8,128)(2,1)}, bf16[16,32,384]{2,0,1:T(8,128)(2,1)}, u32[]{:S(2)}, u32[]{:S(2)}) %collective-permute-start.31) | collective-permute-done | bytes 393248 | tf_op jit(solution)/shard_map/ppermute | solution.py:31
  346.1 2.6 pad_maximum_fusion.9
  348.7 3.3 gather_fusion.9
  352.0 2.4 select_bitcast_fusion.2
  370.7 25.9 %collective-permute-done.32 = bf16[2048,384]{1,0:T(8,128)(2,1)S(1)} collective-permute-done((bf16[2048,384]{1,0:T(8,128)(2,1)S(1)}, bf16[2048,384]{1,0:T(8,128)(2,1)S(1)}, u32[]{:S(2)}, u32[]{:S(2)}) %collective-permute-start.32) | collective-permute-done | bytes 1572896 | tf_op jit(solution)/shard_map/ppermute | solution.py:9
  399.8 2.2 collective-permute-start.33
  402.1 6.6 %add_bitcast_fusion = f32[1,32,64,256]{3,2,1,0:T(8,128)} fusion(f32[32,64,256]{2,1,0:T(8,128)S(1)} %fusion.69, bf16[64,32,384]{2,1,0:T(8,128)(2,1)} %bitcast.405, f32[32,384,256]{2,1,0:T(8,128)S(1)} %bitcast.383), kind=kOutput, calls=%fused_computation.74 | convolution fusion | flops 431489024 | bytes 18350080 | tf_op jit(solution)/shard_map/ifr,nir->inf/dot_general | solution.py:79
  408.7 2.7 add_bitcast_fusion.1
  413.4 3.3 bitcast_convert_fusion.1
  416.7 20.4 %collective-permute-done.33 = bf16[2048,384]{1,0:T(8,128)(2,1)} collective-permute-done((bf16[2048,384]{1,0:T(8,128)(2,1)}, bf16[2048,384]{1,0:T(8,128)(2,1)}, u32[]{:S(2)}, u32[]{:S(2)}) %collective-permute-start.33) | collective-permute-done | bytes 1572896 | tf_op jit(solution)/shard_map/ppermute | solution.py:9
  437.1 3.3 bitcast_convert_fusion
  (221 shorter events, 82.9 us)
Async XLA Ops:
  0.6 84.1 %copy-start = (bf16[1,32,64,256]{3,2,1,0:T(8,128)(2,1)S(1)}, bf16[1,32,64,256]{3,2,1,0:T(8,128)(2,1)}, u32[]{:S(2)}) copy-start(bf16[1,32,64,256]{3,2,1,0:T(8,128)(2,1)} %param.13) | copy-start | bytes 3145732
  0.7 3.5 copy-start.4
  5.3 4.6 %copy-start.7 = (bf16[1,1,2048,384]{3,2,1,0:T(8,128)(2,1)S(1)}, bf16[1,1,2048,384]{3,2,1,0:T(8,128)(2,1)}, u32[]{:S(2)}) copy-start(bf16[1,1,2048,384]{3,2,1,0:T(8,128)(2,1)} %get-tuple-element.27) | copy-start | bytes 4718596
  5.5 11.8 %collective-permute-start.20 = (bf16[16,32,384]{2,1,0:T(8,128)(2,1)S(1)}, bf16[16,32,384]{2,1,0:T(8,128)(2,1)S(1)}, u32[]{:S(2)}, u32[]{:S(2)}) collective-permute-start(bf16[16,32,384]{2,1,0:T(8,128)(2,1)S(1)} %get-tuple-element.76), channel_id=1, source_target_pairs={{0,1},{1,2},{2,3},{3,0},{4,5},{5,6},{6,7},{7,4},{8,9},{9,10},{10,1... | collective-permute-start | bytes 1179656 | tf_op jit(solution)/shard_map/ppermute | solution.py:31
  6.0 12.5 %collective-permute-start.21 = (bf16[16,32,384]{2,1,0:T(8,128)(2,1)S(1)}, bf16[16,32,384]{2,1,0:T(8,128)(2,1)S(1)}, u32[]{:S(2)}, u32[]{:S(2)}) collective-permute-start(bf16[16,32,384]{2,1,0:T(8,128)(2,1)S(1)} %get-tuple-element.75), channel_id=1, source_target_pairs={{0,2},{1,3},{2,0},{3,1},{4,6},{5,7},{6,4},{7,5},{8,10},{9,11},{10,... | collective-permute-start | bytes 1179656 | tf_op jit(solution)/shard_map/ppermute | solution.py:31
  8.6 19.8 %collective-permute-start.22 = (bf16[16,32,384]{2,1,0:T(8,128)(2,1)S(1)}, bf16[16,32,384]{2,1,0:T(8,128)(2,1)S(1)}, u32[]{:S(2)}, u32[]{:S(2)}) collective-permute-start(bf16[16,32,384]{2,1,0:T(8,128)(2,1)S(1)} %get-tuple-element.74), channel_id=1, source_target_pairs={{0,3},{1,0},{2,1},{3,2},{4,7},{5,4},{6,5},{7,6},{8,11},{9,8},{10,9... | collective-permute-start | bytes 1179656 | tf_op jit(solution)/shard_map/ppermute | solution.py:31
  10.8 22.7 %collective-permute-start.10 = (bf16[16,32,384]{2,1,0:T(8,128)(2,1)S(1)}, bf16[16,32,384]{2,1,0:T(8,128)(2,1)S(1)}, u32[]{:S(2)}, u32[]{:S(2)}) collective-permute-start(bf16[16,32,384]{2,1,0:T(8,128)(2,1)S(1)} %get-tuple-element.64), channel_id=1, source_target_pairs={{0,1},{1,2},{2,3},{3,0},{4,5},{5,6},{6,7},{7,4},{8,9},{9,10},{10,1... | collective-permute-start | bytes 1179656 | tf_op jit(solution)/shard_map/ppermute | solution.py:31
  10.8 25.3 %collective-permute-start.11 = (bf16[16,32,384]{2,1,0:T(8,128)(2,1)S(1)}, bf16[16,32,384]{2,1,0:T(8,128)(2,1)S(1)}, u32[]{:S(2)}, u32[]{:S(2)}) collective-permute-start(bf16[16,32,384]{2,1,0:T(8,128)(2,1)S(1)} %get-tuple-element.63), channel_id=1, source_target_pairs={{0,2},{1,3},{2,0},{3,1},{4,6},{5,7},{6,4},{7,5},{8,10},{9,11},{10,... | collective-permute-start | bytes 1179656 | tf_op jit(solution)/shard_map/ppermute | solution.py:31
  17.3 26.0 %collective-permute-start.12 = (bf16[16,32,384]{2,1,0:T(8,128)(2,1)S(1)}, bf16[16,32,384]{2,1,0:T(8,128)(2,1)S(1)}, u32[]{:S(2)}, u32[]{:S(2)}) collective-permute-start(bf16[16,32,384]{2,1,0:T(8,128)(2,1)S(1)} %get-tuple-element.62), channel_id=1, source_target_pairs={{0,3},{1,0},{2,1},{3,2},{4,7},{5,4},{6,5},{7,6},{8,11},{9,8},{10,9... | collective-permute-start | bytes 1179656 | tf_op jit(solution)/shard_map/ppermute | solution.py:31
  18.5 33.2 %collective-permute-start.2 = (bf16[16,32,384]{2,1,0:T(8,128)(2,1)S(1)}, bf16[16,32,384]{2,1,0:T(8,128)(2,1)S(1)}, u32[]{:S(2)}, u32[]{:S(2)}) collective-permute-start(bf16[16,32,384]{2,1,0:T(8,128)(2,1)S(1)} %get-tuple-element.70), channel_id=1, source_target_pairs={{0,3},{1,0},{2,1},{3,2},{4,7},{5,4},{6,5},{7,6},{8,11},{9,8},{10,9... | collective-permute-start | bytes 1179656 | tf_op jit(solution)/shard_map/ppermute | solution.py:31
  28.4 31.0 %collective-permute-start = (bf16[16,32,384]{2,1,0:T(8,128)(2,1)}, bf16[16,32,384]{2,1,0:T(8,128)(2,1)}, u32[]{:S(2)}, u32[]{:S(2)}) collective-permute-start(bf16[16,32,384]{2,1,0:T(8,128)(2,1)} %get-tuple-element.72), channel_id=1, source_target_pairs={{0,1},{1,2},{2,3},{3,0},{4,5},{5,6},{6,7},{7,4},{8,9},{9,10},{10,1... | collective-permute-start | bytes 1179656 | tf_op jit(solution)/shard_map/ppermute | solution.py:31
  33.5 20.3 %copy-start.41 = (bf16[16,32,384]{2,1,0:T(8,128)(2,1)}, bf16[16,32,384]{2,1,0:T(8,128)(2,1)S(1)}, u32[]{:S(2)}) copy-start(bf16[16,32,384]{2,1,0:T(8,128)(2,1)S(1)} %collective-permute-done.10) | copy-start | bytes 1179652
  33.5 27.2 %collective-permute-start.1 = (bf16[16,32,384]{2,1,0:T(8,128)(2,1)}, bf16[16,32,384]{2,1,0:T(8,128)(2,1)}, u32[]{:S(2)}, u32[]{:S(2)}) collective-permute-start(bf16[16,32,384]{2,1,0:T(8,128)(2,1)} %get-tuple-element.71), channel_id=1, source_target_pairs={{0,2},{1,3},{2,0},{3,1},{4,6},{5,7},{6,4},{7,5},{8,10},{9,11},{10,... | collective-permute-start | bytes 1179656 | tf_op jit(solution)/shard_map/ppermute | solution.py:31
  36.2 17.6 %copy-start.42 = (bf16[16,32,384]{2,1,0:T(8,128)(2,1)}, bf16[16,32,384]{2,1,0:T(8,128)(2,1)S(1)}, u32[]{:S(2)}) copy-start(bf16[16,32,384]{2,1,0:T(8,128)(2,1)S(1)} %collective-permute-done.11) | copy-start | bytes 1179652
  36.2 31.2 %collective-permute-start.7 = (bf16[16,32,384]{2,1,0:T(8,128)(2,1)}, bf16[16,32,384]{2,1,0:T(8,128)(2,1)}, u32[]{:S(2)}, u32[]{:S(2)}) collective-permute-start(bf16[16,32,384]{2,1,0:T(8,128)(2,1)} %get-tuple-element.60), channel_id=1, source_target_pairs={{0,1},{1,2},{2,3},{3,0},{4,5},{5,6},{6,7},{7,4},{8,9},{9,10},{10,1... | collective-permute-start | bytes 1179656 | tf_op jit(solution)/shard_map/ppermute | solution.py:31
  43.3 10.5 %copy-start.45 = (bf16[16,32,384]{2,1,0:T(8,128)(2,1)}, bf16[16,32,384]{2,1,0:T(8,128)(2,1)S(1)}, u32[]{:S(2)}) copy-start(bf16[16,32,384]{2,1,0:T(8,128)(2,1)S(1)} %collective-permute-done.12) | copy-start | bytes 1179652
  43.3 25.9 %collective-permute-start.8 = (bf16[16,32,384]{2,1,0:T(8,128)(2,1)}, bf16[16,32,384]{2,1,0:T(8,128)(2,1)}, u32[]{:S(2)}, u32[]{:S(2)}) collective-permute-start(bf16[16,32,384]{2,1,0:T(8,128)(2,1)} %get-tuple-element.59), channel_id=1, source_target_pairs={{0,2},{1,3},{2,0},{3,1},{4,6},{5,7},{6,4},{7,5},{8,10},{9,11},{10,... | collective-permute-start | bytes 1179656 | tf_op jit(solution)/shard_map/ppermute | solution.py:31
  51.7 24.8 %collective-permute-start.9 = (bf16[16,32,384]{2,1,0:T(8,128)(2,1)}, bf16[16,32,384]{2,1,0:T(8,128)(2,1)}, u32[]{:S(2)}, u32[]{:S(2)}) collective-permute-start(bf16[16,32,384]{2,1,0:T(8,128)(2,1)} %get-tuple-element.58), channel_id=1, source_target_pairs={{0,3},{1,0},{2,1},{3,2},{4,7},{5,4},{6,5},{7,6},{8,11},{9,8},{10,9... | collective-permute-start | bytes 1179656 | tf_op jit(solution)/shard_map/ppermute | solution.py:31
  62.2 14.3 %copy-start.35 = (bf16[1,16,32,384]{3,2,1,0:T(8,128)(2,1)S(1)}, bf16[1,16,32,384]{3,2,1,0:T(8,128)(2,1)}, u32[]{:S(2)}) copy-start(bf16[1,16,32,384]{3,2,1,0:T(8,128)(2,1)} %get-tuple-element.57) | copy-start | bytes 1179652
  84.7 7.6 %copy-start.22 = (bf16[4,16,32,384]{3,2,1,0:T(8,128)(2,1)}, bf16[4,16,32,384]{3,2,1,0:T(8,128)(2,1)S(1)}, u32[]{:S(2)}) copy-start(bf16[4,16,32,384]{3,2,1,0:T(8,128)(2,1)S(1)} %get-tuple-element.87) | copy-start | bytes 4718596
  84.7 13.6 %copy-start.24 = (bf16[4,16,32,384]{3,2,1,0:T(8,128)(2,1)}, bf16[4,16,32,384]{3,2,1,0:T(8,128)(2,1)S(1)}, u32[]{:S(2)}) copy-start(bf16[4,16,32,384]{3,2,1,0:T(8,128)(2,1)S(1)} %get-tuple-element.85) | copy-start | bytes 4718596
  84.7 7.6 %copy-start.38 = (bf16[1,32,64,256]{3,2,1,0:T(8,128)(2,1)S(1)}, bf16[1,32,64,256]{3,2,1,0:T(8,128)(2,1)}, u32[]{:S(2)}) copy-start(bf16[1,32,64,256]{3,2,1,0:T(8,128)(2,1)} %param.14) | copy-start | bytes 3145732
  96.0 36.4 %collective-permute-start.34 = (bf16[16,32,384]{2,0,1:T(8,128)(2,1)}, bf16[16,32,384]{2,0,1:T(8,128)(2,1)}, u32[]{:S(2)}, u32[]{:S(2)}) collective-permute-start(bf16[16,32,384]{2,0,1:T(8,128)(2,1)} %get-tuple-element.36), channel_id=1, source_target_pairs={{0,1},{1,2},{2,3},{3,0},{4,5},{5,6},{6,7},{7,4},{8,9},{9,10},{10,1... | collective-permute-start | bytes 1179656 | tf_op jit(solution)/shard_map/ppermute | solution.py:31
  96.0 37.7 %collective-permute-start.35 = (bf16[16,32,384]{2,0,1:T(8,128)(2,1)}, bf16[16,32,384]{2,0,1:T(8,128)(2,1)}, u32[]{:S(2)}, u32[]{:S(2)}) collective-permute-start(bf16[16,32,384]{2,0,1:T(8,128)(2,1)} %get-tuple-element.35), channel_id=1, source_target_pairs={{0,2},{1,3},{2,0},{3,1},{4,6},{5,7},{6,4},{7,5},{8,10},{9,11},{10,... | collective-permute-start | bytes 1179656 | tf_op jit(solution)/shard_map/ppermute | solution.py:31
  98.3 43.4 %collective-permute-start.36 = (bf16[16,32,384]{2,0,1:T(8,128)(2,1)}, bf16[16,32,384]{2,0,1:T(8,128)(2,1)}, u32[]{:S(2)}, u32[]{:S(2)}) collective-permute-start(bf16[16,32,384]{2,0,1:T(8,128)(2,1)} %get-tuple-element.34), channel_id=1, source_target_pairs={{0,3},{1,0},{2,1},{3,2},{4,7},{5,4},{6,5},{7,6},{8,11},{9,8},{10,9... | collective-permute-start | bytes 1179656 | tf_op jit(solution)/shard_map/ppermute | solution.py:31
  113.8 28.6 %collective-permute-start.13 = (bf16[16,32,384]{2,0,1:T(8,128)(2,1)}, bf16[16,32,384]{2,0,1:T(8,128)(2,1)}, u32[]{:S(2)}, u32[]{:S(2)}) collective-permute-start(bf16[16,32,384]{2,0,1:T(8,128)(2,1)} %get-tuple-element.56), channel_id=1, source_target_pairs={{0,1},{1,2},{2,3},{3,0},{4,5},{5,6},{6,7},{7,4},{8,9},{9,10},{10,1... | collective-permute-start | bytes 1179656 | tf_op jit(solution)/shard_map/ppermute | solution.py:31
  114.6 30.5 %collective-permute-start.14 = (bf16[16,32,384]{2,0,1:T(8,128)(2,1)}, bf16[16,32,384]{2,0,1:T(8,128)(2,1)}, u32[]{:S(2)}, u32[]{:S(2)}) collective-permute-start(bf16[16,32,384]{2,0,1:T(8,128)(2,1)} %get-tuple-element.55), channel_id=1, source_target_pairs={{0,2},{1,3},{2,0},{3,1},{4,6},{5,7},{6,4},{7,5},{8,10},{9,11},{10,... | collective-permute-start | bytes 1179656 | tf_op jit(solution)/shard_map/ppermute | solution.py:31
  125.9 6.4 %copy-start.47 = (bf16[16,32,384]{2,0,1:T(8,128)(2,1)S(1)}, bf16[16,32,384]{2,0,1:T(8,128)(2,1)}, u32[]{:S(2)}) copy-start(bf16[16,32,384]{2,0,1:T(8,128)(2,1)} %get-tuple-element.54) | copy-start | bytes 1179652
  125.9 7.8 %copy-start.39 = (bf16[1,32,64,256]{3,2,1,0:T(8,128)(2,1)S(1)}, bf16[1,32,64,256]{3,2,1,0:T(8,128)(2,1)}, u32[]{:S(2)}) copy-start(bf16[1,32,64,256]{3,2,1,0:T(8,128)(2,1)} %param.14) | copy-start | bytes 3145732
  132.3 12.8 %collective-permute-start.15 = (bf16[16,32,384]{2,0,1:T(8,128)(2,1)S(1)}, bf16[16,32,384]{2,0,1:T(8,128)(2,1)S(1)}, u32[]{:S(2)}, u32[]{:S(2)}) collective-permute-start(bf16[16,32,384]{2,0,1:T(8,128)(2,1)S(1)} %copy-done.47), channel_id=1, source_target_pairs={{0,3},{1,0},{2,1},{3,2},{4,7},{5,4},{6,5},{7,6},{8,11},{9,8},{10,9... | collective-permute-start | bytes 1179656 | tf_op jit(solution)/shard_map/ppermute | solution.py:31
  133.7 12.8 %collective-permute-start.3 = (bf16[16,32,384]{2,0,1:T(8,128)(2,1)S(1)}, bf16[16,32,384]{2,0,1:T(8,128)(2,1)S(1)}, u32[]{:S(2)}, u32[]{:S(2)}) collective-permute-start(bf16[16,32,384]{2,0,1:T(8,128)(2,1)S(1)} %get-tuple-element.68), channel_id=1, source_target_pairs={{0,1},{1,2},{2,3},{3,0},{4,5},{5,6},{6,7},{7,4},{8,9},{9,10},{10,1... | collective-permute-start | bytes 1179656 | tf_op jit(solution)/shard_map/ppermute | solution.py:31
  141.7 18.7 %collective-permute-start.4 = (bf16[16,32,384]{2,0,1:T(8,128)(2,1)}, bf16[16,32,384]{2,0,1:T(8,128)(2,1)}, u32[]{:S(2)}, u32[]{:S(2)}) collective-permute-start(bf16[16,32,384]{2,0,1:T(8,128)(2,1)} %get-tuple-element.67), channel_id=1, source_target_pairs={{0,2},{1,3},{2,0},{3,1},{4,6},{5,7},{6,4},{7,5},{8,10},{9,11},{10,... | collective-permute-start | bytes 1179656 | tf_op jit(solution)/shard_map/ppermute | solution.py:31
  142.4 17.9 %collective-permute-start.5 = (bf16[16,32,384]{2,0,1:T(8,128)(2,1)}, bf16[16,32,384]{2,0,1:T(8,128)(2,1)}, u32[]{:S(2)}, u32[]{:S(2)}) collective-permute-start(bf16[16,32,384]{2,0,1:T(8,128)(2,1)} %get-tuple-element.66), channel_id=1, source_target_pairs={{0,3},{1,0},{2,1},{3,2},{4,7},{5,4},{6,5},{7,6},{8,11},{9,8},{10,9... | collective-permute-start | bytes 1179656 | tf_op jit(solution)/shard_map/ppermute | solution.py:31
  145.1 21.3 %collective-permute-start.37 = (bf16[16,32,384]{2,0,1:T(8,128)(2,1)}, bf16[16,32,384]{2,0,1:T(8,128)(2,1)}, u32[]{:S(2)}, u32[]{:S(2)}) collective-permute-start(bf16[16,32,384]{2,0,1:T(8,128)(2,1)} %get-tuple-element.32), channel_id=1, source_target_pairs={{0,1},{1,2},{2,3},{3,0},{4,5},{5,6},{6,7},{7,4},{8,9},{9,10},{10,1... | collective-permute-start | bytes 1179656 | tf_op jit(solution)/shard_map/ppermute | solution.py:31
  145.1 25.6 %collective-permute-start.38 = (bf16[16,32,384]{2,0,1:T(8,128)(2,1)}, bf16[16,32,384]{2,0,1:T(8,128)(2,1)}, u32[]{:S(2)}, u32[]{:S(2)}) collective-permute-start(bf16[16,32,384]{2,0,1:T(8,128)(2,1)} %get-tuple-element.31), channel_id=1, source_target_pairs={{0,2},{1,3},{2,0},{3,1},{4,6},{5,7},{6,4},{7,5},{8,10},{9,11},{10,... | collective-permute-start | bytes 1179656 | tf_op jit(solution)/shard_map/ppermute | solution.py:31
  146.5 26.8 %collective-permute-start.39 = (bf16[16,32,384]{2,0,1:T(8,128)(2,1)}, bf16[16,32,384]{2,0,1:T(8,128)(2,1)}, u32[]{:S(2)}, u32[]{:S(2)}) collective-permute-start(bf16[16,32,384]{2,0,1:T(8,128)(2,1)} %get-tuple-element.30), channel_id=1, source_target_pairs={{0,3},{1,0},{2,1},{3,2},{4,7},{5,4},{6,5},{7,6},{8,11},{9,8},{10,9... | collective-permute-start | bytes 1179656 | tf_op jit(solution)/shard_map/ppermute | solution.py:31
  156.9 3.5 copy-start.34
  163.0 10.4 %copy-start.36 = (bf16[1,16,32,384]{3,1,0,2:T(8,128)(2,1)S(1)}, bf16[1,16,32,384]{3,1,0,2:T(8,128)(2,1)}, u32[]{:S(2)}) copy-start(bf16[1,16,32,384]{3,1,0,2:T(8,128)(2,1)} %get-tuple-element.29) | copy-start | bytes 1179652
  187.8 39.5 %collective-permute-start.6 = (bf16[2048,384]{1,0:T(8,128)(2,1)S(1)}, bf16[2048,384]{1,0:T(8,128)(2,1)S(1)}, u32[]{:S(2)}, u32[]{:S(2)}) collective-permute-start(bf16[2048,384]{1,0:T(8,128)(2,1)S(1)} %fusion.49), channel_id=1, source_target_pairs={{0,4},{4,8},{8,12},{12,16},{16,20},{20,24},{24,28},{28,0},{1,5},{5... | collective-permute-start | bytes 4718600 | tf_op jit(solution)/shard_map/ppermute | solution.py:9
  227.3 36.7 %collective-permute-start.16 = (bf16[2048,384]{1,0:T(8,128)(2,1)S(1)}, bf16[2048,384]{1,0:T(8,128)(2,1)S(1)}, u32[]{:S(2)}, u32[]{:S(2)}) collective-permute-start(bf16[2048,384]{1,0:T(8,128)(2,1)S(1)} %fusion.48), channel_id=1, source_target_pairs={{0,28},{4,0},{8,4},{12,8},{16,12},{20,16},{24,20},{28,24},{1,29},{... | collective-permute-start | bytes 4718600 | tf_op jit(solution)/shard_map/ppermute | solution.py:9
  230.1 37.2 %collective-permute-start.26 = (bf16[16,32,384]{2,1,0:T(8,128)(2,1)S(1)}, bf16[16,32,384]{2,1,0:T(8,128)(2,1)S(1)}, u32[]{:S(2)}, u32[]{:S(2)}) collective-permute-start(bf16[16,32,384]{2,1,0:T(8,128)(2,1)S(1)} %get-tuple-element.44), channel_id=1, source_target_pairs={{0,1},{1,2},{2,3},{3,0},{4,5},{5,6},{6,7},{7,4},{8,9},{9,10},{10,1... | collective-permute-start | bytes 1179656 | tf_op jit(solution)/shard_map/ppermute | solution.py:31
  230.2 38.7 %collective-permute-start.27 = (bf16[16,32,384]{2,1,0:T(8,128)(2,1)S(1)}, bf16[16,32,384]{2,1,0:T(8,128)(2,1)S(1)}, u32[]{:S(2)}, u32[]{:S(2)}) collective-permute-start(bf16[16,32,384]{2,1,0:T(8,128)(2,1)S(1)} %get-tuple-element.43), channel_id=1, source_target_pairs={{0,2},{1,3},{2,0},{3,1},{4,6},{5,7},{6,4},{7,5},{8,10},{9,11},{10,... | collective-permute-start | bytes 1179656 | tf_op jit(solution)/shard_map/ppermute | solution.py:31
  231.7 37.3 %collective-permute-start.28 = (bf16[16,32,384]{2,1,0:T(8,128)(2,1)S(1)}, bf16[16,32,384]{2,1,0:T(8,128)(2,1)S(1)}, u32[]{:S(2)}, u32[]{:S(2)}) collective-permute-start(bf16[16,32,384]{2,1,0:T(8,128)(2,1)S(1)} %get-tuple-element.42), channel_id=1, source_target_pairs={{0,3},{1,0},{2,1},{3,2},{4,7},{5,4},{6,5},{7,6},{8,11},{9,8},{10,9... | collective-permute-start | bytes 1179656 | tf_op jit(solution)/shard_map/ppermute | solution.py:31
  266.2 11.2 %collective-permute-start.17 = (bf16[16,32,384]{2,1,0:T(8,128)(2,1)}, bf16[16,32,384]{2,1,0:T(8,128)(2,1)}, u32[]{:S(2)}, u32[]{:S(2)}) collective-permute-start(bf16[16,32,384]{2,1,0:T(8,128)(2,1)} %get-tuple-element.52), channel_id=1, source_target_pairs={{0,1},{1,2},{2,3},{3,0},{4,5},{5,6},{6,7},{7,4},{8,9},{9,10},{10,1... | collective-permute-start | bytes 1179656 | tf_op jit(solution)/shard_map/ppermute | solution.py:31
  266.2 12.3 %collective-permute-start.18 = (bf16[16,32,384]{2,1,0:T(8,128)(2,1)}, bf16[16,32,384]{2,1,0:T(8,128)(2,1)}, u32[]{:S(2)}, u32[]{:S(2)}) collective-permute-start(bf16[16,32,384]{2,1,0:T(8,128)(2,1)} %get-tuple-element.51), channel_id=1, source_target_pairs={{0,2},{1,3},{2,0},{3,1},{4,6},{5,7},{6,4},{7,5},{8,10},{9,11},{10,... | collective-permute-start | bytes 1179656 | tf_op jit(solution)/shard_map/ppermute | solution.py:31
  267.4 17.6 %collective-permute-start.19 = (bf16[16,32,384]{2,1,0:T(8,128)(2,1)}, bf16[16,32,384]{2,1,0:T(8,128)(2,1)}, u32[]{:S(2)}, u32[]{:S(2)}) collective-permute-start(bf16[16,32,384]{2,1,0:T(8,128)(2,1)} %get-tuple-element.50), channel_id=1, source_target_pairs={{0,3},{1,0},{2,1},{3,2},{4,7},{5,4},{6,5},{7,6},{8,11},{9,8},{10,9... | collective-permute-start | bytes 1179656 | tf_op jit(solution)/shard_map/ppermute | solution.py:31
  291.0 3.5 copy-start.40
  294.5 12.3 %copy-start.30 = (bf16[4,16,32,384]{3,2,1,0:T(8,128)(2,1)}, bf16[4,16,32,384]{3,2,1,0:T(8,128)(2,1)S(1)}, u32[]{:S(2)}) copy-start(bf16[4,16,32,384]{3,2,1,0:T(8,128)(2,1)S(1)} %get-tuple-element.84) | copy-start | bytes 4718596
  310.5 14.5 %collective-permute-start.23 = (bf16[16,32,384]{2,0,1:T(8,128)(2,1)}, bf16[16,32,384]{2,0,1:T(8,128)(2,1)}, u32[]{:S(2)}, u32[]{:S(2)}) collective-permute-start(bf16[16,32,384]{2,0,1:T(8,128)(2,1)} %get-tuple-element.48), channel_id=1, source_target_pairs={{0,1},{1,2},{2,3},{3,0},{4,5},{5,6},{6,7},{7,4},{8,9},{9,10},{10,1... | collective-permute-start | bytes 1179656 | tf_op jit(solution)/shard_map/ppermute | solution.py:31
  311.6 14.8 %collective-permute-start.24 = (bf16[16,32,384]{2,0,1:T(8,128)(2,1)}, bf16[16,32,384]{2,0,1:T(8,128)(2,1)}, u32[]{:S(2)}, u32[]{:S(2)}) collective-permute-start(bf16[16,32,384]{2,0,1:T(8,128)(2,1)} %get-tuple-element.47), channel_id=1, source_target_pairs={{0,2},{1,3},{2,0},{3,1},{4,6},{5,7},{6,4},{7,5},{8,10},{9,11},{10,... | collective-permute-start | bytes 1179656 | tf_op jit(solution)/shard_map/ppermute | solution.py:31
  312.8 18.3 %collective-permute-start.25 = (bf16[16,32,384]{2,0,1:T(8,128)(2,1)}, bf16[16,32,384]{2,0,1:T(8,128)(2,1)}, u32[]{:S(2)}, u32[]{:S(2)}) collective-permute-start(bf16[16,32,384]{2,0,1:T(8,128)(2,1)} %get-tuple-element.46), channel_id=1, source_target_pairs={{0,3},{1,0},{2,1},{3,2},{4,7},{5,4},{6,5},{7,6},{8,11},{9,8},{10,9... | collective-permute-start | bytes 1179656 | tf_op jit(solution)/shard_map/ppermute | solution.py:31
  323.6 14.0 %collective-permute-start.29 = (bf16[16,32,384]{2,0,1:T(8,128)(2,1)}, bf16[16,32,384]{2,0,1:T(8,128)(2,1)}, u32[]{:S(2)}, u32[]{:S(2)}) collective-permute-start(bf16[16,32,384]{2,0,1:T(8,128)(2,1)} %get-tuple-element.40), channel_id=1, source_target_pairs={{0,1},{1,2},{2,3},{3,0},{4,5},{5,6},{6,7},{7,4},{8,9},{9,10},{10,1... | collective-permute-start | bytes 1179656 | tf_op jit(solution)/shard_map/ppermute | solution.py:31
  324.1 16.8 %collective-permute-start.30 = (bf16[16,32,384]{2,0,1:T(8,128)(2,1)}, bf16[16,32,384]{2,0,1:T(8,128)(2,1)}, u32[]{:S(2)}, u32[]{:S(2)}) collective-permute-start(bf16[16,32,384]{2,0,1:T(8,128)(2,1)} %get-tuple-element.39), channel_id=1, source_target_pairs={{0,2},{1,3},{2,0},{3,1},{4,6},{5,7},{6,4},{7,5},{8,10},{9,11},{10,... | collective-permute-start | bytes 1179656 | tf_op jit(solution)/shard_map/ppermute | solution.py:31
  325.0 21.0 %collective-permute-start.31 = (bf16[16,32,384]{2,0,1:T(8,128)(2,1)}, bf16[16,32,384]{2,0,1:T(8,128)(2,1)}, u32[]{:S(2)}, u32[]{:S(2)}) collective-permute-start(bf16[16,32,384]{2,0,1:T(8,128)(2,1)} %get-tuple-element.38), channel_id=1, source_target_pairs={{0,3},{1,0},{2,1},{3,2},{4,7},{5,4},{6,5},{7,6},{8,11},{9,8},{10,9... | collective-permute-start | bytes 1179656 | tf_op jit(solution)/shard_map/ppermute | solution.py:31
  333.7 12.3 %copy-start.37 = (bf16[1,16,32,384]{3,1,0,2:T(8,128)(2,1)S(1)}, bf16[1,16,32,384]{3,1,0,2:T(8,128)(2,1)}, u32[]{:S(2)}) copy-start(bf16[1,16,32,384]{3,1,0,2:T(8,128)(2,1)} %get-tuple-element.37) | copy-start | bytes 1179652
  352.0 5.3 %slice-start = ((s8[6291456]{0:T(1024)(128)(4,1)}), s8[4194304]{0:T(1024)(128)(4,1)S(1)}, s32[]{:S(2)}) async-start(s8[6291456]{0:T(1024)(128)(4,1)} %bitcast.362), calls=%async_computation | async-start | bytes 8388608
  357.2 3.4 copy-start.23
  357.3 39.4 %collective-permute-start.32 = (bf16[2048,384]{1,0:T(8,128)(2,1)S(1)}, bf16[2048,384]{1,0:T(8,128)(2,1)S(1)}, u32[]{:S(2)}, u32[]{:S(2)}) collective-permute-start(bf16[2048,384]{1,0:T(8,128)(2,1)S(1)} %fusion.47), channel_id=1, source_target_pairs={{0,4},{4,8},{8,12},{12,16},{16,20},{20,24},{24,28},{28,0},{1,5},{5... | collective-permute-start | bytes 4718600 | tf_op jit(solution)/shard_map/ppermute | solution.py:9
  358.5 43.6 %slice-start.6 = ((s8[12582912]{0:T(1024)(128)(4,1)}), s8[4194304]{0:T(1024)(128)(4,1)S(1)}, s32[]{:S(2)}) async-start(s8[12582912]{0:T(1024)(128)(4,1)} %bitcast.382), calls=%async_computation.6 | async-start | bytes 8388608
  360.7 41.4 %slice-start.7 = ((s8[12582912]{0:T(1024)(128)(4,1)}), s8[4194304]{0:T(1024)(128)(4,1)S(1)}, s32[]{:S(2)}) async-start(s8[12582912]{0:T(1024)(128)(4,1)} %bitcast.382), calls=%async_computation.7 | async-start | bytes 8388608
  368.6 33.5 %slice-start.8 = ((s8[12582912]{0:T(1024)(128)(4,1)}), s8[4194304]{0:T(1024)(128)(4,1)S(1)}, s32[]{:S(2)}) async-start(s8[12582912]{0:T(1024)(128)(4,1)} %bitcast.382), calls=%async_computation.8 | async-start | bytes 8388608
  398.3 10.3 %slice-start.4 = ((s8[6291456]{0:T(1024)(128)(4,1)}), s8[4194304]{0:T(1024)(128)(4,1)S(1)}, s32[]{:S(2)}) async-start(s8[6291456]{0:T(1024)(128)(4,1)} %bitcast.366), calls=%async_computation.4 | async-start | bytes 8388608
  399.8 8.8 %slice-start.5 = ((s8[6291456]{0:T(1024)(128)(4,1)}), s8[2097152]{0:T(1024)(128)(4,1)S(1)}, s32[]{:S(2)}) async-start(s8[6291456]{0:T(1024)(128)(4,1)} %bitcast.366), calls=%async_computation.5 | async-start | bytes 4194304
  399.8 37.3 %collective-permute-start.33 = (bf16[2048,384]{1,0:T(8,128)(2,1)}, bf16[2048,384]{1,0:T(8,128)(2,1)}, u32[]{:S(2)}, u32[]{:S(2)}) collective-permute-start(bf16[2048,384]{1,0:T(8,128)(2,1)} %fusion.46), channel_id=1, source_target_pairs={{0,28},{4,0},{8,4},{12,8},{16,12},{20,16},{24,20},{28,24},{1,29},{... | collective-permute-start | bytes 4718600 | tf_op jit(solution)/shard_map/ppermute | solution.py:9
  (33 other events, 63.8 us)

commit v6 on v4

--- a/solution.py
+++ b/solution.py
@@ -124,10 +124,7 @@
     near_activation = shifted(sent, "pipe", 1)
 
     stored = stash[0, 0].reshape(blocks, width, rows)
-    behind = front(
-        stored, up_first, up_second, down_first,
-        to_columns_by_permutes, to_rows_by_permutes,
-    )
+    behind = front(stored, up_first, up_second, down_first)
     grad_step, totals = backward(
         stored, cotangent, up_first, up_second, down_first, down_second, behind
     )

time: 385 us -> 396 us (1.029)
  waiting for transfers between devices: 100 us -> 127 us
  other arithmetic: 35.2 us -> 24.7 us
  local copies, waits for them, and re-layouts: 71.7 us -> 66.8 us
    all_to_all x4 -> x5, waiting for transfers between devices: 20.3 us -> 43.7 us  [to_columns(): lax.all_to_all(value, 'tensor', split_axis=1, concat_axis=0, tiled=True)]
    gather x4 -> x2, local copies, waits for them, and re-layouts: 13.4 us -> 5.23 us  [swapped(): return jnp.take(jnp.stack(arrived), order, axis=0)]
    another operation x4 -> x2, other arithmetic: 10.5 us -> 2.86 us  [swapped(): return jnp.take(jnp.stack(arrived), order, axis=0)]
    all_to_all x4 -> x5, starting transfers between devices: 17.6 us -> 22.4 us  [to_columns(): lax.all_to_all(value, 'tensor', split_axis=1, concat_axis=0, tiled=True)]
    ppermute x12 -> x6, starting transfers between devices: 12 us -> 7.42 us  [swapped(): lax.ppermute(piece, 'tensor', [(i, (i + shift) % count) for i in range(co...]
    all_to_all x4 -> x5, starting transfers between devices: 17.9 us -> 22.1 us  [to_rows(): lax.all_to_all(value, 'tensor', split_axis=0, concat_axis=1, tiled=True)]
    all_to_all x4 -> x5, local copies, waits for them, and re-layouts: 10.3 us -> 13.8 us  [to_columns(): lax.all_to_all(value, 'tensor', split_axis=1, concat_axis=0, tiled=True)]
    ppermute x12 -> x6, waiting for transfers between devices: 27 us -> 29.9 us  [swapped(): lax.ppermute(piece, 'tensor', [(i, (i + shift) % count) for i in range(co...]
  transfers between devices with their start and end apart: 24 -> 20, of which waited for: 12 -> 14; matrix products, arithmetic and copies ran while one was open for 53% -> 40% of each run, Pallas kernels for 0% -> 0%
where the time goes in v6:
time: 396 us; the launch traced here: 389 us
  waiting for transfers between devices  127 us (32%)
  matrix products  111 us (28%)
  local copies, waits for them, and re-layouts  66.8 us (17%)
  starting transfers between devices  58.2 us (15%)
  other arithmetic  24.7 us (6%)
    all_to_all x5, waiting for transfers between devices, to_columns(): lax.all_to_all(value, 'tensor', split_axis=1, concat_axis=0, tiled=True)  43.7 us
    ppermute x4, waiting for transfers between devices, shifted(): lax.ppermute(value, axis, [(i, (i + by) % count) for i in range(count)])  36 us
    ppermute x6, waiting for transfers between devices, swapped(): lax.ppermute(piece, 'tensor', [(i, (i + shift) % count) for i in range(co...  29.9 us
    dot_general x4, matrix products, front(): jnp.einsum('ifr,inf->nir', hidden, first_down, preferred_element_type=jnp...  28.3 us
    dot_general x2, matrix products, backward(): jnp.einsum('nir,inf->ifr', grad_folded, first_down, preferred_element_typ...  25.5 us
    all_to_all x5, starting transfers between devices, to_columns(): lax.all_to_all(value, 'tensor', split_axis=1, concat_axis=0, tiled=True)  22.4 us
    all_to_all x5, starting transfers between devices, to_rows(): lax.all_to_all(value, 'tensor', split_axis=0, concat_axis=1, tiled=True)  22.1 us
    all_to_all x5, waiting for transfers between devices, to_rows(): lax.all_to_all(value, 'tensor', split_axis=0, concat_axis=1, tiled=True)  17.3 us
  transfers between devices with their start and end apart: 20, of which 14 were waited for; matrix products, arithmetic and copies ran while one was open for 40% of the time, Pallas kernels for 0%

profile of v6, /device:TPU:0, one launch (start us, length us, event | category | flops | bytes accessed | tf_op | source)
XLA Modules:
  0.0 388.9 jit_solution(6271201539042543001)
XLA Ops:
  0.7 2.3 fusion.112
  4.8 2.1 copy.85
  6.9 4.4 %all-to-all-start.3 = ((bf16[16,128,384]{2,0,1:T(8,128)(2,1)}), bf16[16,128,384]{2,0,1:T(8,128)(2,1)}, u32[]{:S(2)}, u32[]{:S(2)}) async-start(bf16[16,128,384]{2,0,1:T(8,128)(2,1)} %copy.85), calls=%async_computation.3 | async-start | bytes 3145728 | tf_op jit(solution)/shard_map/all_to_all | solution.py:17
  11.2 2.1 convert_element_type.119
  15.1 2.1 copy.82
  17.2 14.8 %all-to-all-done.3 = bf16[16,128,384]{2,0,1:T(8,128)(2,1)} async-done(((bf16[16,128,384]{2,0,1:T(8,128)(2,1)}), bf16[16,128,384]{2,0,1:T(8,128)(2,1)}, u32[]{:S(2)}, u32[]{:S(2)}) %all-to-all-start.3) | async-done | bytes 1572896 | tf_op jit(solution)/shard_map/all_to_all | solution.py:17
  32.0 4.3 %all-to-all-start.2 = ((bf16[16,128,384]{2,0,1:T(8,128)(2,1)}), bf16[16,128,384]{2,0,1:T(8,128)(2,1)}, u32[]{:S(2)}, u32[]{:S(2)}) async-start(bf16[16,128,384]{2,0,1:T(8,128)(2,1)} %copy.82), calls=%async_computation.2 | async-start | bytes 3145728 | tf_op jit(solution)/shard_map/all_to_all | solution.py:17
  36.4 2.1 convert_element_type.112
  39.1 2.1 copy.76
  41.1 15.3 %all-to-all-done.2 = bf16[16,128,384]{2,0,1:T(8,128)(2,1)} async-done(((bf16[16,128,384]{2,0,1:T(8,128)(2,1)}), bf16[16,128,384]{2,0,1:T(8,128)(2,1)}, u32[]{:S(2)}, u32[]{:S(2)}) %all-to-all-start.2) | async-done | bytes 1572896 | tf_op jit(solution)/shard_map/all_to_all | solution.py:17
  56.5 4.4 %all-to-all-start = ((bf16[16,128,384]{2,0,1:T(8,128)(2,1)}), bf16[16,128,384]{2,0,1:T(8,128)(2,1)}, u32[]{:S(2)}, u32[]{:S(2)}) async-start(bf16[16,128,384]{2,0,1:T(8,128)(2,1)} %copy.76), calls=%async_computation | async-start | bytes 3145728 | tf_op jit(solution)/shard_map/all_to_all | solution.py:17
  63.9 1.8 collective-permute-start.4
  65.7 23.1 %collective-permute-done.2 = bf16[16,32,384]{2,1,0:T(8,128)(2,1)S(1)} collective-permute-done((bf16[16,32,384]{2,1,0:T(8,128)(2,1)S(1)}, bf16[16,32,384]{2,1,0:T(8,128)(2,1)S(1)}, u32[]{:S(2)}, u32[]{:S(2)}) %collective-permute-start.2) | collective-permute-done | bytes 393248 | tf_op jit(solution)/shard_map/ppermute | solution.py:31
  89.8 5.8 %collective-permute-done.4 = bf16[16,32,384]{2,1,0:T(8,128)(2,1)S(1)} collective-permute-done((bf16[16,32,384]{2,1,0:T(8,128)(2,1)S(1)}, bf16[16,32,384]{2,1,0:T(8,128)(2,1)S(1)}, u32[]{:S(2)}, u32[]{:S(2)}) %collective-permute-start.4) | collective-permute-done | bytes 393248 | tf_op jit(solution)/shard_map/ppermute | solution.py:31
  95.9 1.9 gather_fusion
  99.4 3.4 copy.86
  102.8 2.8 copy.83
  105.7 3.0 copy.77
  108.6 8.8 %fusion.34 = (bf16[32,256,384]{1,2,0:T(8,128)(2,1)}, f32[32,384,256]{2,1,0:T(8,128)}) fusion(bf16[64,32,384]{2,0,1:T(8,128)(2,1)S(1)} %bitcast.302, bf16[1,32,64,256]{3,2,1,0:T(8,128)(2,1)S(1)} %copy-done), kind=kOutput, calls=%fused_computation.47 | convolution fusion | flops 430964736 | bytes 21495808 | tf_op jit(solution)/shard_map/nir,inf->ifr/dot_general | solution.py:60
  117.4 7.6 %fusion.59 = bf16[64,32,384]{2,0,1:T(8,128)(2,1)} fusion(bf16[64,32,384]{2,0,1:T(8,128)(2,1)} %bitcast.312, bf16[1,32,64,256]{3,2,1,0:T(8,128)(2,1)} %param.14, bf16[1,32,64,256]{3,2,1,0:T(8,128)(2,1)S(1)} %copy-done), kind=kOutput, calls=%fused_computation.85 | convolution fusion | flops 834404352 | bytes 5242880 | tf_op jit(solution)/shard_map/ifr,inf->nir/dot_general | solution.py:62
  125.1 3.5 copy.79
  128.5 4.5 %all-to-all-start.1 = ((bf16[64,32,384]{2,1,0:T(8,128)(2,1)}), bf16[64,32,384]{2,1,0:T(8,128)(2,1)}, u32[]{:S(2)}, u32[]{:S(2)}) async-start(bf16[64,32,384]{2,1,0:T(8,128)(2,1)} %copy.79), calls=%async_computation.1 | async-start | bytes 3145728 | tf_op jit(solution)/shard_map/all_to_all | solution.py:21
  133.0 13.3 %fusion.6 = bf16[32,256,384]{1,2,0:T(8,128)(2,1)S(1)} fusion(f32[32,384,256]{2,1,0:T(8,128)} %get-tuple-element.44, bf16[64,32,384]{2,0,1:T(8,128)(2,1)} %bitcast.300, bf16[1,32,64,256]{3,2,1,0:T(8,128)(2,1)} %param.14), kind=kOutput, calls=%fused_computation.14 | convolution fusion | flops 465567744 | bytes 21495808 | tf_op jit(solution)/shard_map/nir,inf->ifr/dot_general | solution.py:82
  146.4 2.1 fusion.62
  149.0 2.1 copy.88
  151.1 2.2 all-to-all-done.1
  153.3 4.4 %all-to-all-start.4 = ((bf16[64,32,384]{2,1,0:T(8,128)(2,1)}), bf16[64,32,384]{2,1,0:T(8,128)(2,1)}, u32[]{:S(2)}, u32[]{:S(2)}) async-start(bf16[64,32,384]{2,1,0:T(8,128)(2,1)} %copy.88), calls=%async_computation.4 | async-start | bytes 3145728 | tf_op jit(solution)/shard_map/all_to_all | solution.py:21
  162.8 2.6 collective-permute-start
  165.4 6.4 %fusion.68 = f32[32,384,256]{2,1,0:T(8,128)} fusion(bf16[64,32,384]{2,1,0:T(8,128)(2,1)S(1)} %bitcast.298, bf16[1,32,64,256]{3,2,1,0:T(8,128)(2,1)S(1)} %copy-done), kind=kOutput, calls=%fused_computation.92 | convolution fusion | flops 402653184 | bytes 15204352 | tf_op jit(solution)/shard_map/nir,inf->ifr/dot_general | solution.py:60
  171.8 6.0 %all-to-all-done.4 = bf16[64,32,384]{2,1,0:T(8,128)(2,1)} async-done(((bf16[64,32,384]{2,1,0:T(8,128)(2,1)}), bf16[64,32,384]{2,1,0:T(8,128)(2,1)}, u32[]{:S(2)}, u32[]{:S(2)}) %all-to-all-start.4) | async-done | bytes 1572896 | tf_op jit(solution)/shard_map/all_to_all | solution.py:21
  184.0 19.7 %collective-permute-done = bf16[2048,384]{1,0:T(8,128)(2,1)} collective-permute-done((bf16[2048,384]{1,0:T(8,128)(2,1)}, bf16[2048,384]{1,0:T(8,128)(2,1)}, u32[]{:S(2)}, u32[]{:S(2)}) %collective-permute-start) | collective-permute-done | bytes 1572896 | tf_op jit(solution)/shard_map/ppermute | solution.py:9
  203.8 2.0 fusion.66
  205.8 1.9 copy.100
  207.7 4.5 %all-to-all-start.7 = ((bf16[16,128,384]{2,0,1:T(8,128)(2,1)}), bf16[16,128,384]{2,0,1:T(8,128)(2,1)}, u32[]{:S(2)}, u32[]{:S(2)}) async-start(bf16[16,128,384]{2,0,1:T(8,128)(2,1)} %copy.100), calls=%async_computation.7 | async-start | bytes 3145728 | tf_op jit(solution)/shard_map/all_to_all | solution.py:17
  212.2 7.9 %convolution_convert_fusion.6 = bf16[32,384,64]{1,2,0:T(8,128)(2,1)S(1)} fusion(bf16[1,32,64,256]{3,2,1,0:T(8,128)(2,1)S(1)} %copy-done.28, f32[32,384,256]{2,1,0:T(8,128)} %fusion.68), kind=kOutput, calls=%fused_computation.74 | convolution fusion | flops 431751168 | bytes 15204352 | tf_op jit(solution)/shard_map/ifr,inf->nir/dot_general | solution.py:62
  224.6 2.0 collective-permute-start.1
  226.6 6.2 %all-to-all-done.7 = bf16[16,128,384]{2,0,1:T(8,128)(2,1)} async-done(((bf16[16,128,384]{2,0,1:T(8,128)(2,1)}), bf16[16,128,384]{2,0,1:T(8,128)(2,1)}, u32[]{:S(2)}, u32[]{:S(2)}) %all-to-all-start.7) | async-done | bytes 1572896 | tf_op jit(solution)/shard_map/all_to_all | solution.py:17
  232.8 2.8 copy.102
  235.6 7.6 %fusion.56 = bf16[64,32,384]{2,0,1:T(8,128)(2,1)} fusion(bf16[64,32,384]{2,0,1:T(8,128)(2,1)} %bitcast.313, bf16[1,32,64,256]{3,2,1,0:T(8,128)(2,1)} %param.14, bf16[1,32,64,256]{3,2,1,0:T(8,128)(2,1)S(1)} %copy-done), kind=kOutput, calls=%fused_computation.84 | convolution fusion | flops 834404352 | bytes 5242880 | tf_op jit(solution)/shard_map/ifr,inf->nir/dot_general | solution.py:62
  243.3 3.5 copy.104
  246.7 4.4 %all-to-all-start.8 = ((bf16[64,32,384]{2,1,0:T(8,128)(2,1)}), bf16[64,32,384]{2,1,0:T(8,128)(2,1)}, u32[]{:S(2)}, u32[]{:S(2)}) async-start(bf16[64,32,384]{2,1,0:T(8,128)(2,1)} %copy.104), calls=%async_computation.8 | async-start | bytes 3145728 | tf_op jit(solution)/shard_map/all_to_all | solution.py:21
  251.1 2.6 pad_maximum_fusion.1
  253.8 3.3 gather_fusion.1
  260.4 5.5 %fusion.114 = f32[32,64,256]{2,1,0:T(8,128)} fusion(bf16[64,32,384]{2,0,1:T(8,128)(2,1)S(1)} %bitcast.303, bf16[32,256,384]{1,2,0:T(8,128)(2,1)} %copy-done.1), kind=kOutput, calls=%fused_computation.150 | convolution fusion | flops 402653184 | bytes 9961472 | tf_op jit(solution)/shard_map/nir,ifr->inf/dot_general | solution.py:87
  265.8 1.8 fusion.65
  267.6 3.0 copy.91
  271.2 4.8 %all-to-all-start.5 = ((bf16[16,128,384]{2,0,1:T(8,128)(2,1)}), bf16[16,128,384]{2,0,1:T(8,128)(2,1)}, u32[]{:S(2)}, u32[]{:S(2)}) async-start(bf16[16,128,384]{2,0,1:T(8,128)(2,1)} %copy.91), calls=%async_computation.5 | async-start | bytes 3145728 | tf_op jit(solution)/shard_map/all_to_all | solution.py:17
  276.1 5.1 %fusion.64 = bf16[64,32,384]{2,0,1:T(8,128)(2,1)S(1)} fusion(bf16[32,256,384]{1,2,0:T(8,128)(2,1)} %get-tuple-element.43, bf16[1,32,64,256]{3,2,1,0:T(8,128)(2,1)} %param.14), kind=kOutput, calls=%fused_computation.88 | convolution fusion | flops 403439616 | bytes 8912896 | tf_op jit(solution)/shard_map/ifr,inf->nir/dot_general | solution.py:62
  281.2 2.1 copy.113
  285.6 3.3 fusion.47
  288.9 7.3 %all-to-all-done.5 = bf16[16,128,384]{2,0,1:T(8,128)(2,1)} async-done(((bf16[16,128,384]{2,0,1:T(8,128)(2,1)}), bf16[16,128,384]{2,0,1:T(8,128)(2,1)}, u32[]{:S(2)}, u32[]{:S(2)}) %all-to-all-start.5) | async-done | bytes 1572896 | tf_op jit(solution)/shard_map/all_to_all | solution.py:17
  296.2 4.4 %all-to-all-start.9 = ((bf16[64,32,384]{2,1,0:T(8,128)(2,1)}), bf16[64,32,384]{2,1,0:T(8,128)(2,1)}, u32[]{:S(2)}, u32[]{:S(2)}) async-start(bf16[64,32,384]{2,1,0:T(8,128)(2,1)} %copy.113), calls=%async_computation.9 | async-start | bytes 3145728 | tf_op jit(solution)/shard_map/all_to_all | solution.py:21
  302.4 12.2 %fusion.13 = bf16[32,256,384]{1,2,0:T(8,128)(2,1)S(1)} fusion(f32[32,384,256]{2,1,0:T(8,128)} %fusion.68, bf16[64,32,384]{2,0,1:T(8,128)(2,1)S(1)} %bitcast.310, bf16[1,32,64,256]{3,2,1,0:T(8,128)(2,1)S(1)} %copy-done.29), kind=kOutput, calls=%fused_computation.21 | convolution fusion | flops 465567744 | bytes 21495808 | tf_op jit(solution)/shard_map/nir,inf->ifr/dot_general | solution.py:82
  314.6 2.1 fusion.63
  317.3 2.1 copy.97
  320.7 4.5 %all-to-all-start.6 = ((bf16[64,32,384]{2,1,0:T(8,128)(2,1)}), bf16[64,32,384]{2,1,0:T(8,128)(2,1)}, u32[]{:S(2)}, u32[]{:S(2)}) async-start(bf16[64,32,384]{2,1,0:T(8,128)(2,1)} %copy.97), calls=%async_computation.6 | async-start | bytes 3145728 | tf_op jit(solution)/shard_map/all_to_all | solution.py:21
  325.3 5.8 %fusion.115 = f32[32,64,256]{2,1,0:T(8,128)} fusion(bf16[64,32,384]{2,0,1:T(8,128)(2,1)} %bitcast.301, bf16[32,256,384]{1,2,0:T(8,128)(2,1)} %get-tuple-element.43), kind=kOutput, calls=%fused_computation.151 | convolution fusion | flops 402653184 | bytes 9961472 | tf_op jit(solution)/shard_map/ifr,nir->inf/dot_general | solution.py:79
  331.1 1.8 copy.114
  338.4 7.0 %all-to-all-done.6 = bf16[64,32,384]{2,1,0:T(8,128)(2,1)} async-done(((bf16[64,32,384]{2,1,0:T(8,128)(2,1)}), bf16[64,32,384]{2,1,0:T(8,128)(2,1)}, u32[]{:S(2)}, u32[]{:S(2)}) %all-to-all-start.6) | async-done | bytes 1572896 | tf_op jit(solution)/shard_map/all_to_all | solution.py:21
  350.9 10.1 %add_bitcast_fusion = f32[1,32,64,256]{3,2,1,0:T(8,128)} fusion(f32[32,64,256]{2,1,0:T(8,128)S(1)} %copy-done.25, bf16[64,32,384]{2,0,1:T(8,128)(2,1)S(1)} %bitcast.311, f32[32,384,256]{2,1,0:T(8,128)} %fusion.68), kind=kOutput, calls=%fused_computation.64 | convolution fusion | flops 431489024 | bytes 18350080 | tf_op jit(solution)/shard_map/ifr,nir->inf/dot_general | solution.py:79
  361.0 2.7 add_bitcast_fusion.1
  365.8 3.3 bitcast_convert_fusion.1
  369.1 16.3 %collective-permute-done.6 = bf16[2048,384]{1,0:T(8,128)(2,1)} collective-permute-done((bf16[2048,384]{1,0:T(8,128)(2,1)}, bf16[2048,384]{1,0:T(8,128)(2,1)}, u32[]{:S(2)}, u32[]{:S(2)}) %collective-permute-start.6) | collective-permute-done | bytes 1572896 | tf_op jit(solution)/shard_map/ppermute | solution.py:9
  385.4 3.3 bitcast_convert_fusion
  (111 shorter events, 49.6 us)
Async XLA Ops:
  0.6 108.0 %copy-start = (bf16[1,32,64,256]{3,2,1,0:T(8,128)(2,1)S(1)}, bf16[1,32,64,256]{3,2,1,0:T(8,128)(2,1)}, u32[]{:S(2)}) copy-start(bf16[1,32,64,256]{3,2,1,0:T(8,128)(2,1)} %param.13) | copy-start | bytes 3145732
  0.6 3.5 copy-start.3
  3.0 1.2 copy-start.6
  3.0 57.9 %copy-start.4 = (bf16[1,1,2048,384]{3,2,1,0:T(8,128)(2,1)}, bf16[1,1,2048,384]{3,2,1,0:T(8,128)(2,1)S(1)}, u32[]{:S(2)}) copy-start(bf16[1,1,2048,384]{3,2,1,0:T(8,128)(2,1)S(1)} %get-tuple-element.34) | copy-start | bytes 4718596
  6.9 25.1 %all-to-all-start.3 = ((bf16[16,128,384]{2,0,1:T(8,128)(2,1)}), bf16[16,128,384]{2,0,1:T(8,128)(2,1)}, u32[]{:S(2)}, u32[]{:S(2)}) async-start(bf16[16,128,384]{2,0,1:T(8,128)(2,1)} %copy.85), calls=%async_computation.3 | async-start | bytes 3145728 | tf_op jit(solution)/shard_map/all_to_all | solution.py:17
  11.2 3.3 copy-start.16
  13.4 1.2 copy-start.8
  32.0 24.5 %all-to-all-start.2 = ((bf16[16,128,384]{2,0,1:T(8,128)(2,1)}), bf16[16,128,384]{2,0,1:T(8,128)(2,1)}, u32[]{:S(2)}, u32[]{:S(2)}) async-start(bf16[16,128,384]{2,0,1:T(8,128)(2,1)} %copy.82), calls=%async_computation.2 | async-start | bytes 3145728 | tf_op jit(solution)/shard_map/all_to_all | solution.py:17
  56.5 49.2 %all-to-all-start = ((bf16[16,128,384]{2,0,1:T(8,128)(2,1)}), bf16[16,128,384]{2,0,1:T(8,128)(2,1)}, u32[]{:S(2)}, u32[]{:S(2)}) async-start(bf16[16,128,384]{2,0,1:T(8,128)(2,1)} %copy.76), calls=%async_computation | async-start | bytes 3145728 | tf_op jit(solution)/shard_map/all_to_all | solution.py:17
  61.7 27.1 %collective-permute-start.2 = (bf16[16,32,384]{2,1,0:T(8,128)(2,1)S(1)}, bf16[16,32,384]{2,1,0:T(8,128)(2,1)S(1)}, u32[]{:S(2)}, u32[]{:S(2)}) collective-permute-start(bf16[16,32,384]{2,1,0:T(8,128)(2,1)S(1)} %get-tuple-element.42), channel_id=1, source_target_pairs={{0,1},{1,2},{2,3},{3,0},{4,5},{5,6},{6,7},{7,4},{8,9},{9,10},{10,1... | collective-permute-start | bytes 1179656 | tf_op jit(solution)/shard_map/ppermute | solution.py:31
  62.2 27.6 %collective-permute-start.3 = (bf16[16,32,384]{2,1,0:T(8,128)(2,1)S(1)}, bf16[16,32,384]{2,1,0:T(8,128)(2,1)S(1)}, u32[]{:S(2)}, u32[]{:S(2)}) collective-permute-start(bf16[16,32,384]{2,1,0:T(8,128)(2,1)S(1)} %get-tuple-element.41), channel_id=1, source_target_pairs={{0,2},{1,3},{2,0},{3,1},{4,6},{5,7},{6,4},{7,5},{8,10},{9,11},{10,... | collective-permute-start | bytes 1179656 | tf_op jit(solution)/shard_map/ppermute | solution.py:31
  63.9 31.8 %collective-permute-start.4 = (bf16[16,32,384]{2,1,0:T(8,128)(2,1)S(1)}, bf16[16,32,384]{2,1,0:T(8,128)(2,1)S(1)}, u32[]{:S(2)}, u32[]{:S(2)}) collective-permute-start(bf16[16,32,384]{2,1,0:T(8,128)(2,1)S(1)} %get-tuple-element.40), channel_id=1, source_target_pairs={{0,3},{1,0},{2,1},{3,2},{4,7},{5,4},{6,5},{7,6},{8,11},{9,8},{10,9... | collective-permute-start | bytes 1179656 | tf_op jit(solution)/shard_map/ppermute | solution.py:31
  99.4 66.0 %copy-start.12 = (bf16[4,16,32,384]{3,2,1,0:T(8,128)(2,1)}, bf16[4,16,32,384]{3,2,1,0:T(8,128)(2,1)S(1)}, u32[]{:S(2)}) copy-start(bf16[4,16,32,384]{3,2,1,0:T(8,128)(2,1)S(1)} %broadcast_select_fusion) | copy-start | bytes 4718596
  105.7 3.0 copy-start.21
  128.5 24.8 %all-to-all-start.1 = ((bf16[64,32,384]{2,1,0:T(8,128)(2,1)}), bf16[64,32,384]{2,1,0:T(8,128)(2,1)}, u32[]{:S(2)}, u32[]{:S(2)}) async-start(bf16[64,32,384]{2,1,0:T(8,128)(2,1)} %copy.79), calls=%async_computation.1 | async-start | bytes 3145728 | tf_op jit(solution)/shard_map/all_to_all | solution.py:21
  146.4 2.7 copy-start.1
  153.3 24.5 %all-to-all-start.4 = ((bf16[64,32,384]{2,1,0:T(8,128)(2,1)}), bf16[64,32,384]{2,1,0:T(8,128)(2,1)}, u32[]{:S(2)}, u32[]{:S(2)}) async-start(bf16[64,32,384]{2,1,0:T(8,128)(2,1)} %copy.88), calls=%async_computation.4 | async-start | bytes 3145728 | tf_op jit(solution)/shard_map/all_to_all | solution.py:21
  157.7 1.7 copy-start.17
  159.5 1.9 copy-start.14
  162.8 40.9 %collective-permute-start = (bf16[2048,384]{1,0:T(8,128)(2,1)}, bf16[2048,384]{1,0:T(8,128)(2,1)}, u32[]{:S(2)}, u32[]{:S(2)}) collective-permute-start(bf16[2048,384]{1,0:T(8,128)(2,1)} %fusion.49), channel_id=1, source_target_pairs={{0,4},{4,8},{8,12},{12,16},{16,20},{20,24},{24,28},{28,0},{1,5},{5... | collective-permute-start | bytes 4718600 | tf_op jit(solution)/shard_map/ppermute | solution.py:9
  179.5 1.2 copy-start.10
  180.7 1.9 copy-start.15
  207.7 4.5 %copy-start.28 = (bf16[1,32,64,256]{3,2,1,0:T(8,128)(2,1)S(1)}, bf16[1,32,64,256]{3,2,1,0:T(8,128)(2,1)}, u32[]{:S(2)}) copy-start(bf16[1,32,64,256]{3,2,1,0:T(8,128)(2,1)} %param.14) | copy-start | bytes 3145732
  207.7 25.1 %all-to-all-start.7 = ((bf16[16,128,384]{2,0,1:T(8,128)(2,1)}), bf16[16,128,384]{2,0,1:T(8,128)(2,1)}, u32[]{:S(2)}, u32[]{:S(2)}) async-start(bf16[16,128,384]{2,0,1:T(8,128)(2,1)} %copy.100), calls=%async_computation.7 | async-start | bytes 3145728 | tf_op jit(solution)/shard_map/all_to_all | solution.py:17
  221.2 29.9 %collective-permute-start.7 = (bf16[16,32,384]{2,0,1:T(8,128)(2,1)}, bf16[16,32,384]{2,0,1:T(8,128)(2,1)}, u32[]{:S(2)}, u32[]{:S(2)}) collective-permute-start(bf16[16,32,384]{2,0,1:T(8,128)(2,1)} %get-tuple-element.38), channel_id=1, source_target_pairs={{0,1},{1,2},{2,3},{3,0},{4,5},{5,6},{6,7},{7,4},{8,9},{9,10},{10,1... | collective-permute-start | bytes 1179656 | tf_op jit(solution)/shard_map/ppermute | solution.py:31
  221.7 29.5 %collective-permute-start.8 = (bf16[16,32,384]{2,0,1:T(8,128)(2,1)}, bf16[16,32,384]{2,0,1:T(8,128)(2,1)}, u32[]{:S(2)}, u32[]{:S(2)}) collective-permute-start(bf16[16,32,384]{2,0,1:T(8,128)(2,1)} %get-tuple-element.37), channel_id=1, source_target_pairs={{0,2},{1,3},{2,0},{3,1},{4,6},{5,7},{6,4},{7,5},{8,10},{9,11},{10,... | collective-permute-start | bytes 1179656 | tf_op jit(solution)/shard_map/ppermute | solution.py:31
  223.3 27.8 %collective-permute-start.9 = (bf16[16,32,384]{2,0,1:T(8,128)(2,1)}, bf16[16,32,384]{2,0,1:T(8,128)(2,1)}, u32[]{:S(2)}, u32[]{:S(2)}) collective-permute-start(bf16[16,32,384]{2,0,1:T(8,128)(2,1)} %get-tuple-element.36), channel_id=1, source_target_pairs={{0,3},{1,0},{2,1},{3,2},{4,7},{5,4},{6,5},{7,6},{8,11},{9,8},{10,9... | collective-permute-start | bytes 1179656 | tf_op jit(solution)/shard_map/ppermute | solution.py:31
  224.6 41.2 %collective-permute-start.1 = (bf16[2048,384]{1,0:T(8,128)(2,1)}, bf16[2048,384]{1,0:T(8,128)(2,1)S(1)}, u32[]{:S(2)}, u32[]{:S(2)}) collective-permute-start(bf16[2048,384]{1,0:T(8,128)(2,1)} %fusion.48), channel_id=1, source_target_pairs={{0,28},{4,0},{8,4},{12,8},{16,12},{20,16},{24,20},{28,24},{1,29},{... | collective-permute-start | bytes 4718600 | tf_op jit(solution)/shard_map/ppermute | solution.py:9
  246.7 24.5 %all-to-all-start.8 = ((bf16[64,32,384]{2,1,0:T(8,128)(2,1)}), bf16[64,32,384]{2,1,0:T(8,128)(2,1)}, u32[]{:S(2)}, u32[]{:S(2)}) async-start(bf16[64,32,384]{2,1,0:T(8,128)(2,1)} %copy.104), calls=%async_computation.8 | async-start | bytes 3145728 | tf_op jit(solution)/shard_map/all_to_all | solution.py:21
  258.7 1.6 copy-start.22
  260.4 5.5 %copy-start.18 = (bf16[1,16,128,128]{3,2,1,0:T(8,128)(2,1)S(1)}, bf16[1,16,128,128]{3,2,1,0:T(8,128)(2,1)}, u32[]{:S(2)}) copy-start(bf16[1,16,128,128]{3,2,1,0:T(8,128)(2,1)} %param.15) | copy-start | bytes 1572868
  271.2 25.0 %all-to-all-start.5 = ((bf16[16,128,384]{2,0,1:T(8,128)(2,1)}), bf16[16,128,384]{2,0,1:T(8,128)(2,1)}, u32[]{:S(2)}, u32[]{:S(2)}) async-start(bf16[16,128,384]{2,0,1:T(8,128)(2,1)} %copy.91), calls=%async_computation.5 | async-start | bytes 3145728 | tf_op jit(solution)/shard_map/all_to_all | solution.py:17
  283.2 1.7 copy-start.19
  288.9 58.2 %collective-permute-start.5 = (bf16[2048,384]{1,0:T(8,128)(2,1)}, bf16[2048,384]{1,0:T(8,128)(2,1)}, u32[]{:S(2)}, u32[]{:S(2)}) collective-permute-start(bf16[2048,384]{1,0:T(8,128)(2,1)} %fusion.47), channel_id=1, source_target_pairs={{0,4},{4,8},{8,12},{12,16},{16,20},{20,24},{24,28},{28,0},{1,5},{5... | collective-permute-start | bytes 4718600 | tf_op jit(solution)/shard_map/ppermute | solution.py:9
  296.2 24.5 %all-to-all-start.9 = ((bf16[64,32,384]{2,1,0:T(8,128)(2,1)}), bf16[64,32,384]{2,1,0:T(8,128)(2,1)}, u32[]{:S(2)}, u32[]{:S(2)}) async-start(bf16[64,32,384]{2,1,0:T(8,128)(2,1)} %copy.113), calls=%async_computation.9 | async-start | bytes 3145728 | tf_op jit(solution)/shard_map/all_to_all | solution.py:21
  300.6 1.8 copy-start.29
  302.4 12.2 %copy-start.26 = (bf16[4,16,32,384]{3,1,0,2:T(8,128)(2,1)}, bf16[4,16,32,384]{3,1,0,2:T(8,128)(2,1)S(1)}, u32[]{:S(2)}) copy-start(bf16[4,16,32,384]{3,1,0,2:T(8,128)(2,1)S(1)} %copy.93) | copy-start | bytes 4718596
  314.6 2.7 copy-start.2
  320.7 24.7 %all-to-all-start.6 = ((bf16[64,32,384]{2,1,0:T(8,128)(2,1)}), bf16[64,32,384]{2,1,0:T(8,128)(2,1)}, u32[]{:S(2)}, u32[]{:S(2)}) async-start(bf16[64,32,384]{2,1,0:T(8,128)(2,1)} %copy.97), calls=%async_computation.6 | async-start | bytes 3145728 | tf_op jit(solution)/shard_map/all_to_all | solution.py:21
  331.1 1.9 copy-start.7
  331.1 2.4 copy-start.11
  333.4 1.8 copy-start.9
  335.2 1.4 copy-start.23
  347.0 3.9 copy-start.27
  347.6 3.3 copy-start.25
  347.6 13.3 %slice-start = ((s8[6291456]{0:T(1024)(128)(4,1)}), s8[4194304]{0:T(1024)(128)(4,1)S(1)}, s32[]{:S(2)}) async-start(s8[6291456]{0:T(1024)(128)(4,1)} %bitcast.284), calls=%async_computation.10 | async-start | bytes 8388608
  349.2 11.8 %slice-start.1 = ((s8[6291456]{0:T(1024)(128)(4,1)}), s8[2097152]{0:T(1024)(128)(4,1)S(1)}, s32[]{:S(2)}) async-start(s8[6291456]{0:T(1024)(128)(4,1)} %bitcast.284), calls=%async_computation.11 | async-start | bytes 4194304
  349.2 11.8 %copy-start.13 = (bf16[4,16,32,384]{3,2,1,0:T(8,128)(2,1)S(1)}, bf16[4,16,32,384]{3,2,1,0:T(8,128)(2,1)}, u32[]{:S(2)}) copy-start(bf16[4,16,32,384]{3,2,1,0:T(8,128)(2,1)} %copy-done.12) | copy-start | bytes 4718596
  349.2 11.8 %copy-start.20 = (f32[32,64,256]{2,1,0:T(8,128)S(1)}, f32[32,64,256]{2,1,0:T(8,128)}, u32[]{:S(2)}) copy-start(f32[32,64,256]{2,1,0:T(8,128)} %fusion.114) | copy-start | bytes 6291460
  349.2 36.2 %collective-permute-start.6 = (bf16[2048,384]{1,0:T(8,128)(2,1)}, bf16[2048,384]{1,0:T(8,128)(2,1)}, u32[]{:S(2)}, u32[]{:S(2)}) collective-permute-start(bf16[2048,384]{1,0:T(8,128)(2,1)} %fusion.46), channel_id=1, source_target_pairs={{0,28},{4,0},{8,4},{12,8},{16,12},{20,16},{24,20},{28,24},{1,29},{... | collective-permute-start | bytes 4718600 | tf_op jit(solution)/shard_map/ppermute | solution.py:9
  361.0 2.7 copy-start.5
  361.0 2.7 copy-start.24

commit v7 on v4

--- a/solution.py
+++ b/solution.py
@@ -143,10 +143,7 @@
     last_activation = shifted(sent, "pipe", 1)
 
     stored = stash[1, 0].reshape(blocks, width, rows)
-    behind = front(
-        stored, up_first, up_second, down_first,
-        to_columns_by_permutes, to_rows_by_permutes,
-    )
+    behind = front(stored, up_first, up_second, down_first)
     grad_step, terms, last_activation = backward(
         stored, near_cotangent, up_first, up_second, down_first, down_second, behind,
         last_activation,

time: 385 us -> 389 us (1.010)
  waiting for transfers between devices: 100 us -> 119 us
  other arithmetic: 35.2 us -> 24.7 us
  local copies, waits for them, and re-layouts: 71.7 us -> 63.9 us
  starting transfers between devices: 56.2 us -> 60.4 us
    ppermute x12 -> x6, waiting for transfers between devices: 27 us -> 44.4 us  [swapped(): lax.ppermute(piece, 'tensor', [(i, (i + shift) % count) for i in range(co...]
    all_to_all x4 -> x5, waiting for transfers between devices: 20.3 us -> 11.4 us  [to_columns(): lax.all_to_all(value, 'tensor', split_axis=1, concat_axis=0, tiled=True)]
    another operation x4 -> x2, other arithmetic: 10.5 us -> 2.76 us  [swapped(): return jnp.take(jnp.stack(arrived), order, axis=0)]
    all_to_all x4 -> x5, waiting for transfers between devices: 15.6 us -> 22.7 us  [to_rows(): lax.all_to_all(value, 'tensor', split_axis=0, concat_axis=1, tiled=True)]
    gather x4 -> x2, local copies, waits for them, and re-layouts: 13.4 us -> 6.67 us  [swapped(): return jnp.take(jnp.stack(arrived), order, axis=0)]
    all_to_all x4 -> x5, starting transfers between devices: 17.9 us -> 22.9 us  [to_rows(): lax.all_to_all(value, 'tensor', split_axis=0, concat_axis=1, tiled=True)]
    ppermute x12 -> x6, starting transfers between devices: 12 us -> 7.96 us  [swapped(): lax.ppermute(piece, 'tensor', [(i, (i + shift) % count) for i in range(co...]
    dynamic_slice x4 -> x2, local copies, waits for them, and re-layouts: 4.43 us -> 0.42 us  [swapped(): lax.dynamic_index_in_dim(pieces, (me + shift) % count, 0, keepdims=False)]
  transfers between devices with their start and end apart: 24 -> 20, of which waited for: 12 -> 17; matrix products, arithmetic and copies ran while one was open for 53% -> 43% of each run, Pallas kernels for 0% -> 0%
where the time goes in v7:
time: 389 us; the launch traced here: 383 us
  waiting for transfers between devices  119 us (31%)
  matrix products  114 us (29%)
  local copies, waits for them, and re-layouts  63.9 us (16%)
  starting transfers between devices  60.4 us (16%)
  other arithmetic  24.7 us (6%)
    ppermute x6, waiting for transfers between devices, swapped(): lax.ppermute(piece, 'tensor', [(i, (i + shift) % count) for i in range(co...  44.4 us
    ppermute x4, waiting for transfers between devices, shifted(): lax.ppermute(value, axis, [(i, (i + by) % count) for i in range(count)])  40.3 us
    dot_general x4, matrix products, front(): jnp.einsum('ifr,inf->nir', hidden, first_down, preferred_element_type=jnp...  29.4 us
    dot_general x2, matrix products, backward(): jnp.einsum('nir,inf->ifr', grad_folded, first_down, preferred_element_typ...  24.9 us
    all_to_all x5, starting transfers between devices, to_rows(): lax.all_to_all(value, 'tensor', split_axis=0, concat_axis=1, tiled=True)  22.9 us
    all_to_all x5, waiting for transfers between devices, to_rows(): lax.all_to_all(value, 'tensor', split_axis=0, concat_axis=1, tiled=True)  22.7 us
    all_to_all x5, starting transfers between devices, to_columns(): lax.all_to_all(value, 'tensor', split_axis=1, concat_axis=0, tiled=True)  21.4 us
    dot_general x2, matrix products, front(): jnp.einsum('nir,inf->ifr', spread, second_up, preferred_element_type=jnp....  15.4 us
  transfers between devices with their start and end apart: 20, of which 17 were waited for; matrix products, arithmetic and copies ran while one was open for 43% of the time, Pallas kernels for 0%

profile of v7, /device:TPU:0, one launch (start us, length us, event | category | flops | bytes accessed | tf_op | source)
XLA Modules:
  0.0 382.8 jit_solution(91419098510423917)
XLA Ops:
  0.7 2.2 convert_element_type.119
  3.4 2.1 copy.82
  5.5 4.3 %all-to-all-start.2 = ((bf16[16,128,384]{2,0,1:T(8,128)(2,1)}), bf16[16,128,384]{2,0,1:T(8,128)(2,1)}, u32[]{:S(2)}, u32[]{:S(2)}) async-start(bf16[16,128,384]{2,0,1:T(8,128)(2,1)} %copy.82), calls=%async_computation.2 | async-start | bytes 3145728 | tf_op jit(solution)/shard_map/all_to_all | solution.py:17
  9.9 3.9 %fusion.113 = (bf16[1,1,2048,384]{3,2,1,0:T(8,128)(2,1)}, bf16[1,1,2048,384]{3,2,1,0:T(8,128)(2,1)}) fusion(bf16[2,1,2048,384]{3,2,1,0:T(8,128)(2,1)} %param.10), kind=kLoop, calls=%fused_computation.149 | loop fusion | bytes 6291456 | tf_op jit(solution)/shard_map/slice | solution.py:126
  16.6 2.6 collective-permute-start.2
  21.4 2.1 copy.76
  23.5 14.6 %collective-permute-done.1 = bf16[16,32,384]{2,1,0:T(8,128)(2,1)S(1)} collective-permute-done((bf16[16,32,384]{2,1,0:T(8,128)(2,1)S(1)}, bf16[16,32,384]{2,1,0:T(8,128)(2,1)S(1)}, u32[]{:S(2)}, u32[]{:S(2)}) %collective-permute-start.1) | collective-permute-done | bytes 393248 | tf_op jit(solution)/shard_map/ppermute | solution.py:31
  39.8 4.8 %collective-permute-done.3 = bf16[16,32,384]{2,1,0:T(8,128)(2,1)S(1)} collective-permute-done((bf16[16,32,384]{2,1,0:T(8,128)(2,1)S(1)}, bf16[16,32,384]{2,1,0:T(8,128)(2,1)S(1)}, u32[]{:S(2)}, u32[]{:S(2)}) %collective-permute-start.3) | collective-permute-done | bytes 393248 | tf_op jit(solution)/shard_map/ppermute | solution.py:31
  46.0 3.3 gather_fusion
  49.3 4.7 %all-to-all-start = ((bf16[16,128,384]{2,0,1:T(8,128)(2,1)}), bf16[16,128,384]{2,0,1:T(8,128)(2,1)}, u32[]{:S(2)}, u32[]{:S(2)}) async-start(bf16[16,128,384]{2,0,1:T(8,128)(2,1)} %copy.76), calls=%async_computation | async-start | bytes 3145728 | tf_op jit(solution)/shard_map/all_to_all | solution.py:17
  55.7 9.0 %fusion.34 = (bf16[32,256,384]{1,2,0:T(8,128)(2,1)}, f32[32,384,256]{2,1,0:T(8,128)}) fusion(bf16[1,32,64,256]{3,2,1,0:T(8,128)(2,1)S(1)} %copy-done, bf16[64,32,384]{2,1,0:T(8,128)(2,1)S(1)} %bitcast.300), kind=kOutput, calls=%fused_computation.47 | convolution fusion | flops 430964736 | bytes 21495808 | tf_op jit(solution)/shard_map/nir,inf->ifr/dot_general | solution.py:60
  64.7 2.8 copy.83
  67.5 6.8 %all-to-all-done = bf16[16,128,384]{2,0,1:T(8,128)(2,1)} async-done(((bf16[16,128,384]{2,0,1:T(8,128)(2,1)}), bf16[16,128,384]{2,0,1:T(8,128)(2,1)}, u32[]{:S(2)}, u32[]{:S(2)}) %all-to-all-start) | async-done | bytes 1572896 | tf_op jit(solution)/shard_map/all_to_all | solution.py:17
  74.3 2.8 copy.77
  77.1 7.6 %fusion.59 = bf16[64,32,384]{2,0,1:T(8,128)(2,1)} fusion(bf16[64,32,384]{2,0,1:T(8,128)(2,1)} %bitcast.314, bf16[1,32,64,256]{3,2,1,0:T(8,128)(2,1)} %param.14, bf16[1,32,64,256]{3,2,1,0:T(8,128)(2,1)S(1)} %copy-done), kind=kOutput, calls=%fused_computation.85 | convolution fusion | flops 834404352 | bytes 5242880 | tf_op jit(solution)/shard_map/ifr,inf->nir/dot_general | solution.py:62
  84.7 3.5 copy.79
  88.2 4.9 %all-to-all-start.1 = ((bf16[64,32,384]{2,1,0:T(8,128)(2,1)}), bf16[64,32,384]{2,1,0:T(8,128)(2,1)}, u32[]{:S(2)}, u32[]{:S(2)}) async-start(bf16[64,32,384]{2,1,0:T(8,128)(2,1)} %copy.79), calls=%async_computation.1 | async-start | bytes 3145728 | tf_op jit(solution)/shard_map/all_to_all | solution.py:21
  93.1 13.3 %fusion.6 = bf16[32,256,384]{1,2,0:T(8,128)(2,1)S(1)} fusion(f32[32,384,256]{2,1,0:T(8,128)} %get-tuple-element.44, bf16[64,32,384]{2,0,1:T(8,128)(2,1)} %bitcast.302, bf16[1,32,64,256]{3,2,1,0:T(8,128)(2,1)} %param.14), kind=kOutput, calls=%fused_computation.14 | convolution fusion | flops 465567744 | bytes 21495808 | tf_op jit(solution)/shard_map/nir,inf->ifr/dot_general | solution.py:82
  106.4 2.1 fusion.62
  109.1 2.1 copy.87
  111.1 2.1 all-to-all-done.1
  113.2 4.4 %all-to-all-start.3 = ((bf16[64,32,384]{2,1,0:T(8,128)(2,1)}), bf16[64,32,384]{2,1,0:T(8,128)(2,1)}, u32[]{:S(2)}, u32[]{:S(2)}) async-start(bf16[64,32,384]{2,1,0:T(8,128)(2,1)} %copy.87), calls=%async_computation.3 | async-start | bytes 3145728 | tf_op jit(solution)/shard_map/all_to_all | solution.py:21
  122.7 3.0 collective-permute-start
  125.6 12.1 %all-to-all-done.3 = bf16[64,32,384]{2,1,0:T(8,128)(2,1)} async-done(((bf16[64,32,384]{2,1,0:T(8,128)(2,1)}), bf16[64,32,384]{2,1,0:T(8,128)(2,1)}, u32[]{:S(2)}, u32[]{:S(2)}) %all-to-all-start.3) | async-done | bytes 1572896 | tf_op jit(solution)/shard_map/all_to_all | solution.py:21
  143.9 20.1 %collective-permute-done = bf16[2048,384]{1,0:T(8,128)(2,1)} collective-permute-done((bf16[2048,384]{1,0:T(8,128)(2,1)}, bf16[2048,384]{1,0:T(8,128)(2,1)}, u32[]{:S(2)}, u32[]{:S(2)}) %collective-permute-start) | collective-permute-done | bytes 1572896 | tf_op jit(solution)/shard_map/ppermute | solution.py:9
  164.0 3.2 fusion.66
  167.2 2.9 copy.100
  170.1 4.5 %all-to-all-start.7 = ((bf16[16,128,384]{2,0,1:T(8,128)(2,1)}), bf16[16,128,384]{2,0,1:T(8,128)(2,1)}, u32[]{:S(2)}, u32[]{:S(2)}) async-start(bf16[16,128,384]{2,0,1:T(8,128)(2,1)} %copy.100), calls=%async_computation.7 | async-start | bytes 3145728 | tf_op jit(solution)/shard_map/all_to_all | solution.py:17
  174.6 5.1 %convolution_convert_fusion.7 = bf16[32,384,64]{1,2,0:T(8,128)(2,1)S(1)} fusion(bf16[32,256,384]{1,2,0:T(8,128)(2,1)} %get-tuple-element.43, bf16[1,32,64,256]{3,2,1,0:T(8,128)(2,1)} %param.14), kind=kOutput, calls=%fused_computation.75 | convolution fusion | flops 403439616 | bytes 8912896 | tf_op jit(solution)/shard_map/ifr,inf->nir/dot_general | solution.py:62
  184.1 2.1 copy.94
  186.1 16.4 %collective-permute-done.7 = bf16[16,32,384]{2,0,1:T(8,128)(2,1)S(1)} collective-permute-done((bf16[16,32,384]{2,0,1:T(8,128)(2,1)S(1)}, bf16[16,32,384]{2,0,1:T(8,128)(2,1)S(1)}, u32[]{:S(2)}, u32[]{:S(2)}) %collective-permute-start.7) | collective-permute-done | bytes 393248 | tf_op jit(solution)/shard_map/ppermute | solution.py:31
  203.5 5.8 %collective-permute-done.9 = bf16[16,32,384]{2,0,1:T(8,128)(2,1)S(1)} collective-permute-done((bf16[16,32,384]{2,0,1:T(8,128)(2,1)S(1)}, bf16[16,32,384]{2,0,1:T(8,128)(2,1)S(1)}, u32[]{:S(2)}, u32[]{:S(2)}) %collective-permute-start.9) | collective-permute-done | bytes 393248 | tf_op jit(solution)/shard_map/ppermute | solution.py:31
  210.7 3.4 gather_fusion.1
  214.1 4.4 %all-to-all-start.5 = ((bf16[16,128,384]{2,0,1:T(8,128)(2,1)}), bf16[16,128,384]{2,0,1:T(8,128)(2,1)}, u32[]{:S(2)}, u32[]{:S(2)}) async-start(bf16[16,128,384]{2,0,1:T(8,128)(2,1)} %copy.94), calls=%async_computation.5 | async-start | bytes 3145728 | tf_op jit(solution)/shard_map/all_to_all | solution.py:17
  223.4 2.8 copy.102
  226.2 7.6 %fusion.56 = bf16[64,32,384]{2,0,1:T(8,128)(2,1)} fusion(bf16[64,32,384]{2,0,1:T(8,128)(2,1)} %bitcast.315, bf16[1,32,64,256]{3,2,1,0:T(8,128)(2,1)} %param.14, bf16[1,32,64,256]{3,2,1,0:T(8,128)(2,1)S(1)} %copy-done), kind=kOutput, calls=%fused_computation.84 | convolution fusion | flops 834404352 | bytes 5242880 | tf_op jit(solution)/shard_map/ifr,inf->nir/dot_general | solution.py:62
  233.9 3.5 copy.104
  238.7 4.6 %all-to-all-start.8 = ((bf16[64,32,384]{2,1,0:T(8,128)(2,1)}), bf16[64,32,384]{2,1,0:T(8,128)(2,1)}, u32[]{:S(2)}, u32[]{:S(2)}) async-start(bf16[64,32,384]{2,1,0:T(8,128)(2,1)} %copy.104), calls=%async_computation.8 | async-start | bytes 3145728 | tf_op jit(solution)/shard_map/all_to_all | solution.py:21
  243.3 3.2 fusion.116
  248.1 6.4 %fusion.82 = f32[32,384,256]{2,1,0:T(8,128)} fusion(bf16[64,32,384]{2,0,1:T(8,128)(2,1)S(1)} %bitcast.296, bf16[1,32,64,256]{3,2,1,0:T(8,128)(2,1)S(1)} %copy-done), kind=kOutput, calls=%fused_computation.107 | convolution fusion | flops 402653184 | bytes 15204352 | tf_op jit(solution)/shard_map/nir,inf->ifr/dot_general | solution.py:60
  254.6 3.7 collective-permute-done.4
  258.3 2.0 fusion.65
  263.4 3.6 all-to-all-start.4
  267.0 9.1 %fusion.64 = bf16[64,32,384]{2,0,1:T(8,128)(2,1)S(1)} fusion(bf16[1,32,64,256]{3,2,1,0:T(8,128)(2,1)} %param.14, f32[32,384,256]{2,1,0:T(8,128)} %fusion.82), kind=kOutput, calls=%fused_computation.88 | convolution fusion | flops 431751168 | bytes 15204352 | tf_op jit(solution)/shard_map/ifr,inf->nir/dot_general | solution.py:62
  276.0 2.1 copy.115
  280.4 3.3 fusion.47
  283.7 3.3 all-to-all-done.4
  287.0 4.8 %all-to-all-start.9 = ((bf16[64,32,384]{2,1,0:T(8,128)(2,1)}), bf16[64,32,384]{2,1,0:T(8,128)(2,1)}, u32[]{:S(2)}, u32[]{:S(2)}) async-start(bf16[64,32,384]{2,1,0:T(8,128)(2,1)} %copy.115), calls=%async_computation.9 | async-start | bytes 3145728 | tf_op jit(solution)/shard_map/all_to_all | solution.py:21
  293.0 11.6 %fusion.13 = bf16[32,256,384]{1,2,0:T(8,128)(2,1)S(1)} fusion(f32[32,384,256]{2,1,0:T(8,128)} %fusion.82, bf16[64,32,384]{2,0,1:T(8,128)(2,1)S(1)} %bitcast.312, bf16[1,32,64,256]{3,2,1,0:T(8,128)(2,1)S(1)} %copy-done.25), kind=kOutput, calls=%fused_computation.21 | convolution fusion | flops 465567744 | bytes 21495808 | tf_op jit(solution)/shard_map/nir,inf->ifr/dot_general | solution.py:82
  304.7 2.1 fusion.63
  307.3 2.1 copy.97
  309.4 2.5 all-to-all-done.9
  311.9 4.4 %all-to-all-start.6 = ((bf16[64,32,384]{2,1,0:T(8,128)(2,1)}), bf16[64,32,384]{2,1,0:T(8,128)(2,1)}, u32[]{:S(2)}, u32[]{:S(2)}) async-start(bf16[64,32,384]{2,1,0:T(8,128)(2,1)} %copy.97), calls=%async_computation.6 | async-start | bytes 3145728 | tf_op jit(solution)/shard_map/all_to_all | solution.py:21
  316.3 6.0 %fusion.115 = f32[32,64,256]{2,1,0:T(8,128)} fusion(bf16[64,32,384]{2,0,1:T(8,128)(2,1)} %bitcast.303, bf16[32,256,384]{1,2,0:T(8,128)(2,1)} %get-tuple-element.43), kind=kOutput, calls=%fused_computation.151 | convolution fusion | flops 402653184 | bytes 9961472 | tf_op jit(solution)/shard_map/ifr,nir->inf/dot_general | solution.py:79
  322.3 2.6 fusion.67
  328.4 3.2 fusion.71
  331.6 4.8 %all-to-all-done.6 = bf16[64,32,384]{2,1,0:T(8,128)(2,1)} async-done(((bf16[64,32,384]{2,1,0:T(8,128)(2,1)}), bf16[64,32,384]{2,1,0:T(8,128)(2,1)}, u32[]{:S(2)}, u32[]{:S(2)}) %all-to-all-start.6) | async-done | bytes 1572896 | tf_op jit(solution)/shard_map/all_to_all | solution.py:21
  338.7 3.5 fusion.46
  342.2 3.4 collective-permute-start.6
  345.6 9.3 %add_bitcast_fusion = f32[1,32,64,256]{3,2,1,0:T(8,128)} fusion(f32[32,64,256]{2,1,0:T(8,128)S(1)} %copy-done.22, bf16[64,32,384]{2,0,1:T(8,128)(2,1)S(1)} %bitcast.313, f32[32,384,256]{2,1,0:T(8,128)} %fusion.82), kind=kOutput, calls=%fused_computation.64 | convolution fusion | flops 431489024 | bytes 18350080 | tf_op jit(solution)/shard_map/ifr,nir->inf/dot_general | solution.py:79
  354.9 2.6 add_bitcast_fusion.1
  359.6 3.3 bitcast_convert_fusion.1
  362.9 16.5 %collective-permute-done.6 = bf16[2048,384]{1,0:T(8,128)(2,1)} collective-permute-done((bf16[2048,384]{1,0:T(8,128)(2,1)}, bf16[2048,384]{1,0:T(8,128)(2,1)}, u32[]{:S(2)}, u32[]{:S(2)}) %collective-permute-start.6) | collective-permute-done | bytes 1572896 | tf_op jit(solution)/shard_map/ppermute | solution.py:9
  379.3 3.3 bitcast_convert_fusion
  (108 shorter events, 52.0 us)
Async XLA Ops:
  0.6 55.0 %copy-start = (bf16[1,32,64,256]{3,2,1,0:T(8,128)(2,1)S(1)}, bf16[1,32,64,256]{3,2,1,0:T(8,128)(2,1)}, u32[]{:S(2)}) copy-start(bf16[1,32,64,256]{3,2,1,0:T(8,128)(2,1)} %param.13) | copy-start | bytes 3145732
  0.6 2.2 copy-start.15
  5.5 43.8 %all-to-all-start.2 = ((bf16[16,128,384]{2,0,1:T(8,128)(2,1)}), bf16[16,128,384]{2,0,1:T(8,128)(2,1)}, u32[]{:S(2)}, u32[]{:S(2)}) async-start(bf16[16,128,384]{2,0,1:T(8,128)(2,1)} %copy.82), calls=%async_computation.2 | async-start | bytes 3145728 | tf_op jit(solution)/shard_map/all_to_all | solution.py:17
  9.9 3.9 %copy-start.3 = (bf16[1,16,128,128]{3,2,1,0:T(8,128)(2,1)S(1)}, bf16[1,16,128,128]{3,2,1,0:T(8,128)(2,1)}, u32[]{:S(2)}) copy-start(bf16[1,16,128,128]{3,2,1,0:T(8,128)(2,1)} %param.12) | copy-start | bytes 1572868
  15.9 4.7 %copy-start.12 = (f32[1,2048,384]{2,1,0:T(8,128)S(1)}, f32[1,2048,384]{2,1,0:T(8,128)}, u32[]{:S(2)}) copy-start(f32[1,2048,384]{2,1,0:T(8,128)} %param.9) | copy-start | bytes 9437188
  16.1 22.0 %collective-permute-start.1 = (bf16[16,32,384]{2,1,0:T(8,128)(2,1)S(1)}, bf16[16,32,384]{2,1,0:T(8,128)(2,1)S(1)}, u32[]{:S(2)}, u32[]{:S(2)}) collective-permute-start(bf16[16,32,384]{2,1,0:T(8,128)(2,1)S(1)} %get-tuple-element.42), channel_id=1, source_target_pairs={{0,1},{1,2},{2,3},{3,0},{4,5},{5,6},{6,7},{7,4},{8,9},{9,10},{10,1... | collective-permute-start | bytes 1179656 | tf_op jit(solution)/shard_map/ppermute | solution.py:31
  16.6 23.2 %collective-permute-start.2 = (bf16[16,32,384]{2,1,0:T(8,128)(2,1)S(1)}, bf16[16,32,384]{2,1,0:T(8,128)(2,1)S(1)}, u32[]{:S(2)}, u32[]{:S(2)}) collective-permute-start(bf16[16,32,384]{2,1,0:T(8,128)(2,1)S(1)} %get-tuple-element.41), channel_id=1, source_target_pairs={{0,2},{1,3},{2,0},{3,1},{4,6},{5,7},{6,4},{7,5},{8,10},{9,11},{10,... | collective-permute-start | bytes 1179656 | tf_op jit(solution)/shard_map/ppermute | solution.py:31
  19.2 25.5 %collective-permute-start.3 = (bf16[16,32,384]{2,1,0:T(8,128)(2,1)S(1)}, bf16[16,32,384]{2,1,0:T(8,128)(2,1)S(1)}, u32[]{:S(2)}, u32[]{:S(2)}) collective-permute-start(bf16[16,32,384]{2,1,0:T(8,128)(2,1)S(1)} %get-tuple-element.40), channel_id=1, source_target_pairs={{0,3},{1,0},{2,1},{3,2},{4,7},{5,4},{6,5},{7,6},{8,11},{9,8},{10,9... | collective-permute-start | bytes 1179656 | tf_op jit(solution)/shard_map/ppermute | solution.py:31
  49.3 24.9 %all-to-all-start = ((bf16[16,128,384]{2,0,1:T(8,128)(2,1)}), bf16[16,128,384]{2,0,1:T(8,128)(2,1)}, u32[]{:S(2)}, u32[]{:S(2)}) async-start(bf16[16,128,384]{2,0,1:T(8,128)(2,1)} %copy.76), calls=%async_computation | async-start | bytes 3145728 | tf_op jit(solution)/shard_map/all_to_all | solution.py:17
  55.7 9.0 %copy-start.19 = (bf16[4,16,32,384]{3,2,1,0:T(8,128)(2,1)}, bf16[4,16,32,384]{3,2,1,0:T(8,128)(2,1)S(1)}, u32[]{:S(2)}) copy-start(bf16[4,16,32,384]{3,2,1,0:T(8,128)(2,1)S(1)} %broadcast_select_fusion) | copy-start | bytes 4718596
  88.2 25.0 %all-to-all-start.1 = ((bf16[64,32,384]{2,1,0:T(8,128)(2,1)}), bf16[64,32,384]{2,1,0:T(8,128)(2,1)}, u32[]{:S(2)}, u32[]{:S(2)}) async-start(bf16[64,32,384]{2,1,0:T(8,128)(2,1)} %copy.79), calls=%async_computation.1 | async-start | bytes 3145728 | tf_op jit(solution)/shard_map/all_to_all | solution.py:21
  106.4 2.7 copy-start.1
  113.2 24.5 %all-to-all-start.3 = ((bf16[64,32,384]{2,1,0:T(8,128)(2,1)}), bf16[64,32,384]{2,1,0:T(8,128)(2,1)}, u32[]{:S(2)}, u32[]{:S(2)}) async-start(bf16[64,32,384]{2,1,0:T(8,128)(2,1)} %copy.87), calls=%async_computation.3 | async-start | bytes 3145728 | tf_op jit(solution)/shard_map/all_to_all | solution.py:21
  117.6 1.7 copy-start.16
  119.3 1.9 copy-start.13
  122.7 41.3 %collective-permute-start = (bf16[2048,384]{1,0:T(8,128)(2,1)}, bf16[2048,384]{1,0:T(8,128)(2,1)}, u32[]{:S(2)}, u32[]{:S(2)}) collective-permute-start(bf16[2048,384]{1,0:T(8,128)(2,1)} %fusion.49), channel_id=1, source_target_pairs={{0,4},{4,8},{8,12},{12,16},{16,20},{20,24},{24,28},{28,0},{1,5},{5... | collective-permute-start | bytes 4718600 | tf_op jit(solution)/shard_map/ppermute | solution.py:9
  139.4 1.1 copy-start.8
  140.5 1.9 copy-start.14
  170.1 44.0 %all-to-all-start.7 = ((bf16[16,128,384]{2,0,1:T(8,128)(2,1)}), bf16[16,128,384]{2,0,1:T(8,128)(2,1)}, u32[]{:S(2)}, u32[]{:S(2)}) async-start(bf16[16,128,384]{2,0,1:T(8,128)(2,1)} %copy.100), calls=%async_computation.7 | async-start | bytes 3145728 | tf_op jit(solution)/shard_map/all_to_all | solution.py:17
  179.7 3.8 copy-start.5
  179.9 22.6 %collective-permute-start.7 = (bf16[16,32,384]{2,0,1:T(8,128)(2,1)S(1)}, bf16[16,32,384]{2,0,1:T(8,128)(2,1)S(1)}, u32[]{:S(2)}, u32[]{:S(2)}) collective-permute-start(bf16[16,32,384]{2,0,1:T(8,128)(2,1)S(1)} %get-tuple-element.38), channel_id=1, source_target_pairs={{0,1},{1,2},{2,3},{3,0},{4,5},{5,6},{6,7},{7,4},{8,9},{9,10},{10,1... | collective-permute-start | bytes 1179656 | tf_op jit(solution)/shard_map/ppermute | solution.py:31
  180.5 23.1 %collective-permute-start.8 = (bf16[16,32,384]{2,0,1:T(8,128)(2,1)S(1)}, bf16[16,32,384]{2,0,1:T(8,128)(2,1)S(1)}, u32[]{:S(2)}, u32[]{:S(2)}) collective-permute-start(bf16[16,32,384]{2,0,1:T(8,128)(2,1)S(1)} %get-tuple-element.37), channel_id=1, source_target_pairs={{0,2},{1,3},{2,0},{3,1},{4,6},{5,7},{6,4},{7,5},{8,10},{9,11},{10,... | collective-permute-start | bytes 1179656 | tf_op jit(solution)/shard_map/ppermute | solution.py:31
  182.1 27.2 %collective-permute-start.9 = (bf16[16,32,384]{2,0,1:T(8,128)(2,1)S(1)}, bf16[16,32,384]{2,0,1:T(8,128)(2,1)S(1)}, u32[]{:S(2)}, u32[]{:S(2)}) collective-permute-start(bf16[16,32,384]{2,0,1:T(8,128)(2,1)S(1)} %get-tuple-element.36), channel_id=1, source_target_pairs={{0,3},{1,0},{2,1},{3,2},{4,7},{5,4},{6,5},{7,6},{8,11},{9,8},{10,9... | collective-permute-start | bytes 1179656 | tf_op jit(solution)/shard_map/ppermute | solution.py:31
  214.1 24.6 %all-to-all-start.5 = ((bf16[16,128,384]{2,0,1:T(8,128)(2,1)}), bf16[16,128,384]{2,0,1:T(8,128)(2,1)}, u32[]{:S(2)}, u32[]{:S(2)}) async-start(bf16[16,128,384]{2,0,1:T(8,128)(2,1)} %copy.94), calls=%async_computation.5 | async-start | bytes 3145728 | tf_op jit(solution)/shard_map/all_to_all | solution.py:17
  221.7 36.6 %collective-permute-start.4 = (bf16[2048,384]{1,0:T(8,128)(2,1)}, bf16[2048,384]{1,0:T(8,128)(2,1)}, u32[]{:S(2)}, u32[]{:S(2)}) collective-permute-start(bf16[2048,384]{1,0:T(8,128)(2,1)} %fusion.48), channel_id=1, source_target_pairs={{0,28},{4,0},{8,4},{12,8},{16,12},{20,16},{24,20},{28,24},{1,29},{... | collective-permute-start | bytes 4718600 | tf_op jit(solution)/shard_map/ppermute | solution.py:9
  238.7 24.7 %all-to-all-start.8 = ((bf16[64,32,384]{2,1,0:T(8,128)(2,1)}), bf16[64,32,384]{2,1,0:T(8,128)(2,1)}, u32[]{:S(2)}, u32[]{:S(2)}) async-start(bf16[64,32,384]{2,1,0:T(8,128)(2,1)} %copy.104), calls=%async_computation.8 | async-start | bytes 3145728 | tf_op jit(solution)/shard_map/all_to_all | solution.py:21
  248.1 6.4 %copy-start.10 = (bf16[16,4,32,384]{3,0,1,2:T(8,128)(2,1)}, bf16[16,4,32,384]{3,0,1,2:T(8,128)(2,1)S(1)}, u32[]{:S(2)}) copy-start(bf16[16,4,32,384]{3,0,1,2:T(8,128)(2,1)S(1)} %copy.95) | copy-start | bytes 4718596
  248.1 10.1 %copy-start.17 = (bf16[1,16,128,128]{3,2,1,0:T(8,128)(2,1)S(1)}, bf16[1,16,128,128]{3,2,1,0:T(8,128)(2,1)}, u32[]{:S(2)}) copy-start(bf16[1,16,128,128]{3,2,1,0:T(8,128)(2,1)} %param.15) | copy-start | bytes 1572868
  263.4 23.6 %all-to-all-start.4 = ((bf16[16,128,384]{2,0,1:T(8,128)(2,1)}), bf16[16,128,384]{2,0,1:T(8,128)(2,1)S(1)}, u32[]{:S(2)}, u32[]{:S(2)}) async-start(bf16[16,128,384]{2,0,1:T(8,128)(2,1)} %copy.90), calls=%async_computation.4 | async-start | bytes 3145728 | tf_op jit(solution)/shard_map/all_to_all | solution.py:17
  283.7 54.4 %collective-permute-start.5 = (bf16[2048,384]{1,0:T(8,128)(2,1)}, bf16[2048,384]{1,0:T(8,128)(2,1)}, u32[]{:S(2)}, u32[]{:S(2)}) collective-permute-start(bf16[2048,384]{1,0:T(8,128)(2,1)} %fusion.47), channel_id=1, source_target_pairs={{0,4},{4,8},{8,12},{12,16},{16,20},{20,24},{24,28},{28,0},{1,5},{5... | collective-permute-start | bytes 4718600 | tf_op jit(solution)/shard_map/ppermute | solution.py:9
  287.0 24.9 %all-to-all-start.9 = ((bf16[64,32,384]{2,1,0:T(8,128)(2,1)}), bf16[64,32,384]{2,1,0:T(8,128)(2,1)}, u32[]{:S(2)}, u32[]{:S(2)}) async-start(bf16[64,32,384]{2,1,0:T(8,128)(2,1)} %copy.115), calls=%async_computation.9 | async-start | bytes 3145728 | tf_op jit(solution)/shard_map/all_to_all | solution.py:21
  291.8 1.2 copy-start.25
  292.1 12.6 %copy-start.23 = (bf16[4,16,32,384]{3,1,0,2:T(8,128)(2,1)}, bf16[4,16,32,384]{3,1,0,2:T(8,128)(2,1)S(1)}, u32[]{:S(2)}) copy-start(bf16[4,16,32,384]{3,1,0,2:T(8,128)(2,1)S(1)} %copy.92) | copy-start | bytes 4718596
  304.7 2.7 copy-start.2
  307.3 14.9 %slice-start = ((s8[6291456]{0:T(1024)(128)(4,1)}), s8[2097152]{0:T(1024)(128)(4,1)S(1)}, s32[]{:S(2)}) async-start(s8[6291456]{0:T(1024)(128)(4,1)} %bitcast.284), calls=%async_computation.10 | async-start | bytes 4194304
  311.9 24.5 %all-to-all-start.6 = ((bf16[64,32,384]{2,1,0:T(8,128)(2,1)}), bf16[64,32,384]{2,1,0:T(8,128)(2,1)}, u32[]{:S(2)}, u32[]{:S(2)}) async-start(bf16[64,32,384]{2,1,0:T(8,128)(2,1)} %copy.97), calls=%async_computation.6 | async-start | bytes 3145728 | tf_op jit(solution)/shard_map/all_to_all | solution.py:21
  316.3 6.0 %slice-start.1 = ((s8[6291456]{0:T(1024)(128)(4,1)}), s8[4194304]{0:T(1024)(128)(4,1)S(1)}, s32[]{:S(2)}) async-start(s8[6291456]{0:T(1024)(128)(4,1)} %bitcast.284), calls=%async_computation.11 | async-start | bytes 8388608
  316.3 6.0 %copy-start.20 = (bf16[4,16,32,384]{3,2,1,0:T(8,128)(2,1)S(1)}, bf16[4,16,32,384]{3,2,1,0:T(8,128)(2,1)}, u32[]{:S(2)}) copy-start(bf16[4,16,32,384]{3,2,1,0:T(8,128)(2,1)} %copy-done.19) | copy-start | bytes 4718596
  324.8 1.9 copy-start.7
  324.8 2.4 copy-start.9
  327.2 1.2 copy-start.21
  331.6 6.5 %copy-start.4 = (bf16[1,16,128,128]{3,2,1,0:T(8,128)(2,1)S(1)}, bf16[1,16,128,128]{3,2,1,0:T(8,128)(2,1)}, u32[]{:S(2)}) copy-start(bf16[1,16,128,128]{3,2,1,0:T(8,128)(2,1)} %param.12) | copy-start | bytes 1572868
  338.1 7.5 %copy-start.24 = (bf16[4,16,32,384]{3,1,0,2:T(8,128)(2,1)S(1)}, bf16[4,16,32,384]{3,1,0,2:T(8,128)(2,1)}, u32[]{:S(2)}) copy-start(bf16[4,16,32,384]{3,1,0,2:T(8,128)(2,1)} %copy-done.23) | copy-start | bytes 4718596
  338.7 6.9 %copy-start.22 = (f32[32,64,256]{2,1,0:T(8,128)S(1)}, f32[32,64,256]{2,1,0:T(8,128)}, u32[]{:S(2)}) copy-start(f32[32,64,256]{2,1,0:T(8,128)} %fusion.115) | copy-start | bytes 6291460
  338.7 16.2 %slice-start.2 = ((s8[6291456]{0:T(1024)(128)(4,1)}), s8[4194304]{0:T(1024)(128)(4,1)S(1)}, s32[]{:S(2)}) async-start(s8[6291456]{0:T(1024)(128)(4,1)} %bitcast.286), calls=%async_computation.12 | async-start | bytes 8388608
  342.2 12.7 %slice-start.3 = ((s8[6291456]{0:T(1024)(128)(4,1)}), s8[2097152]{0:T(1024)(128)(4,1)S(1)}, s32[]{:S(2)}) async-start(s8[6291456]{0:T(1024)(128)(4,1)} %bitcast.286), calls=%async_computation.13 | async-start | bytes 4194304
  342.2 12.7 %copy-start.11 = (bf16[16,4,32,384]{3,0,1,2:T(8,128)(2,1)S(1)}, bf16[16,4,32,384]{3,0,1,2:T(8,128)(2,1)}, u32[]{:S(2)}) copy-start(bf16[16,4,32,384]{3,0,1,2:T(8,128)(2,1)} %copy-done.10) | copy-start | bytes 4718596
  342.2 12.7 %copy-start.18 = (f32[32,64,256]{2,1,0:T(8,128)S(1)}, f32[32,64,256]{2,1,0:T(8,128)}, u32[]{:S(2)}) copy-start(f32[32,64,256]{2,1,0:T(8,128)} %fusion.67) | copy-start | bytes 6291460
  342.2 37.2 %collective-permute-start.6 = (bf16[2048,384]{1,0:T(8,128)(2,1)}, bf16[2048,384]{1,0:T(8,128)(2,1)}, u32[]{:S(2)}, u32[]{:S(2)}) collective-permute-start(bf16[2048,384]{1,0:T(8,128)(2,1)} %fusion.46), channel_id=1, source_target_pairs={{0,28},{4,0},{8,4},{12,8},{16,12},{20,16},{24,20},{28,24},{1,29},{... | collective-permute-start | bytes 4718600 | tf_op jit(solution)/shard_map/ppermute | solution.py:9
  354.9 2.6 copy-start.6
